TPU v7x, 32 devices: a whole 2x2x4 slice. The times are simulated.
32 devices in a mesh: groups: 2 (over x), rows: 16 (over z, y, core).
Axes of the slice: x: 2, y: 2, z: 4, core: 2. Of those that a mesh axis runs over, the one named last changes fastest.
Arguments:
- source_emb: float32 [65536, 128], P(('groups', 'rows')), parts along dimension 0, may hold values from -6 to 6
- target_emb: float32 [16384, 128], P(('groups', 'rows')), parts along dimension 0, may hold values from -6 to 6
- tile_source: int32 [4096], P(('groups', 'rows')), parts along dimension 0, may hold values from 0 to 15, as said below
- tile_slot: int32 [4096], P(('groups', 'rows')), parts along dimension 0, may hold values from 0 to 15
- tile_count: int32 [32], P(('groups', 'rows')), parts along dimension 0, may hold values from 21 to 128, as said below
- wanted: int32 [512, 1], P(('groups', 'rows')), parts along dimension 0, may hold values from 0 to 3, as said below
Outputs:
- aligned: float32 [65536, 128], P(('groups', 'rows')), parts along dimension 0
- row_mass: float32 [65536], P(('groups', 'rows')), parts along dimension 0
There are 2 independent parts, one for each index of `groups`. A program takes and returns all parts, laid end to end along the dimension named above; each array names one. Nothing has to cross between parts.
Inputs may be any that keep to these rules, and one draw needn't show every extreme that they name: Within one device the 128 pairs (tile_source, tile_slot) are distinct, live or not. `tile_count`: some device has exactly 128 live tiles. `wanted`: the 1 block that one device requests from one owner are distinct; each owner has one block that no device requests.
All inputs are finite; a program needn't handle non-finite values.
Results may differ from a plain program's by a relative error of at most 0.0003.
Values sent between devices are 32-bit elements; how exact they have to be, the bound alone decides.
No kernel may reach another device: no remote copies, remote signals or barrier semaphores. Data moves between devices by JAX's collectives and lax.ppermute only.
A program may use at most 128 MiB of HBM per device.

v0:
```python
import math

import jax
import jax.numpy as jnp
from jax import lax
from jax.sharding import PartitionSpec as P

E = 128
BLOCK = 128
SB_DEV = 16
NEED = 1
ITERS = 2


EPSILON = 1e-06
SOFTMAX_WARMTH = 0.03
ROW_MINIMUM = 1.0
COLUMN_FLOOR = 0.01
HIGHEST = lax.Precision.HIGHEST


def unit_rows(values):
    return values * lax.rsqrt(jnp.sum(values * values, axis=-1, keepdims=True) + EPSILON)


def tile_kernel(source_tiles, target_tiles):
    cosine_affinity = jnp.einsum("tie,tje->tij", source_tiles, target_tiles, precision=HIGHEST)
    return jnp.exp(cosine_affinity / SOFTMAX_WARMTH)


def on_device(source_emb, target_emb, tile_source, tile_slot, tile_count, wanted):
    devices_rows = lax.axis_size("rows")
    target_blocks = target_emb.shape[0] // BLOCK
    all_blocks = target_blocks * devices_rows
    capacity = tile_source.shape[0]
    group_size = math.gcd(capacity, 64)
    group_count = capacity // group_size
    source_normalized = unit_rows(source_emb).reshape(-1, BLOCK, E)
    request_flattened = wanted.reshape(-1)
    matches = tile_slot[:, None] == jnp.arange(request_flattened.shape[0])[None, :]
    local_blocks = jnp.sum(jnp.where(matches, request_flattened[None, :], 0), axis=1)
    global_ids = tile_slot // NEED * target_blocks + local_blocks
    live_slots = (jnp.arange(capacity) < tile_count[0]).astype(jnp.float32)
    asked = lax.all_to_all(wanted, "rows", split_axis=0, concat_axis=0, tiled=True)
    own_unit = unit_rows(target_emb).reshape(target_blocks, BLOCK, E)
    outgoing = own_unit[asked.reshape(-1)]
    fetched = lax.all_to_all(outgoing, "rows", split_axis=0, concat_axis=0, tiled=True)
    grouped = (
        tile_source.reshape(group_count, group_size),
        tile_slot.reshape(group_count, group_size),
        global_ids.reshape(group_count, group_size),
        live_slots.reshape(group_count, group_size),
    )
    source_onehot = (tile_source[:, None] == jnp.arange(SB_DEV)[None, :]).astype(jnp.float32)
    target_onehot = (global_ids[:, None] == jnp.arange(all_blocks)[None, :]).astype(jnp.float32)

    def affinity_tiles(source_ids, fetch_group, live_group):
        return (
            tile_kernel(source_normalized[source_ids], fetched[fetch_group])
            * live_group[:, None, None]
        )

    column_scale = jnp.ones((all_blocks, BLOCK), jnp.float32)
    row_scale = jnp.ones((SB_DEV, BLOCK), jnp.float32)
    for iteration in range(ITERS):

        def row_per_group(inputs):
            source_ids, fetch_group, global_group, live_group = inputs
            tiles = affinity_tiles(source_ids, fetch_group, live_group)
            return jnp.einsum("tij,tj->ti", tiles, column_scale[global_group], precision=HIGHEST)

        row_partials = lax.map(row_per_group, grouped).reshape(capacity, BLOCK)
        row_sums = jnp.einsum("ts,ti->si", source_onehot, row_partials, precision=HIGHEST)
        row_scale = 1.0 / jnp.maximum(row_sums, ROW_MINIMUM)

        def column_per_group(inputs):
            source_ids, fetch_group, global_group, live_group = inputs
            tiles = affinity_tiles(source_ids, fetch_group, live_group)
            return jnp.einsum("tij,ti->tj", tiles, row_scale[source_ids], precision=HIGHEST)

        partials = lax.map(column_per_group, grouped).reshape(capacity, BLOCK)
        column_partial = jnp.einsum(
            "tn,tj->nj", target_onehot, partials, precision=HIGHEST
        ).reshape(-1)
        column_total = lax.psum(column_partial, "rows")
        scales = 1.0 / jnp.maximum(column_total, COLUMN_FLOOR)
        column_scale = scales.reshape(all_blocks, BLOCK)

    def accumulate(carry, inputs):
        aligned_sum, mass_sum = carry
        source_ids, fetch_group, global_group, live_group = inputs
        tiles = affinity_tiles(source_ids, fetch_group, live_group)
        weights = tiles * row_scale[source_ids][:, :, None] * column_scale[global_group][:, None, :]
        onehot = (source_ids[:, None] == jnp.arange(SB_DEV)[None, :]).astype(jnp.float32)
        vectors = jnp.einsum("tij,tje->tie", weights, fetched[fetch_group], precision=HIGHEST)
        aligned_sum = aligned_sum + jnp.einsum("ts,tie->sie", onehot, vectors, precision=HIGHEST)
        mass_sum = mass_sum + jnp.einsum(
            "ts,ti->si", onehot, jnp.sum(weights, axis=2), precision=HIGHEST
        )
        return ((aligned_sum, mass_sum), None)

    start_state = (
        jnp.zeros((SB_DEV, BLOCK, E), jnp.float32),
        jnp.zeros((SB_DEV, BLOCK), jnp.float32),
    )
    (aligned_sum, mass_sum), unused = lax.scan(accumulate, start_state, grouped)
    aligned = (aligned_sum * math.sqrt(E)).reshape(-1, E)
    return (aligned, mass_sum.reshape(-1))


def solution(mesh):
    placed = (
        P(("groups", "rows"), None),
        P(("groups", "rows"), None),
        P(("groups", "rows")),
        P(("groups", "rows")),
        P(("groups", "rows")),
        P(("groups", "rows"), None),
    )
    return jax.shard_map(
        on_device,
        mesh=mesh,
        in_specs=placed,
        out_specs=(P(("groups", "rows"), None), P(("groups", "rows"))),
        check_vma=False,
    )
```

profile of v0, /device:TPU:0, one launch (start us, length us, event | category | flops | bytes accessed | tf_op | source)
XLA Modules:
  0.0 460.6 jit_solution(3760560023906276125)
XLA Ops:
  2.1 7.4 %all-to-all-start = ((s32[16,1,1]{2,1,0:T(1,128)}), s32[16,1,1]{2,1,0:T(1,128)S(1)}, u32[]{:S(2)}, u32[]{:S(2)}) async-start(s32[16,1,1]{2,1,0:T(1,128)} %copy.17), calls=%async_computation | async-start | bytes 16384 | tf_op jit(solution)/shard_map/all_to_all | solution.py:44
  11.7 4.1 all-to-all-done
  17.8 3.7 all-to-all-start.1
  23.2 21.1 %all-to-all-done.1 = f32[16,128,128]{2,1,0:T(8,128)S(1)} async-done(((f32[16,128,128]{2,1,0:T(8,128)}), f32[16,128,128]{2,1,0:T(8,128)S(1)}, u32[]{:S(2)}, u32[]{:S(2)}) %all-to-all-start.1) | async-done | bytes 1048608 | tf_op jit(solution)/shard_map/all_to_all | solution.py:47
  44.4 58.4 %while.53 = (s32[]{:T(128)}, f32[2,64,128]{2,1,0:T(8,128)S(1)}, s32[2,64]{1,0:T(2,128)S(1)}, f32[16,128,128]{2,1,0:T(8,128)S(1)}, s32[2,64]{1,0:T(2,128)S(1)}, /...) while((s32[]{:T(128)}, f32[2,64,128]{2,1,0:T(8,128)S(1)}, ...), condition=%wide.region_4.5_spmd, body=%wide.region_3.4_spmd.sunk | while | flops 1625296512 | bytes 33800056 | solution.py:72
  44.4 2.7 gather_fusion.1
  47.1 2.8 gather_fusion.2
  49.9 14.3 %fusion.159 = f32[64,128,128]{2,1,0:T(8,128)} fusion(f32[64,128,128]{2,1,0:T(8,128)} %gather_fusion.1, f32[64,128,128]{2,1,0:T(8,128)} %gather_fusion.2), kind=kOutput, calls=%fused_computation.168.clone.1 | convolution fusion | flops 1610612736 | bytes 12582912 | tf_op jit(solution)/shard_map/while/body/eval_jaxpr/tie,tje->tij/dot_general | solution.py:27
  64.9 8.7 %fusion.161 = f32[64,1,128]{2,1,0:T(1,128)S(1)} fusion(f32[64,128,1]{1,2,0:T(1,128)S(1)} %bitcast.287, f32[64,128,128]{2,1,0:T(8,128)} %fusion.159, f32[64]{0:T(128)S(1)} %fusion.160), kind=kOutput, calls=%fused_computation.17.clone.1 | convolution fusion | flops 14680064 | bytes 4260096 | tf_op jit(solution)/shard_map/while/body/eval_jaxpr/tij,tj->ti/dot_general | solution.py:70
  76.3 2.8 gather_fusion.2
  79.1 14.3 %fusion.159 = f32[64,128,128]{2,1,0:T(8,128)} fusion(f32[64,128,128]{2,1,0:T(8,128)} %gather_fusion.1, f32[64,128,128]{2,1,0:T(8,128)} %gather_fusion.2), kind=kOutput, calls=%fused_computation.168.clone.1 | convolution fusion | flops 1610612736 | bytes 12582912 | tf_op jit(solution)/shard_map/while/body/eval_jaxpr/tie,tje->tij/dot_general | solution.py:27
  94.1 8.7 %fusion.161 = f32[64,1,128]{2,1,0:T(1,128)S(1)} fusion(f32[64,128,1]{1,2,0:T(1,128)S(1)} %bitcast.287, f32[64,128,128]{2,1,0:T(8,128)} %fusion.159, f32[64]{0:T(128)S(1)} %fusion.160), kind=kOutput, calls=%fused_computation.17.clone.1 | convolution fusion | flops 14680064 | bytes 4260096 | tf_op jit(solution)/shard_map/while/body/eval_jaxpr/tij,tj->ti/dot_general | solution.py:70
  103.0 53.4 %while.54 = (s32[]{:T(128)}, f32[2,64,128]{2,1,0:T(8,128)S(1)}, s32[2,64]{1,0:T(2,128)S(1)}, f32[16,128,128]{2,1,0:T(8,128)S(1)}, s32[2,64]{1,0:T(2,128)S(1)}, /...) while((s32[]{:T(128)}, f32[2,64,128]{2,1,0:T(8,128)S(1)}, ...), condition=%wide.region_6.7_spmd, body=%wide.region_5.6_spmd.sunk | while | flops 1625295232 | bytes 33762408 | solution.py:81
  106.3 2.8 gather_fusion.5
  109.1 14.3 %fusion.167 = f32[64,128,128]{2,1,0:T(8,128)} fusion(f32[64,128,128]{2,1,0:T(8,128)} %gather_fusion.4, f32[64,128,128]{2,1,0:T(8,128)} %gather_fusion.5), kind=kOutput, calls=%fused_computation.169.clone.1 | convolution fusion | flops 1610612736 | bytes 12582912 | tf_op jit(solution)/shard_map/while/body/eval_jaxpr/tie,tje->tij/dot_general | solution.py:27
  124.0 6.0 %fusion.169 = f32[64,1,128]{2,1,0:T(1,128)S(1)} fusion(f32[64,128,1]{1,2,0:T(1,128)S(1)} %bitcast.288, f32[64,128,128]{2,1,0:T(8,128)} %fusion.167, f32[64]{0:T(128)S(1)} %fusion.168), kind=kOutput, calls=%fused_computation.42.clone.1 | convolution fusion | flops 14680064 | bytes 4260096 | tf_op jit(solution)/shard_map/while/body/eval_jaxpr/tij,ti->tj/dot_general | solution.py:79
  130.0 2.7 gather_fusion.4
  132.8 2.8 gather_fusion.5
  135.6 14.3 %fusion.167 = f32[64,128,128]{2,1,0:T(8,128)} fusion(f32[64,128,128]{2,1,0:T(8,128)} %gather_fusion.4, f32[64,128,128]{2,1,0:T(8,128)} %gather_fusion.5), kind=kOutput, calls=%fused_computation.169.clone.1 | convolution fusion | flops 1610612736 | bytes 12582912 | tf_op jit(solution)/shard_map/while/body/eval_jaxpr/tie,tje->tij/dot_general | solution.py:27
  150.5 6.0 %fusion.169 = f32[64,1,128]{2,1,0:T(1,128)S(1)} fusion(f32[64,128,1]{1,2,0:T(1,128)S(1)} %bitcast.288, f32[64,128,128]{2,1,0:T(8,128)} %fusion.167, f32[64]{0:T(128)S(1)} %fusion.168), kind=kOutput, calls=%fused_computation.42.clone.1 | convolution fusion | flops 14680064 | bytes 4260096 | tf_op jit(solution)/shard_map/while/body/eval_jaxpr/tij,ti->tj/dot_general | solution.py:79
  156.8 63.1 %psum.14 = f32[8192]{0:T(1024)S(1)} all-reduce(f32[8192]{0:T(1024)S(1)} %convolution_bitcast_fusion.1), channel_id=1, replica_groups=mesh['groups'=2,'rows'=16] {'rows'}, use_global_device_ids=true, to_apply=%region_7.8 | all-reduce | flops 8192 | bytes 65536 | tf_op jit(solution)/shard_map/psum | solution.py:85
  219.9 58.3 %while.55 = (s32[]{:T(128)}, f32[2,64,128]{2,1,0:T(8,128)S(1)}, s32[2,64]{1,0:T(2,128)S(1)}, f32[16,128,128]{2,1,0:T(8,128)S(1)}, s32[2,64]{1,0:T(2,128)S(1)}, /...) while((s32[]{:T(128)}, f32[2,64,128]{2,1,0:T(8,128)S(1)}, ...), condition=%wide.region_9.10_spmd, body=%wide.region_8.9_spmd.sunk | while | flops 1625296512 | bytes 33767284 | solution.py:72
  220.0 2.7 gather_fusion.7
  222.7 2.8 gather_fusion.8
  225.5 14.3 %fusion.176 = f32[64,128,128]{2,1,0:T(8,128)} fusion(f32[64,128,128]{2,1,0:T(8,128)} %gather_fusion.7, f32[64,128,128]{2,1,0:T(8,128)} %gather_fusion.8), kind=kOutput, calls=%fused_computation.170.clone.1 | convolution fusion | flops 1610612736 | bytes 12582912 | tf_op jit(solution)/shard_map/while/body/eval_jaxpr/tie,tje->tij/dot_general | solution.py:27
  240.4 8.7 %fusion.178 = f32[64,1,128]{2,1,0:T(1,128)S(1)} fusion(f32[64,128,1]{1,2,0:T(1,128)S(1)} %bitcast.289, f32[64,128,128]{2,1,0:T(8,128)} %fusion.176, f32[64]{0:T(128)S(1)} %fusion.177), kind=kOutput, calls=%fused_computation.62.clone.1 | convolution fusion | flops 14680064 | bytes 4260096 | tf_op jit(solution)/shard_map/while/body/eval_jaxpr/tij,tj->ti/dot_general | solution.py:70
  251.9 2.8 gather_fusion.8
  254.7 14.3 %fusion.176 = f32[64,128,128]{2,1,0:T(8,128)} fusion(f32[64,128,128]{2,1,0:T(8,128)} %gather_fusion.7, f32[64,128,128]{2,1,0:T(8,128)} %gather_fusion.8), kind=kOutput, calls=%fused_computation.170.clone.1 | convolution fusion | flops 1610612736 | bytes 12582912 | tf_op jit(solution)/shard_map/while/body/eval_jaxpr/tie,tje->tij/dot_general | solution.py:27
  269.6 8.7 %fusion.178 = f32[64,1,128]{2,1,0:T(1,128)S(1)} fusion(f32[64,128,1]{1,2,0:T(1,128)S(1)} %bitcast.289, f32[64,128,128]{2,1,0:T(8,128)} %fusion.176, f32[64]{0:T(128)S(1)} %fusion.177), kind=kOutput, calls=%fused_computation.62.clone.1 | convolution fusion | flops 14680064 | bytes 4260096 | tf_op jit(solution)/shard_map/while/body/eval_jaxpr/tij,tj->ti/dot_general | solution.py:70
  278.6 53.2 %while.56 = (s32[]{:T(128)}, f32[2,64,128]{2,1,0:T(8,128)S(1)}, s32[2,64]{1,0:T(2,128)S(1)}, f32[16,128,128]{2,1,0:T(8,128)S(1)}, s32[2,64]{1,0:T(2,128)S(1)}, /...) while((s32[]{:T(128)}, f32[2,64,128]{2,1,0:T(8,128)S(1)}, ...), condition=%wide.region_11.12_spmd, body=%wide.region_10.11_spmd.sunk | while | flops 1625295232 | bytes 33762408 | solution.py:81
  278.9 2.7 gather_fusion.10
  281.6 2.8 gather_fusion.11
  284.4 14.3 %fusion.184 = f32[64,128,128]{2,1,0:T(8,128)} fusion(f32[64,128,128]{2,1,0:T(8,128)} %gather_fusion.10, f32[64,128,128]{2,1,0:T(8,128)} %gather_fusion.11), kind=kOutput, calls=%fused_computation.171.clone.1 | convolution fusion | flops 1610612736 | bytes 12582912 | tf_op jit(solution)/shard_map/while/body/eval_jaxpr/tie,tje->tij/dot_general | solution.py:27
  299.3 6.0 %fusion.186 = f32[64,1,128]{2,1,0:T(1,128)S(1)} fusion(f32[64,128,1]{1,2,0:T(1,128)S(1)} %bitcast.290, f32[64,128,128]{2,1,0:T(8,128)} %fusion.184, f32[64]{0:T(128)S(1)} %fusion.185), kind=kOutput, calls=%fused_computation.87.clone.1 | convolution fusion | flops 14680064 | bytes 4260096 | tf_op jit(solution)/shard_map/while/body/eval_jaxpr/tij,ti->tj/dot_general | solution.py:79
  308.1 2.8 gather_fusion.11
  310.9 14.3 %fusion.184 = f32[64,128,128]{2,1,0:T(8,128)} fusion(f32[64,128,128]{2,1,0:T(8,128)} %gather_fusion.10, f32[64,128,128]{2,1,0:T(8,128)} %gather_fusion.11), kind=kOutput, calls=%fused_computation.171.clone.1 | convolution fusion | flops 1610612736 | bytes 12582912 | tf_op jit(solution)/shard_map/while/body/eval_jaxpr/tie,tje->tij/dot_general | solution.py:27
  325.8 6.0 %fusion.186 = f32[64,1,128]{2,1,0:T(1,128)S(1)} fusion(f32[64,128,1]{1,2,0:T(1,128)S(1)} %bitcast.290, f32[64,128,128]{2,1,0:T(8,128)} %fusion.184, f32[64]{0:T(128)S(1)} %fusion.185), kind=kOutput, calls=%fused_computation.87.clone.1 | convolution fusion | flops 14680064 | bytes 4260096 | tf_op jit(solution)/shard_map/while/body/eval_jaxpr/tij,ti->tj/dot_general | solution.py:79
  332.1 57.6 %psum.15 = f32[8192]{0:T(1024)S(1)} all-reduce(f32[8192]{0:T(1024)S(1)} %convolution_bitcast_fusion), channel_id=1, replica_groups=mesh['groups'=2,'rows'=16] {'rows'}, use_global_device_ids=true, to_apply=%region_12.13 | all-reduce | flops 8192 | bytes 65536 | tf_op jit(solution)/shard_map/psum | solution.py:85
  389.7 69.0 %while.57 = (s32[]{:T(128)}, f32[16,128,128]{2,0,1:T(8,128)S(1)}, f32[16,128]{1,0:T(8,128)S(1)}, s32[2,64]{1,0:T(2,128)S(1)}, f32[16,128,128]{2,1,0:T(8,128)S(1)...) while((s32[]{:T(128)}, f32[16,128,128]{2,0,1:T(8,128)S(1)}, ...), condition=%wide.region_15.16_spmd.clone, body=%wide.region_13.15_spmd.clone.sunk | while | flops 3434087936 | bytes 65373616 | solution.py:106
  390.6 2.7 gather_fusion.12
  393.4 2.8 gather_fusion.15
  396.8 12.0 %fusion.196 = (f32[64,128]{1,0:T(8,128)S(1)}, f32[64,128,128]{1,2,0:T(8,128)S(1)}) fusion(f32[64,128]{1,0:T(8,128)S(1)} %gather_fusion.13, f32[64,128]{1,0:T(8,128)S(1)} %gather_fusion.14, f32[64]{0:T(128)S(1)} %fusion.195, f32[64,128,128]{2,1,0:T(8,128)} %gather_fusion.15, f32[64,128,128]{2,1,0:T(8,128)} %gather_fusion.12), kind=kOutput, calls=%fused_computation.110.clone.1 | convolution fusion | flops 1615847424 | bytes 12681472 | tf_op jit(solution)/shard_map/while/body/eval_jaxpr/tie,tje->tij/dot_general | solution.py:27
  408.9 9.5 %fusion.197 = f32[64,128,128]{2,1,0:T(8,128)} fusion(f32[64,128,128]{2,1,0:T(8,128)S(1)} %copy-done, f32[64,128,128]{1,2,0:T(8,128)S(1)} %get-tuple-element.666, f32[64,128]{1,0:T(8,128)S(1)} %gather_fusion.13, f32[64,128]{1,0:T(8,128)S(1)} %gather_fusion.14, f32[64]{0:T(128)S(1)} %fusion.195), kind=kOutput, calls=%fused_computation.111.clone.1 | convolution fusion | flops 1614807040 | bytes 12648704 | tf_op jit(solution)/shard_map/while/body/eval_jaxpr/tij,tje->tie/dot_general | solution.py:95
  418.4 5.9 %fusion.199 = f32[16,128,128]{2,0,1:T(8,128)S(1)} fusion(f32[64,128,128]{2,1,0:T(8,128)} %fusion.197, f32[16,128,128]{2,0,1:T(8,128)S(1)} %get-tuple-element.796, pred[]{:T(512)S(6)} %compare.4, s32[64]{0:T(128)S(1)} %fusion.198), kind=kOutput, calls=%fused_computation.116.clone.1 | convolution fusion | flops 201851904 | bytes 6291713 | tf_op jit(solution)/shard_map/while/body/eval_jaxpr/ts,tie->sie/dot_general | solution.py:96
  427.8 2.8 gather_fusion.15
  431.2 12.0 %fusion.196 = (f32[64,128]{1,0:T(8,128)S(1)}, f32[64,128,128]{1,2,0:T(8,128)S(1)}) fusion(f32[64,128]{1,0:T(8,128)S(1)} %gather_fusion.13, f32[64,128]{1,0:T(8,128)S(1)} %gather_fusion.14, f32[64]{0:T(128)S(1)} %fusion.195, f32[64,128,128]{2,1,0:T(8,128)} %gather_fusion.15, f32[64,128,128]{2,1,0:T(8,128)} %gather_fusion.12), kind=kOutput, calls=%fused_computation.110.clone.1 | convolution fusion | flops 1615847424 | bytes 12681472 | tf_op jit(solution)/shard_map/while/body/eval_jaxpr/tie,tje->tij/dot_general | solution.py:27
  443.2 9.5 %fusion.197 = f32[64,128,128]{2,1,0:T(8,128)} fusion(f32[64,128,128]{2,1,0:T(8,128)S(1)} %copy-done, f32[64,128,128]{1,2,0:T(8,128)S(1)} %get-tuple-element.666, f32[64,128]{1,0:T(8,128)S(1)} %gather_fusion.13, f32[64,128]{1,0:T(8,128)S(1)} %gather_fusion.14, f32[64]{0:T(128)S(1)} %fusion.195), kind=kOutput, calls=%fused_computation.111.clone.1 | convolution fusion | flops 1614807040 | bytes 12648704 | tf_op jit(solution)/shard_map/while/body/eval_jaxpr/tij,tje->tie/dot_general | solution.py:95
  452.7 5.9 %fusion.199 = f32[16,128,128]{2,0,1:T(8,128)S(1)} fusion(f32[64,128,128]{2,1,0:T(8,128)} %fusion.197, f32[16,128,128]{2,0,1:T(8,128)S(1)} %get-tuple-element.796, pred[]{:T(512)S(6)} %compare.4, s32[64]{0:T(128)S(1)} %fusion.198), kind=kOutput, calls=%fused_computation.116.clone.1 | convolution fusion | flops 201851904 | bytes 6291713 | tf_op jit(solution)/shard_map/while/body/eval_jaxpr/ts,tie->sie/dot_general | solution.py:96
  (132 shorter events, 30.9 us)
Async XLA Ops:
  0.6 20.9 %copy-start.6 = (s32[16,1]{0,1:T(1,128)S(1)}, s32[16,1]{0,1:T(1,128)}, u32[]{:S(2)}) copy-start(s32[16,1]{0,1:T(1,128)} %param.21) | copy-start | bytes 196
  0.6 20.8 %copy-start.7 = (s32[128]{0:T(128)S(1)}, s32[128]{0:T(128)}, u32[]{:S(2)}) copy-start(s32[128]{0:T(128)} %param.19) | copy-start | bytes 1540
  0.7 21.8 %copy-start.5 = (s32[128]{0:T(128)S(1)}, s32[128]{0:T(128)}, u32[]{:S(2)}) copy-start(s32[128]{0:T(128)} %param.18) | copy-start | bytes 1540
  0.7 21.8 %copy-start.2 = (f32[2048,128]{1,0:T(8,128)S(1)}, f32[2048,128]{1,0:T(8,128)}, u32[]{:S(2)}) copy-start(f32[2048,128]{1,0:T(8,128)} %param.16) | copy-start | bytes 3145732
  2.1 13.7 %all-to-all-start = ((s32[16,1,1]{2,1,0:T(1,128)}), s32[16,1,1]{2,1,0:T(1,128)S(1)}, u32[]{:S(2)}, u32[]{:S(2)}) async-start(s32[16,1,1]{2,1,0:T(1,128)} %copy.17), calls=%async_computation | async-start | bytes 16384 | tf_op jit(solution)/shard_map/all_to_all | solution.py:44
  17.8 26.6 %all-to-all-start.1 = ((f32[16,128,128]{2,1,0:T(8,128)}), f32[16,128,128]{2,1,0:T(8,128)S(1)}, u32[]{:S(2)}, u32[]{:S(2)}) async-start(f32[16,128,128]{2,1,0:T(8,128)} %gather_fusion.16), calls=%async_computation.1 | async-start | bytes 2097152 | tf_op jit(solution)/shard_map/all_to_all | solution.py:47
  278.6 111.1 %copy-start.1 = (f32[16,128,128]{2,0,1:T(8,128)S(1)}, f32[16,128,128]{2,0,1:T(8,128)}, u32[]{:S(2)}) copy-start(f32[16,128,128]{2,0,1:T(8,128)} %custom-call) | copy-start | bytes 3145732
  278.6 111.1 %copy-start.3 = (f32[16,128]{1,0:T(8,128)S(1)}, f32[16,128]{1,0:T(8,128)}, u32[]{:S(2)}) copy-start(f32[16,128]{1,0:T(8,128)} %custom-call.1) | copy-start | bytes 24580
  396.8 12.0 %copy-start = (f32[64,128,128]{2,1,0:T(8,128)S(1)}, f32[64,128,128]{2,1,0:T(8,128)}, u32[]{:S(2)}) copy-start(f32[64,128,128]{2,1,0:T(8,128)} %gather_fusion.12) | copy-start | bytes 12582916 | tf_op jit(solution)/shard_map/while
  431.2 12.0 %copy-start = (f32[64,128,128]{2,1,0:T(8,128)S(1)}, f32[64,128,128]{2,1,0:T(8,128)}, u32[]{:S(2)}) copy-start(f32[64,128,128]{2,1,0:T(8,128)} %gather_fusion.12) | copy-start | bytes 12582916 | tf_op jit(solution)/shard_map/while
  458.7 1.4 copy-start.4
where the time goes:
time: 469 us; the launch traced here: 461 us
  matrix products  229 us (49%)
  blocking collectives  121 us (26%)
  local copies, waits for them, and re-layouts  67.3 us (14%)
  waiting for transfers between devices  25.3 us (5%)
  starting transfers between devices  11 us (2%)
    dot_general x10, matrix products, tile_kernel(): jnp.einsum('tie,tje->tij', source_tiles, target_tiles, precision=HIGHEST)  138 us
    psum x2, blocking collectives, on_device(): column_total = lax.psum(column_partial, 'rows')  121 us
    dot_general x4, matrix products, row_per_group(): jnp.einsum('tij,tj->ti', tiles, column_scale[global_group], precision=HIG...  34.6 us
    gather x10, local copies, waits for them, and re-layouts, affinity_tiles(): fetched[fetch_group]  27.8 us
    gather x10, local copies, waits for them, and re-layouts, affinity_tiles(): source_normalized[source_ids]  27.6 us
    dot_general x4, matrix products, column_per_group(): jnp.einsum('tij,ti->tj', tiles, row_scale[source_ids], precision=HIGHEST)  23.8 us
    all_to_all x1, waiting for transfers between devices, on_device(): lax.all_to_all(outgoing, 'rows', split_axis=0, concat_axis=0, tiled=True)  21.1 us
    dot_general x2, matrix products, accumulate(): jnp.einsum('tij,tje->tie', weights, fetched[fetch_group], precision=HIGHEST)  19 us
  transfers between devices with their start and end apart: 2, of which 2 were waited for; matrix products, arithmetic and copies ran while one was open for 1% of the time, Pallas kernels for 0%

commit v1 on v0

v1 whole, which is shorter than its diff:
```python
import math

import jax
import jax.numpy as jnp
from jax import lax
from jax.experimental import pallas as pl
from jax.experimental.pallas import tpu as pltpu
from jax.sharding import PartitionSpec as P

E = 128
BLOCK = 128
ITERS = 2
SUB = 8

EPSILON = 1e-06
SOFTMAX_WARMTH = 0.03
ROW_MINIMUM = 1.0
COLUMN_FLOOR = 0.01
HIGHEST = lax.Precision.HIGHEST

NT = (((1,), (1,)), ((), ()))


def unit_rows(values):
    return values * lax.rsqrt(jnp.sum(values * values, axis=-1, keepdims=True) + EPSILON)


def _tile(s_ref, t_ref, q, o):
    cosine = lax.dot_general(
        s_ref[q], t_ref[o], NT, precision=HIGHEST, preferred_element_type=jnp.float32
    )
    return jnp.exp(cosine / SOFTMAX_WARMTH)


def _sweep_kernel(src_sm, slot_sm, cnt_sm, s_ref, t_ref, c_ref, r_out, colp_out, k_scr, rs_scr):
    live = cnt_sm[0]
    rs_scr[...] = jnp.zeros_like(rs_scr)
    colp_out[...] = jnp.zeros_like(colp_out)

    def rows(t, carry):
        q = src_sm[t]
        o = slot_sm[t]
        k = _tile(s_ref, t_ref, q, o)
        k_scr[t] = k
        rs_scr[q] += lax.dot_general(
            c_ref[o], k, NT, precision=HIGHEST, preferred_element_type=jnp.float32
        )
        return carry

    lax.fori_loop(0, live, rows, 0)
    r_out[...] = 1.0 / jnp.maximum(rs_scr[...], ROW_MINIMUM)

    def cols(t, carry):
        q = src_sm[t]
        o = slot_sm[t]
        colp_out[o] += jnp.dot(
            r_out[q], k_scr[t], precision=HIGHEST, preferred_element_type=jnp.float32
        )
        return carry

    lax.fori_loop(0, live, cols, 0)


def _final_kernel(src_sm, slot_sm, cnt_sm, s_ref, t_ref, c_ref, al_out, ms_out):
    live = cnt_sm[0]
    al_out[...] = jnp.zeros_like(al_out)
    ms_out[...] = jnp.zeros_like(ms_out)
    ones = jnp.ones((SUB, BLOCK), jnp.float32)

    def body(t, carry):
        q = src_sm[t]
        o = slot_sm[t]
        k = _tile(s_ref, t_ref, q, o)
        kc = k * c_ref[o][0:1, :]
        al_out[q] += jnp.dot(kc, t_ref[o], precision=HIGHEST, preferred_element_type=jnp.float32)
        ms_out[q] += lax.dot_general(
            ones, kc, NT, precision=HIGHEST, preferred_element_type=jnp.float32
        )
        return carry

    lax.fori_loop(0, live, body, 0)


def _specs(n_smem, n_vmem):
    return [pl.BlockSpec(memory_space=pltpu.SMEM)] * n_smem + [
        pl.BlockSpec(memory_space=pltpu.VMEM)
    ] * n_vmem


def sweep(tile_source, tile_slot, tile_count, source_unit, fetched, col8):
    capacity = tile_source.shape[0]
    sb = source_unit.shape[0]
    slots = fetched.shape[0]
    return pl.pallas_call(
        _sweep_kernel,
        out_shape=(
            jax.ShapeDtypeStruct((sb, SUB, BLOCK), jnp.float32),
            jax.ShapeDtypeStruct((slots, SUB, BLOCK), jnp.float32),
        ),
        in_specs=_specs(3, 3),
        out_specs=(pl.BlockSpec(memory_space=pltpu.VMEM),) * 2,
        scratch_shapes=[
            pltpu.VMEM((capacity, BLOCK, BLOCK), jnp.float32),
            pltpu.VMEM((sb, SUB, BLOCK), jnp.float32),
        ],
    )(tile_source, tile_slot, tile_count, source_unit, fetched, col8)


def final(tile_source, tile_slot, tile_count, source_unit, fetched, col8):
    sb = source_unit.shape[0]
    return pl.pallas_call(
        _final_kernel,
        out_shape=(
            jax.ShapeDtypeStruct((sb, BLOCK, E), jnp.float32),
            jax.ShapeDtypeStruct((sb, SUB, BLOCK), jnp.float32),
        ),
        in_specs=_specs(3, 3),
        out_specs=(pl.BlockSpec(memory_space=pltpu.VMEM),) * 2,
    )(tile_source, tile_slot, tile_count, source_unit, fetched, col8)


def on_device(source_emb, target_emb, tile_source, tile_slot, tile_count, wanted):
    rows_n = lax.axis_size("rows")
    need = wanted.shape[1]
    target_blocks = target_emb.shape[0] // BLOCK
    slots = rows_n * need
    source_unit = unit_rows(source_emb).reshape(-1, BLOCK, E)
    asked = lax.all_to_all(wanted, "rows", split_axis=0, concat_axis=0, tiled=True)
    own_unit = unit_rows(target_emb).reshape(target_blocks, BLOCK, E)
    outgoing = own_unit[asked.reshape(-1)]
    fetched = lax.all_to_all(outgoing, "rows", split_axis=0, concat_axis=0, tiled=True)
    owner_match = asked.reshape(slots)[:, None] == jnp.arange(target_blocks)[None, :]

    def column_scale_of(colp8):
        partial = colp8[:, 0, :].reshape(rows_n, need * BLOCK)
        received = lax.all_to_all(partial, "rows", split_axis=0, concat_axis=0, tiled=True)
        received = received.reshape(slots, BLOCK)
        totals = jnp.sum(
            jnp.where(owner_match[:, :, None], received[:, None, :], 0.0), axis=0
        )
        scales = 1.0 / jnp.maximum(totals, COLUMN_FLOOR)
        back = jnp.take(scales, asked.reshape(slots), axis=0).reshape(rows_n, need * BLOCK)
        col = lax.all_to_all(back, "rows", split_axis=0, concat_axis=0, tiled=True)
        return jnp.broadcast_to(col.reshape(slots, 1, BLOCK), (slots, SUB, BLOCK))

    col8 = jnp.ones((slots, SUB, BLOCK), jnp.float32)
    row8 = None
    for iteration in range(ITERS):
        row8, colp8 = sweep(tile_source, tile_slot, tile_count, source_unit, fetched, col8)
        col8 = column_scale_of(colp8)
    al, ms = final(tile_source, tile_slot, tile_count, source_unit, fetched, col8)
    row_scale = row8[:, 0, :]
    aligned = (al * row_scale[:, :, None]) * math.sqrt(E)
    mass = ms[:, 0, :] * row_scale
    return (aligned.reshape(-1, E), mass.reshape(-1))


def solution(mesh):
    placed = (
        P(("groups", "rows"), None),
        P(("groups", "rows"), None),
        P(("groups", "rows")),
        P(("groups", "rows")),
        P(("groups", "rows")),
        P(("groups", "rows"), None),
    )
    return jax.shard_map(
        on_device,
        mesh=mesh,
        in_specs=placed,
        out_specs=(P(("groups", "rows"), None), P(("groups", "rows"))),
        check_vma=False,
    )
```

time: 469 us -> 395 us (0.84)
  the two profiles are of different devices: /device:TPU:0 before, /device:TPU:23 now
where the time goes in v1:
time: 395 us; the launch traced here: 391 us
  Pallas kernels  304 us (77%)
  blocking collectives  26 us (7%)
  waiting for transfers between devices  24.9 us (6%)
  starting transfers between devices  18.6 us (5%)
  local copies, waits for them, and re-layouts  8.6 us (2%)
  other arithmetic  7.65 us (2%)
    pallas_call x2, Pallas kernels, sweep(): pl.pallas_call(_sweep_kernel, out_shape=(jax.ShapeDtypeStruct((sb, SUB, B...  215 us
    pallas_call x1, Pallas kernels, final(): pl.pallas_call(_final_kernel, out_shape=(jax.ShapeDtypeStruct((sb, BLOCK,...  88.9 us
    all_to_all x1, waiting for transfers between devices, on_device(): lax.all_to_all(outgoing, 'rows', split_axis=0, concat_axis=0, tiled=True)  20.5 us
    all_to_all x2, blocking collectives, column_scale_of(): col = lax.all_to_all(back, 'rows', split_axis=0, concat_axis=0, tiled=True)  17.9 us
    all_to_all x1, blocking collectives, column_scale_of(): lax.all_to_all(partial, 'rows', split_axis=0, concat_axis=0, tiled=True)  8.08 us
  transfers between devices with their start and end apart: 3, of which 3 were waited for; matrix products, arithmetic and copies ran while one was open for 1% of the time, Pallas kernels for 0%

profile of v1, /device:TPU:23, one launch (start us, length us, event | category | flops | bytes accessed | tf_op | source)
XLA Modules:
  0.0 390.8 jit_solution(4107856355249121766)
XLA Ops:
  0.6 0.0 copy-start.3
  0.6 0.0 copy-start.2
  0.7 0.6 copy-done.3
  1.3 0.7 copy.14
  2.0 6.4 %all-to-all-start = ((s32[16,1,1]{2,1,0:T(1,128)}), s32[16,1,1]{2,1,0:T(1,128)S(1)}, u32[]{:S(2)}, u32[]{:S(2)}) async-start(s32[16,1,1]{2,1,0:T(1,128)} %copy.14), calls=%async_computation | async-start | bytes 16384 | tf_op jit(solution)/shard_map/all_to_all | solution.py:128
  8.4 1.1 multiply_reduce_fusion.1
  9.5 0.0 copy-done.2
  9.5 0.1 broadcast_multiply_fusion.1
  9.7 1.6 all-to-all-done
  11.2 0.4 reduce
  11.6 1.6 gather_fusion
  13.3 0.0 copy-start.1
  13.3 7.2 %all-to-all-start.1 = ((f32[16,128,128]{2,1,0:T(8,128)}), f32[16,128,128]{2,1,0:T(8,128)S(1)}, u32[]{:S(2)}, u32[]{:S(2)}) async-start(f32[16,128,128]{2,1,0:T(8,128)} %gather_fusion), calls=%async_computation.1 | async-start | bytes 2097152 | tf_op jit(solution)/shard_map/all_to_all | solution.py:131
  21.1 0.0 copy-done.1
  21.1 0.3 multiply_reduce_fusion
  21.5 1.3 broadcast_multiply_fusion
  22.8 20.5 %all-to-all-done.1.t_ref = f32[16,128,128]{2,1,0:T(8,128)S(1)} async-done(((f32[16,128,128]{2,1,0:T(8,128)}), f32[16,128,128]{2,1,0:T(8,128)S(1)}, u32[]{:S(2)}, u32[]{:S(2)}) %all-to-all-start.1) | async-done | bytes 1048608 | tf_op jit(solution)/shard_map/all_to_all | solution.py:131
  43.4 0.0 copy-start
  43.4 0.7 broadcast_in_dim.68.c_ref
  44.0 0.3 copy-done
  44.4 107.3 %shard_map.77 = (f32[16,8,128]{2,1,0:T(8,128)}, f32[16,8,128]{2,1,0:T(8,128)}) custom-call(s32[128]{0:T(128)} %src_sm.5, s32[128]{0:T(128)} %slot_sm.5, s32[1]{0:T(128)S(6)} %copy.17.cnt_sm, f32[16,128,128]{2,1,0:T(8,128)} %bitcast.20, f32[16,128,128]{2,1,0:T(8,128)} %copy-done, f32[16,8,128]{2,1,0:T(8,128)} %broadcast_in_dim.68.c_ref), custom_call_target="tpu_custom_call" | custom-call | tf_op jit(solution)/shard_map/pallas_call | solution.py:94
  151.7 1.4 slice.12
  153.1 5.0 %all-to-all-start.2 = ((f32[16,1,128]{2,1,0:T(1,128)}), f32[16,1,128]{2,1,0:T(1,128)S(1)}, u32[]{:S(2)}, u32[]{:S(2)}) async-start(f32[16,1,128]{2,1,0:T(1,128)} %slice.12), calls=%async_computation.2 | async-start | bytes 16384 | tf_op jit(solution)/shard_map/all_to_all | solution.py:136
  158.1 2.8 all-to-all-done.2
  160.9 0.1 select_reduce_fusion.1
  161.0 0.6 gather_fusion.1
  161.6 0.1 broadcast_select_fusion.1
  161.7 9.0 %all_to_all.47 = f32[16,1,128]{2,1,0:T(1,128)S(1)} all-to-all(f32[16,1,128]{2,1,0:T(1,128)S(1)} %bitcast.31), channel_id=1, replica_groups=mesh['groups'=2,'rows'=16] {'rows'}, dimensions={0} | all-to-all | bytes 16384 | tf_op jit(solution)/shard_map/all_to_all | solution.py:143
  170.6 0.6 broadcast_in_dim.73.c_ref
  171.3 107.3 %shard_map.78 = (f32[16,8,128]{2,1,0:T(8,128)}, f32[16,8,128]{2,1,0:T(8,128)}) custom-call(s32[128]{0:T(128)} %src_sm.5, s32[128]{0:T(128)} %slot_sm.5, s32[1]{0:T(128)S(6)} %copy.17.cnt_sm, f32[16,128,128]{2,1,0:T(8,128)} %bitcast.21, f32[16,128,128]{2,1,0:T(8,128)} %copy-done, f32[16,8,128]{2,1,0:T(8,128)} %broadcast_in_dim.73.c_ref), custom_call_target="tpu_custom_call" | custom-call | tf_op jit(solution)/shard_map/pallas_call | solution.py:94
  278.6 0.8 slice.13
  279.4 8.1 %all_to_all.48 = f32[16,1,128]{2,1,0:T(1,128)S(1)} all-to-all(f32[16,1,128]{2,1,0:T(1,128)S(1)} %slice.13), channel_id=1, replica_groups=mesh['groups'=2,'rows'=16] {'rows'}, dimensions={0} | all-to-all | bytes 16384 | tf_op jit(solution)/shard_map/all_to_all | solution.py:136
  287.5 0.1 select_reduce_fusion
  287.6 0.6 gather_fusion.2
  288.2 0.1 broadcast_select_fusion
  288.3 9.0 %all_to_all.49 = f32[16,1,128]{2,1,0:T(1,128)S(1)} all-to-all(f32[16,1,128]{2,1,0:T(1,128)S(1)} %bitcast.30), channel_id=1, replica_groups=mesh['groups'=2,'rows'=16] {'rows'}, dimensions={0} | all-to-all | bytes 16384 | tf_op jit(solution)/shard_map/all_to_all | solution.py:143
  297.2 0.6 broadcast_in_dim.77.c_ref
  297.9 88.9 %shard_map.79 = (f32[16,128,128]{2,1,0:T(8,128)}, f32[16,8,128]{2,1,0:T(8,128)}) custom-call(s32[128]{0:T(128)} %src_sm.5, s32[128]{0:T(128)} %slot_sm.5, s32[1]{0:T(128)S(6)} %copy.17.cnt_sm, f32[16,128,128]{2,1,0:T(8,128)} %bitcast.22, f32[16,128,128]{2,1,0:T(8,128)} %copy-done, f32[16,8,128]{2,1,0:T(8,128)} %broadcast_in_dim.77.c_ref), custom_call_target="tpu_custom_call" | custom-call | tf_op jit(solution)/shard_map/pallas_call | solution.py:111
  386.8 1.5 slice_multiply_fusion
  388.3 2.5 multiply_multiply_fusion
  (10 shorter events, 0.1 us)
Async XLA Ops:
  0.6 0.7 copy-start.3
  0.6 8.9 %copy-start.2 = (f32[512,128]{1,0:T(8,128)S(1)}, f32[512,128]{1,0:T(8,128)}, u32[]{:S(2)}) copy-start(f32[512,128]{1,0:T(8,128)} %param.9) | copy-start | bytes 786436
  2.0 9.3 %all-to-all-start = ((s32[16,1,1]{2,1,0:T(1,128)}), s32[16,1,1]{2,1,0:T(1,128)S(1)}, u32[]{:S(2)}, u32[]{:S(2)}) async-start(s32[16,1,1]{2,1,0:T(1,128)} %copy.14), calls=%async_computation | async-start | bytes 16384 | tf_op jit(solution)/shard_map/all_to_all | solution.py:128
  13.3 7.9 %copy-start.1 = (f32[2048,128]{1,0:T(8,128)S(1)}, f32[2048,128]{1,0:T(8,128)}, u32[]{:S(2)}) copy-start(f32[2048,128]{1,0:T(8,128)} %param.8) | copy-start | bytes 3145732
  13.3 30.1 %all-to-all-start.1 = ((f32[16,128,128]{2,1,0:T(8,128)}), f32[16,128,128]{2,1,0:T(8,128)S(1)}, u32[]{:S(2)}, u32[]{:S(2)}) async-start(f32[16,128,128]{2,1,0:T(8,128)} %gather_fusion), calls=%async_computation.1 | async-start | bytes 2097152 | tf_op jit(solution)/shard_map/all_to_all | solution.py:131
  43.4 1.0 copy-start
  153.1 7.8 %all-to-all-start.2 = ((f32[16,1,128]{2,1,0:T(1,128)}), f32[16,1,128]{2,1,0:T(1,128)S(1)}, u32[]{:S(2)}, u32[]{:S(2)}) async-start(f32[16,1,128]{2,1,0:T(1,128)} %slice.12), calls=%async_computation.2 | async-start | bytes 16384 | tf_op jit(solution)/shard_map/all_to_all | solution.py:136

commit v2 on v1

v2 whole, which is shorter than its diff:
```python
import math

import jax
import jax.numpy as jnp
from jax import lax
from jax.experimental import pallas as pl
from jax.experimental.pallas import tpu as pltpu
from jax.sharding import PartitionSpec as P

E = 128
BLOCK = 128
ITERS = 2
UNROLL = 4

EPSILON = 1e-06
SOFTMAX_WARMTH = 0.03
ROW_MINIMUM = 1.0
COLUMN_FLOOR = 0.01
HIGHEST = lax.Precision.HIGHEST

NT = (((1,), (1,)), ((), ()))


def unit_rows(values):
    return values * lax.rsqrt(jnp.sum(values * values, axis=-1, keepdims=True) + EPSILON)


def _tile(s_ref, t_ref, q, o):
    cosine = lax.dot_general(
        s_ref[q], t_ref[o], NT, precision=HIGHEST, preferred_element_type=jnp.float32
    )
    return jnp.exp(cosine / SOFTMAX_WARMTH)


def _sweep_kernel(src_sm, slot_sm, live_ref, s_ref, t_ref, c_ref, r_out, colp_out, k_scr, rs_scr):
    capacity = k_scr.shape[0]
    rs_scr[...] = jnp.zeros_like(rs_scr)
    colp_out[...] = jnp.zeros_like(colp_out)

    def rows(t, carry):
        q = src_sm[t]
        o = slot_sm[t]
        k = _tile(s_ref, t_ref, q, o) * live_ref[t]
        k_scr[t] = k
        rs_scr[q] += jnp.sum(k * c_ref[o], axis=1, keepdims=True)
        return carry

    lax.fori_loop(0, capacity, rows, 0, unroll=UNROLL)
    r_out[...] = 1.0 / jnp.maximum(rs_scr[...], ROW_MINIMUM)

    def cols(t, carry):
        q = src_sm[t]
        o = slot_sm[t]
        colp_out[o] += jnp.sum(k_scr[t] * r_out[q], axis=0, keepdims=True)
        return carry

    lax.fori_loop(0, capacity, cols, 0, unroll=UNROLL)


def _final_kernel(src_sm, slot_sm, live_ref, s_ref, t_ref, c_ref, r_ref, al_out, ms_out):
    capacity = src_sm.shape[0]
    al_out[...] = jnp.zeros_like(al_out)
    ms_out[...] = jnp.zeros_like(ms_out)

    def body(t, carry):
        q = src_sm[t]
        o = slot_sm[t]
        kc = (_tile(s_ref, t_ref, q, o) * live_ref[t]) * c_ref[o]
        al_out[q] += jnp.dot(kc, t_ref[o], precision=HIGHEST, preferred_element_type=jnp.float32)
        ms_out[q] += jnp.sum(kc, axis=1, keepdims=True)
        return carry

    lax.fori_loop(0, capacity, body, 0, unroll=UNROLL)
    r = r_ref[...]
    al_out[...] = al_out[...] * r * math.sqrt(E)
    ms_out[...] = ms_out[...] * r


def _specs(n_smem, n_vmem):
    return [pl.BlockSpec(memory_space=pltpu.SMEM)] * n_smem + [
        pl.BlockSpec(memory_space=pltpu.VMEM)
    ] * n_vmem


def sweep(tile_source, tile_slot, live, source_unit, fetched, col):
    capacity = tile_source.shape[0]
    sb = source_unit.shape[0]
    slots = fetched.shape[0]
    return pl.pallas_call(
        _sweep_kernel,
        out_shape=(
            jax.ShapeDtypeStruct((sb, BLOCK, 1), jnp.float32),
            jax.ShapeDtypeStruct((slots, 1, BLOCK), jnp.float32),
        ),
        in_specs=_specs(3, 3),
        out_specs=(pl.BlockSpec(memory_space=pltpu.VMEM),) * 2,
        scratch_shapes=[
            pltpu.VMEM((capacity, BLOCK, BLOCK), jnp.float32),
            pltpu.VMEM((sb, BLOCK, 1), jnp.float32),
        ],
    )(tile_source, tile_slot, live, source_unit, fetched, col)


def final(tile_source, tile_slot, live, source_unit, fetched, col, row):
    sb = source_unit.shape[0]
    return pl.pallas_call(
        _final_kernel,
        out_shape=(
            jax.ShapeDtypeStruct((sb, BLOCK, E), jnp.float32),
            jax.ShapeDtypeStruct((sb, BLOCK, 1), jnp.float32),
        ),
        in_specs=_specs(3, 4),
        out_specs=(pl.BlockSpec(memory_space=pltpu.VMEM),) * 2,
    )(tile_source, tile_slot, live, source_unit, fetched, col, row)


def on_device(source_emb, target_emb, tile_source, tile_slot, tile_count, wanted):
    rows_n = lax.axis_size("rows")
    need = wanted.shape[1]
    target_blocks = target_emb.shape[0] // BLOCK
    slots = rows_n * need
    source_unit = unit_rows(source_emb).reshape(-1, BLOCK, E)
    asked = lax.all_to_all(wanted, "rows", split_axis=0, concat_axis=0, tiled=True)
    own_unit = unit_rows(target_emb).reshape(target_blocks, BLOCK, E)
    outgoing = own_unit[asked.reshape(-1)]
    fetched = lax.all_to_all(outgoing, "rows", split_axis=0, concat_axis=0, tiled=True)
    owner_match = asked.reshape(slots)[:, None] == jnp.arange(target_blocks)[None, :]

    def column_scale_of(colp):
        partial = colp.reshape(rows_n, need * BLOCK)
        received = lax.all_to_all(partial, "rows", split_axis=0, concat_axis=0, tiled=True)
        received = received.reshape(slots, BLOCK)
        totals = jnp.sum(
            jnp.where(owner_match[:, :, None], received[:, None, :], 0.0), axis=0
        )
        scales = 1.0 / jnp.maximum(totals, COLUMN_FLOOR)
        back = jnp.take(scales, asked.reshape(slots), axis=0).reshape(rows_n, need * BLOCK)
        col = lax.all_to_all(back, "rows", split_axis=0, concat_axis=0, tiled=True)
        return col.reshape(slots, 1, BLOCK)

    live = (jnp.arange(tile_source.shape[0]) < tile_count[0]).astype(jnp.float32)
    col = jnp.ones((slots, 1, BLOCK), jnp.float32)
    row = None
    for iteration in range(ITERS):
        row, colp = sweep(tile_source, tile_slot, live, source_unit, fetched, col)
        col = column_scale_of(colp)
    al, ms = final(tile_source, tile_slot, live, source_unit, fetched, col, row)
    return (al.reshape(-1, E), ms.reshape(-1))


def solution(mesh):
    placed = (
        P(("groups", "rows"), None),
        P(("groups", "rows"), None),
        P(("groups", "rows")),
        P(("groups", "rows")),
        P(("groups", "rows")),
        P(("groups", "rows"), None),
    )
    return jax.shard_map(
        on_device,
        mesh=mesh,
        in_specs=placed,
        out_specs=(P(("groups", "rows"), None), P(("groups", "rows"))),
        check_vma=False,
    )
```

time: 395 us -> 218 us (0.55)
  the two profiles are of different devices: /device:TPU:23 before, /device:TPU:0 now
where the time goes in v2:
time: 218 us; the launch traced here: 217 us
  Pallas kernels  126 us (58%)
  waiting for transfers between devices  31.4 us (14%)
  blocking collectives  28.6 us (13%)
  starting transfers between devices  18 us (8%)
  other arithmetic  6.37 us (3%)
  local copies, waits for them, and re-layouts  5.08 us (2%)
    pallas_call x2, Pallas kernels, sweep(): pl.pallas_call(_sweep_kernel, out_shape=(jax.ShapeDtypeStruct((sb, BLOCK,...  64.1 us
    pallas_call x1, Pallas kernels, final(): pl.pallas_call(_final_kernel, out_shape=(jax.ShapeDtypeStruct((sb, BLOCK,...  62.3 us
    all_to_all x1, waiting for transfers between devices, on_device(): lax.all_to_all(outgoing, 'rows', split_axis=0, concat_axis=0, tiled=True)  20 us
    all_to_all x2, blocking collectives, column_scale_of(): col = lax.all_to_all(back, 'rows', split_axis=0, concat_axis=0, tiled=True)  18.8 us
    all_to_all x1, blocking collectives, column_scale_of(): lax.all_to_all(partial, 'rows', split_axis=0, concat_axis=0, tiled=True)  9.75 us
    all_to_all x1, starting transfers between devices, on_device(): lax.all_to_all(wanted, 'rows', split_axis=0, concat_axis=0, tiled=True)  7.39 us
    all_to_all x1, starting transfers between devices, column_scale_of(): lax.all_to_all(partial, 'rows', split_axis=0, concat_axis=0, tiled=True)  6.81 us
    all_to_all x1, waiting for transfers between devices, column_scale_of(): lax.all_to_all(partial, 'rows', split_axis=0, concat_axis=0, tiled=True)  6.38 us
  transfers between devices with their start and end apart: 3, of which 3 were waited for; matrix products, arithmetic and copies ran while one was open for 2% of the time, Pallas kernels for 0%

profile of v2, /device:TPU:0, one launch (start us, length us, event | category | flops | bytes accessed | tf_op | source)
XLA Modules:
  0.0 217.3 jit_solution(13877032438980300638)
XLA Ops:
  0.6 0.0 copy-start.3
  0.6 0.0 copy-start.2
  0.7 0.6 copy-done.3
  1.3 0.7 copy.10
  2.0 7.4 %all-to-all-start = ((s32[16,1,1]{2,1,0:T(1,128)}), s32[16,1,1]{2,1,0:T(1,128)S(1)}, u32[]{:S(2)}, u32[]{:S(2)}) async-start(s32[16,1,1]{2,1,0:T(1,128)} %copy.10), calls=%async_computation | async-start | bytes 16384 | tf_op jit(solution)/shard_map/all_to_all | solution.py:123
  9.4 1.1 multiply_reduce_fusion.1
  10.5 0.0 copy-done.2
  10.5 0.1 broadcast_multiply_fusion.1
  10.6 5.1 %all-to-all-done = s32[16,1,1]{2,1,0:T(1,128)S(1)} async-done(((s32[16,1,1]{2,1,0:T(1,128)}), s32[16,1,1]{2,1,0:T(1,128)S(1)}, u32[]{:S(2)}, u32[]{:S(2)}) %all-to-all-start) | async-done | bytes 96 | tf_op jit(solution)/shard_map/all_to_all | solution.py:123
  15.7 0.4 reduce
  16.1 1.6 gather_fusion
  17.7 0.0 copy-start.1
  17.7 3.8 %all-to-all-start.1 = ((f32[16,128,128]{2,1,0:T(8,128)}), f32[16,128,128]{2,1,0:T(8,128)S(1)}, u32[]{:S(2)}, u32[]{:S(2)}) async-start(f32[16,128,128]{2,1,0:T(8,128)} %gather_fusion), calls=%async_computation.1 | async-start | bytes 2097152 | tf_op jit(solution)/shard_map/all_to_all | solution.py:126
  22.1 0.5 compare_convert_fusion.live_ref
  22.7 0.0 copy-done.1
  22.7 0.3 multiply_reduce_fusion
  23.0 1.3 broadcast_multiply_fusion
  24.4 20.0 %all-to-all-done.1.t_ref = f32[16,128,128]{2,1,0:T(8,128)S(1)} async-done(((f32[16,128,128]{2,1,0:T(8,128)}), f32[16,128,128]{2,1,0:T(8,128)S(1)}, u32[]{:S(2)}, u32[]{:S(2)}) %all-to-all-start.1) | async-done | bytes 1048608 | tf_op jit(solution)/shard_map/all_to_all | solution.py:126
  44.4 0.0 copy-start
  44.4 0.7 broadcast_in_dim.54.c_ref
  45.0 0.4 copy-done
  45.4 32.1 %shard_map.77 = (f32[16,128,1]{2,1,0:T(8,128)}, f32[16,1,128]{2,1,0:T(1,128)}) custom-call(s32[128]{0:T(128)} %src_sm.5, s32[128]{0:T(128)} %slot_sm.5, f32[128]{0:T(128)} %compare_convert_fusion.live_ref, f32[16,128,128]{2,1,0:T(8,128)} %bitcast.15, f32[16,128,128]{2,1,0:T(8,128)} %copy-done, f32[16,1,128]{2,1,0:T(1,128)} %broadcast_in_dim.54.c_ref), custom_call_target="tpu_custom_call" | custom-call | tf_op jit(solution)/shard_map/pallas_call | solution.py:89
  77.5 6.8 %all-to-all-start.2 = ((f32[16,1,128]{2,1,0:T(1,128)}), f32[16,1,128]{2,1,0:T(1,128)S(1)}, u32[]{:S(2)}, u32[]{:S(2)}) async-start(f32[16,1,128]{2,1,0:T(1,128)} %get-tuple-element.8), calls=%async_computation.2 | async-start | bytes 16384 | tf_op jit(solution)/shard_map/all_to_all | solution.py:131
  84.3 6.4 %all-to-all-done.2 = f32[16,1,128]{2,1,0:T(1,128)S(1)} async-done(((f32[16,1,128]{2,1,0:T(1,128)}), f32[16,1,128]{2,1,0:T(1,128)S(1)}, u32[]{:S(2)}, u32[]{:S(2)}) %all-to-all-start.2) | async-done | bytes 8224 | tf_op jit(solution)/shard_map/all_to_all | solution.py:131
  90.7 0.1 select_reduce_fusion.1
  90.8 0.6 gather_fusion.1
  91.4 0.1 broadcast_select_fusion.1
  91.4 9.4 %all_to_all.47.c_ref = f32[16,1,128]{2,1,0:T(1,128)} all-to-all(f32[16,1,128]{2,1,0:T(1,128)S(1)} %bitcast.22), channel_id=1, replica_groups=mesh['groups'=2,'rows'=16] {'rows'}, dimensions={0} | all-to-all | bytes 16384 | tf_op jit(solution)/shard_map/all_to_all | solution.py:138
  100.8 32.1 %shard_map.78 = (f32[16,128,1]{2,1,0:T(8,128)}, f32[16,1,128]{2,1,0:T(1,128)}) custom-call(s32[128]{0:T(128)} %src_sm.5, s32[128]{0:T(128)} %slot_sm.5, f32[128]{0:T(128)} %compare_convert_fusion.live_ref, f32[16,128,128]{2,1,0:T(8,128)} %bitcast.16, f32[16,128,128]{2,1,0:T(8,128)} %copy-done, f32[16,1,128]{2,1,0:T(1,128)} %all_to_all.47.c_ref), custom_call_target="tpu_custom_call" | custom-call | tf_op jit(solution)/shard_map/pallas_call | solution.py:89
  132.9 9.8 %all_to_all.48 = f32[16,1,128]{2,1,0:T(1,128)S(1)} all-to-all(f32[16,1,128]{2,1,0:T(1,128)} %get-tuple-element.9), channel_id=1, replica_groups=mesh['groups'=2,'rows'=16] {'rows'}, dimensions={0} | all-to-all | bytes 16384 | tf_op jit(solution)/shard_map/all_to_all | solution.py:131
  142.7 0.1 select_reduce_fusion
  142.8 0.6 gather_fusion.2
  143.3 0.1 broadcast_select_fusion
  143.4 9.4 %all_to_all.49.c_ref = f32[16,1,128]{2,1,0:T(1,128)} all-to-all(f32[16,1,128]{2,1,0:T(1,128)S(1)} %bitcast.21), channel_id=1, replica_groups=mesh['groups'=2,'rows'=16] {'rows'}, dimensions={0} | all-to-all | bytes 16384 | tf_op jit(solution)/shard_map/all_to_all | solution.py:138
  152.8 62.3 %shard_map.79 = (f32[16,128,128]{2,1,0:T(8,128)}, f32[16,128,1]{2,1,0:T(8,128)}) custom-call(s32[128]{0:T(128)} %src_sm.5, s32[128]{0:T(128)} %slot_sm.5, f32[128]{0:T(128)} %compare_convert_fusion.live_ref, f32[16,128,128]{2,1,0:T(8,128)} %bitcast.17, f32[16,128,128]{2,1,0:T(8,128)} %copy-done, f32[16,1,128]{2,1,0:T(1,128)} %all_to_all.49.c_ref, ...), custom_call_target="tpu_custom_call" | custom-call | tf_op jit(solution)/shard_map/pallas_call | solution.py:106
  215.1 2.2 reduce.2
  (10 shorter events, 0.1 us)
Async XLA Ops:
  0.6 0.7 copy-start.3
  0.6 9.8 %copy-start.2 = (f32[512,128]{1,0:T(8,128)S(1)}, f32[512,128]{1,0:T(8,128)}, u32[]{:S(2)}) copy-start(f32[512,128]{1,0:T(8,128)} %param.9) | copy-start | bytes 786436
  2.0 13.7 %all-to-all-start = ((s32[16,1,1]{2,1,0:T(1,128)}), s32[16,1,1]{2,1,0:T(1,128)S(1)}, u32[]{:S(2)}, u32[]{:S(2)}) async-start(s32[16,1,1]{2,1,0:T(1,128)} %copy.10), calls=%async_computation | async-start | bytes 16384 | tf_op jit(solution)/shard_map/all_to_all | solution.py:123
  17.7 5.0 %copy-start.1 = (f32[2048,128]{1,0:T(8,128)S(1)}, f32[2048,128]{1,0:T(8,128)}, u32[]{:S(2)}) copy-start(f32[2048,128]{1,0:T(8,128)} %param.8) | copy-start | bytes 3145732
  17.7 26.7 %all-to-all-start.1 = ((f32[16,128,128]{2,1,0:T(8,128)}), f32[16,128,128]{2,1,0:T(8,128)S(1)}, u32[]{:S(2)}, u32[]{:S(2)}) async-start(f32[16,128,128]{2,1,0:T(8,128)} %gather_fusion), calls=%async_computation.1 | async-start | bytes 2097152 | tf_op jit(solution)/shard_map/all_to_all | solution.py:126
  44.4 1.0 copy-start
  77.5 13.2 %all-to-all-start.2 = ((f32[16,1,128]{2,1,0:T(1,128)}), f32[16,1,128]{2,1,0:T(1,128)S(1)}, u32[]{:S(2)}, u32[]{:S(2)}) async-start(f32[16,1,128]{2,1,0:T(1,128)} %get-tuple-element.8), calls=%async_computation.2 | async-start | bytes 16384 | tf_op jit(solution)/shard_map/all_to_all | solution.py:131

commit v3 on v2

--- a/solution.py
+++ b/solution.py
@@ -32,16 +32,15 @@
     return jnp.exp(cosine / SOFTMAX_WARMTH)
 
 
-def _sweep_kernel(src_sm, slot_sm, live_ref, s_ref, t_ref, c_ref, r_out, colp_out, k_scr, rs_scr):
-    capacity = k_scr.shape[0]
+def _rows_cols(src_sm, slot_sm, tile_at, k_ref, c_ref, r_out, colp_out, rs_scr):
+    capacity = src_sm.shape[0]
     rs_scr[...] = jnp.zeros_like(rs_scr)
     colp_out[...] = jnp.zeros_like(colp_out)
 
     def rows(t, carry):
         q = src_sm[t]
         o = slot_sm[t]
-        k = _tile(s_ref, t_ref, q, o) * live_ref[t]
-        k_scr[t] = k
+        k = tile_at(t, q, o)
         rs_scr[q] += jnp.sum(k * c_ref[o], axis=1, keepdims=True)
         return carry
 
@@ -51,13 +50,26 @@
     def cols(t, carry):
         q = src_sm[t]
         o = slot_sm[t]
-        colp_out[o] += jnp.sum(k_scr[t] * r_out[q], axis=0, keepdims=True)
+        colp_out[o] += jnp.sum(k_ref[t] * r_out[q], axis=0, keepdims=True)
         return carry
 
     lax.fori_loop(0, capacity, cols, 0, unroll=UNROLL)
 
 
-def _final_kernel(src_sm, slot_sm, live_ref, s_ref, t_ref, c_ref, r_ref, al_out, ms_out):
+def _first_kernel(src_sm, slot_sm, live_ref, s_ref, t_ref, c_ref, k_out, r_out, colp_out, rs_scr):
+    def build(t, q, o):
+        k = _tile(s_ref, t_ref, q, o) * live_ref[t]
+        k_out[t] = k
+        return k
+
+    _rows_cols(src_sm, slot_sm, build, k_out, c_ref, r_out, colp_out, rs_scr)
+
+
+def _again_kernel(src_sm, slot_sm, k_ref, c_ref, r_out, colp_out, rs_scr):
+    _rows_cols(src_sm, slot_sm, lambda t, q, o: k_ref[t], k_ref, c_ref, r_out, colp_out, rs_scr)
+
+
+def _final_kernel(src_sm, slot_sm, k_ref, t_ref, c_ref, r_ref, al_out, ms_out):
     capacity = src_sm.shape[0]
     al_out[...] = jnp.zeros_like(al_out)
     ms_out[...] = jnp.zeros_like(ms_out)
@@ -65,7 +77,7 @@
     def body(t, carry):
         q = src_sm[t]
         o = slot_sm[t]
-        kc = (_tile(s_ref, t_ref, q, o) * live_ref[t]) * c_ref[o]
+        kc = k_ref[t] * c_ref[o]
         al_out[q] += jnp.dot(kc, t_ref[o], precision=HIGHEST, preferred_element_type=jnp.float32)
         ms_out[q] += jnp.sum(kc, axis=1, keepdims=True)
         return carry
@@ -82,36 +94,52 @@
     ] * n_vmem
 
 
-def sweep(tile_source, tile_slot, live, source_unit, fetched, col):
+def _vmem_out(n):
+    return (pl.BlockSpec(memory_space=pltpu.VMEM),) * n
+
+
+def first_sweep(tile_source, tile_slot, live, source_unit, fetched, col):
     capacity = tile_source.shape[0]
     sb = source_unit.shape[0]
     slots = fetched.shape[0]
     return pl.pallas_call(
-        _sweep_kernel,
+        _first_kernel,
+        out_shape=(
+            jax.ShapeDtypeStruct((capacity, BLOCK, BLOCK), jnp.float32),
+            jax.ShapeDtypeStruct((sb, BLOCK, 1), jnp.float32),
+            jax.ShapeDtypeStruct((slots, 1, BLOCK), jnp.float32),
+        ),
+        in_specs=_specs(3, 3),
+        out_specs=_vmem_out(3),
+        scratch_shapes=[pltpu.VMEM((sb, BLOCK, 1), jnp.float32)],
+    )(tile_source, tile_slot, live, source_unit, fetched, col)
+
+
+def again_sweep(tile_source, tile_slot, kernel, col, sb):
+    slots = col.shape[0]
+    return pl.pallas_call(
+        _again_kernel,
         out_shape=(
             jax.ShapeDtypeStruct((sb, BLOCK, 1), jnp.float32),
             jax.ShapeDtypeStruct((slots, 1, BLOCK), jnp.float32),
         ),
-        in_specs=_specs(3, 3),
-        out_specs=(pl.BlockSpec(memory_space=pltpu.VMEM),) * 2,
-        scratch_shapes=[
-            pltpu.VMEM((capacity, BLOCK, BLOCK), jnp.float32),
-            pltpu.VMEM((sb, BLOCK, 1), jnp.float32),
-        ],
-    )(tile_source, tile_slot, live, source_unit, fetched, col)
+        in_specs=_specs(2, 2),
+        out_specs=_vmem_out(2),
+        scratch_shapes=[pltpu.VMEM((sb, BLOCK, 1), jnp.float32)],
+    )(tile_source, tile_slot, kernel, col)
 
 
-def final(tile_source, tile_slot, live, source_unit, fetched, col, row):
-    sb = source_unit.shape[0]
+def final(tile_source, tile_slot, kernel, fetched, col, row):
+    sb = row.shape[0]
     return pl.pallas_call(
         _final_kernel,
         out_shape=(
             jax.ShapeDtypeStruct((sb, BLOCK, E), jnp.float32),
             jax.ShapeDtypeStruct((sb, BLOCK, 1), jnp.float32),
         ),
-        in_specs=_specs(3, 4),
-        out_specs=(pl.BlockSpec(memory_space=pltpu.VMEM),) * 2,
-    )(tile_source, tile_slot, live, source_unit, fetched, col, row)
+        in_specs=_specs(2, 4),
+        out_specs=_vmem_out(2),
+    )(tile_source, tile_slot, kernel, fetched, col, row)
 
 
 def on_device(source_emb, target_emb, tile_source, tile_slot, tile_count, wanted):
@@ -140,11 +168,13 @@
 
     live = (jnp.arange(tile_source.shape[0]) < tile_count[0]).astype(jnp.float32)
     col = jnp.ones((slots, 1, BLOCK), jnp.float32)
-    row = None
-    for iteration in range(ITERS):
-        row, colp = sweep(tile_source, tile_slot, live, source_unit, fetched, col)
+    sb = source_unit.shape[0]
+    kernel, row, colp = first_sweep(tile_source, tile_slot, live, source_unit, fetched, col)
+    for iteration in range(1, ITERS):
         col = column_scale_of(colp)
-    al, ms = final(tile_source, tile_slot, live, source_unit, fetched, col, row)
+        row, colp = again_sweep(tile_source, tile_slot, kernel, col, sb)
+    col = column_scale_of(colp)
+    al, ms = final(tile_source, tile_slot, kernel, fetched, col, row)
     return (al.reshape(-1, E), ms.reshape(-1))
 
 

time: 218 us -> 158 us (0.72)
  Pallas kernels: 126 us -> 66.8 us
  other arithmetic: 6.37 us -> 9.7 us
  waiting for transfers between devices: 31.4 us -> 28.1 us
    pallas_call x1, Pallas kernels: 62.3 us -> 18.3 us  [final(): pl.pallas_call(_final_kernel, out_shape=(jax.ShapeDtypeStruct((sb, BLOCK,...]
    pallas_call x2, Pallas kernels: 64.1 us -> 48.4 us  [the longest x1 34.6 us: first_sweep(): pl.pallas_call(_first_kernel, out_shape=(jax.ShapeDtypeStruct((capacity,...]
    all_to_all x1, waiting for transfers between devices: 20 us -> 17.6 us  [on_device(): lax.all_to_all(outgoing, 'rows', split_axis=0, concat_axis=0, tiled=True)]
  transfers between devices with their start and end apart: 3 -> 3, of which waited for: 3 -> 3; matrix products, arithmetic and copies ran while one was open for 2% -> 4% of each run, Pallas kernels for 0% -> 0%
where the time goes in v3:
time: 158 us
  Pallas kernels  66.8 us (42%)
  blocking collectives  28.9 us (18%)
  waiting for transfers between devices  28.1 us (18%)
  starting transfers between devices  17.9 us (11%)
  other arithmetic  9.7 us (6%)
  local copies, waits for them, and re-layouts  5.14 us (3%)
    pallas_call x1, Pallas kernels, first_sweep(): pl.pallas_call(_first_kernel, out_shape=(jax.ShapeDtypeStruct((capacity,...  34.6 us
    all_to_all x2, blocking collectives, column_scale_of(): col = lax.all_to_all(back, 'rows', split_axis=0, concat_axis=0, tiled=True)  19.1 us
    pallas_call x1, Pallas kernels, final(): pl.pallas_call(_final_kernel, out_shape=(jax.ShapeDtypeStruct((sb, BLOCK,...  18.3 us
    all_to_all x1, waiting for transfers between devices, on_device(): lax.all_to_all(outgoing, 'rows', split_axis=0, concat_axis=0, tiled=True)  17.6 us
    pallas_call x1, Pallas kernels, again_sweep(): pl.pallas_call(_again_kernel, out_shape=(jax.ShapeDtypeStruct((sb, BLOCK,...  13.8 us
    all_to_all x1, blocking collectives, column_scale_of(): lax.all_to_all(partial, 'rows', split_axis=0, concat_axis=0, tiled=True)  9.75 us
    all_to_all x1, starting transfers between devices, on_device(): lax.all_to_all(wanted, 'rows', split_axis=0, concat_axis=0, tiled=True)  7.39 us
    all_to_all x1, starting transfers between devices, column_scale_of(): lax.all_to_all(partial, 'rows', split_axis=0, concat_axis=0, tiled=True)  6.82 us
  transfers between devices with their start and end apart: 3, of which 3 were waited for; matrix products, arithmetic and copies ran while one was open for 4% of the time, Pallas kernels for 0%

profile of v3, /device:TPU:0, one launch (start us, length us, event | category | flops | bytes accessed | tf_op | source)
XLA Modules:
  0.0 157.8 jit_solution(14262237162247667969)
XLA Ops:
  0.6 1.3 copy.10
  2.0 7.4 %all-to-all-start = ((s32[16,1,1]{2,1,0:T(1,128)}), s32[16,1,1]{2,1,0:T(1,128)S(1)}, u32[]{:S(2)}, u32[]{:S(2)}) async-start(s32[16,1,1]{2,1,0:T(1,128)} %copy.10), calls=%async_computation | async-start | bytes 16384 | tf_op jit(solution)/shard_map/all_to_all | solution.py:151
  9.4 1.1 multiply_reduce_fusion.1
  10.5 1.1 broadcast_multiply_fusion.1
  11.6 4.1 %all-to-all-done = s32[16,1,1]{2,1,0:T(1,128)S(1)} async-done(((s32[16,1,1]{2,1,0:T(1,128)}), s32[16,1,1]{2,1,0:T(1,128)S(1)}, u32[]{:S(2)}, u32[]{:S(2)}) %all-to-all-start) | async-done | bytes 96 | tf_op jit(solution)/shard_map/all_to_all | solution.py:151
  15.7 0.4 reduce
  16.1 1.6 %gather_fusion = f32[16,128,128]{2,1,0:T(8,128)} fusion(f32[4,128,128]{2,1,0:T(8,128)S(1)} %bitcast.15, s32[1024]{0:T(1024)S(1)} %pad_clamp_fusion.1), kind=kCustom, calls=%fused_computation.2 | custom fusion | bytes 2097216 | tf_op jit(solution)/shard_map/gather | solution.py:153
  17.7 3.7 %all-to-all-start.1 = ((f32[16,128,128]{2,1,0:T(8,128)}), f32[16,128,128]{2,1,0:T(8,128)S(1)}, u32[]{:S(2)}, u32[]{:S(2)}) async-start(f32[16,128,128]{2,1,0:T(8,128)} %gather_fusion), calls=%async_computation.1 | async-start | bytes 2097152 | tf_op jit(solution)/shard_map/all_to_all | solution.py:154
  22.0 0.5 compare_convert_fusion.live_ref
  22.5 1.6 multiply_reduce_fusion
  24.1 2.5 %broadcast_multiply_fusion = f32[2048,128]{1,0:T(8,128)} fusion(f32[2048,128]{1,0:T(8,128)} %param.8, f32[2048]{0:T(1024)S(1)} %add_rsqrt_fusion), kind=kLoop, calls=%fused_computation.4 | loop fusion | flops 262144 | bytes 2105344 | tf_op jit(solution)/shard_map/mul | solution.py:25
  26.6 17.6 %all-to-all-done.1.t_ref = f32[16,128,128]{2,1,0:T(8,128)S(1)} async-done(((f32[16,128,128]{2,1,0:T(8,128)}), f32[16,128,128]{2,1,0:T(8,128)S(1)}, u32[]{:S(2)}, u32[]{:S(2)}) %all-to-all-start.1) | async-done | bytes 1048608 | tf_op jit(solution)/shard_map/all_to_all | solution.py:154
  44.2 0.0 copy-start
  44.2 0.7 broadcast_in_dim.53.c_ref
  44.9 0.4 copy-done
  45.3 34.6 %shard_map.77 = (f32[128,128,128]{2,1,0:T(8,128)}, f32[16,128,1]{2,1,0:T(8,128)}, f32[16,1,128]{2,1,0:T(1,128)}) custom-call(s32[128]{0:T(128)} %src_sm.5, s32[128]{0:T(128)} %slot_sm.5, f32[128]{0:T(128)} %compare_convert_fusion.live_ref, f32[16,128,128]{2,1,0:T(8,128)} %bitcast.16, f32[16,128,128]{2,1,0:T(8,128)} %copy-done, ...), custom_call_target="tpu_custom_call" | custom-call | tf_op jit(solution)/shard_map/pallas_call | solution.py:105
  79.9 6.8 %all-to-all-start.2 = ((f32[16,1,128]{2,1,0:T(1,128)}), f32[16,1,128]{2,1,0:T(1,128)S(1)}, u32[]{:S(2)}, u32[]{:S(2)}) async-start(f32[16,1,128]{2,1,0:T(1,128)} %get-tuple-element.10), calls=%async_computation.2 | async-start | bytes 16384 | tf_op jit(solution)/shard_map/all_to_all | solution.py:159
  86.8 6.4 %all-to-all-done.2 = f32[16,1,128]{2,1,0:T(1,128)S(1)} async-done(((f32[16,1,128]{2,1,0:T(1,128)}), f32[16,1,128]{2,1,0:T(1,128)S(1)}, u32[]{:S(2)}, u32[]{:S(2)}) %all-to-all-start.2) | async-done | bytes 8224 | tf_op jit(solution)/shard_map/all_to_all | solution.py:159
  93.2 0.1 select_reduce_fusion.1
  93.3 0.6 gather_fusion.1
  93.8 0.1 broadcast_select_fusion.1
  93.9 9.5 %all_to_all.47.c_ref = f32[16,1,128]{2,1,0:T(1,128)} all-to-all(f32[16,1,128]{2,1,0:T(1,128)S(1)} %bitcast.20), channel_id=1, replica_groups=mesh['groups'=2,'rows'=16] {'rows'}, dimensions={0} | all-to-all | bytes 16384 | tf_op jit(solution)/shard_map/all_to_all | solution.py:166
  103.4 13.8 %shard_map.78 = (f32[16,128,1]{2,1,0:T(8,128)}, f32[16,1,128]{2,1,0:T(1,128)}) custom-call(s32[128]{0:T(128)} %src_sm.5, s32[128]{0:T(128)} %slot_sm.5, f32[128,128,128]{2,1,0:T(8,128)} %get-tuple-element.9.k_ref, f32[16,1,128]{2,1,0:T(1,128)} %all_to_all.47.c_ref), custom_call_target="tpu_custom_call" | custom-call | tf_op jit(solution)/shard_map/pallas_call | solution.py:120
  117.2 9.8 %all_to_all.48 = f32[16,1,128]{2,1,0:T(1,128)S(1)} all-to-all(f32[16,1,128]{2,1,0:T(1,128)} %get-tuple-element.11), channel_id=1, replica_groups=mesh['groups'=2,'rows'=16] {'rows'}, dimensions={0} | all-to-all | bytes 16384 | tf_op jit(solution)/shard_map/all_to_all | solution.py:159
  126.9 0.1 select_reduce_fusion
  127.0 0.6 gather_fusion.2
  127.6 0.1 broadcast_select_fusion
  127.7 9.6 %all_to_all.49.c_ref = f32[16,1,128]{2,1,0:T(1,128)} all-to-all(f32[16,1,128]{2,1,0:T(1,128)S(1)} %bitcast.19), channel_id=1, replica_groups=mesh['groups'=2,'rows'=16] {'rows'}, dimensions={0} | all-to-all | bytes 16384 | tf_op jit(solution)/shard_map/all_to_all | solution.py:166
  137.3 18.3 %shard_map.79 = (f32[16,128,128]{2,1,0:T(8,128)}, f32[16,128,1]{2,1,0:T(8,128)}) custom-call(s32[128]{0:T(128)} %src_sm.5, s32[128]{0:T(128)} %slot_sm.5, f32[128,128,128]{2,1,0:T(8,128)} %get-tuple-element.9.k_ref, f32[16,128,128]{2,1,0:T(8,128)} %copy-done, f32[16,1,128]{2,1,0:T(1,128)} %all_to_all.49.c_ref, f32[16,128,1]{2,1,0:T(8,128)} %get-tuple-element.12.r_ref), custom_call_target="tpu_custom_call" | custom-call | tf_op jit(solution)/shard_map/pallas_call | solution.py:134
  155.6 2.2 %reduce.2 = f32[16,128]{1,0:T(8,128)} reduce(f32[16,128,1]{2,1,0:T(8,128)} %get-tuple-element.14, f32[]{:T(128)} %constant.28), dimensions={2}, to_apply=%get-tuple-element.14.reduce_sub_computation | reduce | bytes 16388 | tf_op jit(solution)/shard_map/pallas_call | solution.py:134
  (10 shorter events, 0.1 us)
Async XLA Ops:
  2.0 13.7 %all-to-all-start = ((s32[16,1,1]{2,1,0:T(1,128)}), s32[16,1,1]{2,1,0:T(1,128)S(1)}, u32[]{:S(2)}, u32[]{:S(2)}) async-start(s32[16,1,1]{2,1,0:T(1,128)} %copy.10), calls=%async_computation | async-start | bytes 16384 | tf_op jit(solution)/shard_map/all_to_all | solution.py:151
  17.7 26.6 %all-to-all-start.1 = ((f32[16,128,128]{2,1,0:T(8,128)}), f32[16,128,128]{2,1,0:T(8,128)S(1)}, u32[]{:S(2)}, u32[]{:S(2)}) async-start(f32[16,128,128]{2,1,0:T(8,128)} %gather_fusion), calls=%async_computation.1 | async-start | bytes 2097152 | tf_op jit(solution)/shard_map/all_to_all | solution.py:154
  44.2 1.1 copy-start
  79.9 13.2 %all-to-all-start.2 = ((f32[16,1,128]{2,1,0:T(1,128)}), f32[16,1,128]{2,1,0:T(1,128)S(1)}, u32[]{:S(2)}, u32[]{:S(2)}) async-start(f32[16,1,128]{2,1,0:T(1,128)} %get-tuple-element.10), calls=%async_computation.2 | async-start | bytes 16384 | tf_op jit(solution)/shard_map/all_to_all | solution.py:159

commit v4 on v3

--- a/solution.py
+++ b/solution.py
@@ -18,17 +18,12 @@
 COLUMN_FLOOR = 0.01
 HIGHEST = lax.Precision.HIGHEST
 
-NT = (((1,), (1,)), ((), ()))
-
-
 def unit_rows(values):
     return values * lax.rsqrt(jnp.sum(values * values, axis=-1, keepdims=True) + EPSILON)
 
 
-def _tile(s_ref, t_ref, q, o):
-    cosine = lax.dot_general(
-        s_ref[q], t_ref[o], NT, precision=HIGHEST, preferred_element_type=jnp.float32
-    )
+def _tile(s_ref, tt_ref, q, o):
+    cosine = jnp.dot(s_ref[q], tt_ref[o], precision=HIGHEST, preferred_element_type=jnp.float32)
     return jnp.exp(cosine / SOFTMAX_WARMTH)
 
 
@@ -69,23 +64,25 @@
     _rows_cols(src_sm, slot_sm, lambda t, q, o: k_ref[t], k_ref, c_ref, r_out, colp_out, rs_scr)
 
 
-def _final_kernel(src_sm, slot_sm, k_ref, t_ref, c_ref, r_ref, al_out, ms_out):
+def _final_kernel(src_sm, slot_sm, k_ref, t_ref, c_ref, r_ref, al_out, ms_out, ms_scr):
     capacity = src_sm.shape[0]
     al_out[...] = jnp.zeros_like(al_out)
-    ms_out[...] = jnp.zeros_like(ms_out)
+    ms_scr[...] = jnp.zeros_like(ms_scr)
 
     def body(t, carry):
         q = src_sm[t]
         o = slot_sm[t]
         kc = k_ref[t] * c_ref[o]
         al_out[q] += jnp.dot(kc, t_ref[o], precision=HIGHEST, preferred_element_type=jnp.float32)
-        ms_out[q] += jnp.sum(kc, axis=1, keepdims=True)
+        ms_scr[q] += jnp.sum(kc, axis=1, keepdims=True)
         return carry
 
     lax.fori_loop(0, capacity, body, 0, unroll=UNROLL)
     r = r_ref[...]
     al_out[...] = al_out[...] * r * math.sqrt(E)
-    ms_out[...] = ms_out[...] * r
+    for q in range(ms_out.shape[0]):
+        mass = jnp.broadcast_to(ms_scr[q] * r_ref[q], (BLOCK, BLOCK))
+        ms_out[q : q + 1, :] = jnp.transpose(mass)[0:1, :]
 
 
 def _specs(n_smem, n_vmem):
@@ -135,10 +132,11 @@
         _final_kernel,
         out_shape=(
             jax.ShapeDtypeStruct((sb, BLOCK, E), jnp.float32),
-            jax.ShapeDtypeStruct((sb, BLOCK, 1), jnp.float32),
+            jax.ShapeDtypeStruct((sb, BLOCK), jnp.float32),
         ),
         in_specs=_specs(2, 4),
         out_specs=_vmem_out(2),
+        scratch_shapes=[pltpu.VMEM((sb, BLOCK, 1), jnp.float32)],
     )(tile_source, tile_slot, kernel, fetched, col, row)
 
 
@@ -169,7 +167,8 @@
     live = (jnp.arange(tile_source.shape[0]) < tile_count[0]).astype(jnp.float32)
     col = jnp.ones((slots, 1, BLOCK), jnp.float32)
     sb = source_unit.shape[0]
-    kernel, row, colp = first_sweep(tile_source, tile_slot, live, source_unit, fetched, col)
+    fetched_t = jnp.swapaxes(fetched, 1, 2)
+    kernel, row, colp = first_sweep(tile_source, tile_slot, live, source_unit, fetched_t, col)
     for iteration in range(1, ITERS):
         col = column_scale_of(colp)
         row, colp = again_sweep(tile_source, tile_slot, kernel, col, sb)

time: 158 us -> 148 us (0.937)
  Pallas kernels: 66.8 us -> 57.4 us
  other arithmetic: 9.7 us -> 7.62 us
    pallas_call x1, Pallas kernels: 34.6 us -> 25.3 us  [first_sweep(): pl.pallas_call(_first_kernel, out_shape=(jax.ShapeDtypeStruct((capacity,...]
    pallas_call x1 -> x0, other arithmetic: 2.17 us -> none  [final(): pl.pallas_call(_final_kernel, out_shape=(jax.ShapeDtypeStruct((sb, BLOCK,...]
  transfers between devices with their start and end apart: 3 -> 3, of which waited for: 3 -> 3; matrix products, arithmetic and copies ran while one was open for 4% -> 5% of each run, Pallas kernels for 0% -> 0%
where the time goes in v4:
time: 148 us; the launch traced here: 147 us
  Pallas kernels  57.4 us (39%)
  blocking collectives  28.7 us (19%)
  waiting for transfers between devices  28 us (19%)
  starting transfers between devices  17.9 us (12%)
  other arithmetic  7.62 us (5%)
  local copies, waits for them, and re-layouts  6.07 us (4%)
    pallas_call x1, Pallas kernels, first_sweep(): pl.pallas_call(_first_kernel, out_shape=(jax.ShapeDtypeStruct((capacity,...  25.3 us
    all_to_all x2, blocking collectives, column_scale_of(): col = lax.all_to_all(back, 'rows', split_axis=0, concat_axis=0, tiled=True)  19 us
    pallas_call x1, Pallas kernels, final(): pl.pallas_call(_final_kernel, out_shape=(jax.ShapeDtypeStruct((sb, BLOCK,...  18.3 us
    all_to_all x1, waiting for transfers between devices, on_device(): lax.all_to_all(outgoing, 'rows', split_axis=0, concat_axis=0, tiled=True)  17.5 us
    pallas_call x1, Pallas kernels, again_sweep(): pl.pallas_call(_again_kernel, out_shape=(jax.ShapeDtypeStruct((sb, BLOCK,...  13.8 us
    all_to_all x1, blocking collectives, column_scale_of(): lax.all_to_all(partial, 'rows', split_axis=0, concat_axis=0, tiled=True)  9.75 us
    all_to_all x1, starting transfers between devices, on_device(): lax.all_to_all(wanted, 'rows', split_axis=0, concat_axis=0, tiled=True)  7.39 us
    all_to_all x1, starting transfers between devices, column_scale_of(): lax.all_to_all(partial, 'rows', split_axis=0, concat_axis=0, tiled=True)  6.82 us
  transfers between devices with their start and end apart: 3, of which 3 were waited for; matrix products, arithmetic and copies ran while one was open for 5% of the time, Pallas kernels for 0%

profile of v4, /device:TPU:0, one launch (start us, length us, event | category | flops | bytes accessed | tf_op | source)
XLA Modules:
  0.0 147.1 jit_solution(4729215275104922032)
XLA Ops:
  0.6 1.3 copy.13
  2.0 7.4 %all-to-all-start = ((s32[16,1,1]{2,1,0:T(1,128)}), s32[16,1,1]{2,1,0:T(1,128)S(1)}, u32[]{:S(2)}, u32[]{:S(2)}) async-start(s32[16,1,1]{2,1,0:T(1,128)} %copy.13), calls=%async_computation | async-start | bytes 16384 | tf_op jit(solution)/shard_map/all_to_all | solution.py:149
  9.4 1.1 multiply_reduce_fusion.1
  10.5 1.1 broadcast_multiply_fusion.1
  11.6 4.1 %all-to-all-done = s32[16,1,1]{2,1,0:T(1,128)S(1)} async-done(((s32[16,1,1]{2,1,0:T(1,128)}), s32[16,1,1]{2,1,0:T(1,128)S(1)}, u32[]{:S(2)}, u32[]{:S(2)}) %all-to-all-start) | async-done | bytes 96 | tf_op jit(solution)/shard_map/all_to_all | solution.py:149
  15.7 0.4 reduce
  16.1 1.6 %gather_fusion = f32[16,128,128]{2,1,0:T(8,128)} fusion(f32[4,128,128]{2,1,0:T(8,128)S(1)} %bitcast.17, s32[1024]{0:T(1024)S(1)} %pad_clamp_fusion.1), kind=kCustom, calls=%fused_computation.2 | custom fusion | bytes 2097216 | tf_op jit(solution)/shard_map/gather | solution.py:151
  17.7 3.7 %all-to-all-start.1 = ((f32[16,128,128]{2,1,0:T(8,128)}), f32[16,128,128]{2,1,0:T(8,128)S(1)}, u32[]{:S(2)}, u32[]{:S(2)}) async-start(f32[16,128,128]{2,1,0:T(8,128)} %gather_fusion), calls=%async_computation.1 | async-start | bytes 2097152 | tf_op jit(solution)/shard_map/all_to_all | solution.py:152
  22.0 0.6 compare_convert_fusion.live_ref
  22.6 1.6 %multiply_reduce_fusion = f32[2048]{0:T(1024)S(1)} fusion(f32[2048,128]{1,0:T(8,128)} %param.8), kind=kLoop, calls=%fused_computation.3 | loop fusion | flops 522240 | bytes 1056768 | tf_op jit(solution)/shard_map/reduce_sum | solution.py:22
  24.2 2.5 %broadcast_multiply_fusion = f32[2048,128]{1,0:T(8,128)} fusion(f32[2048,128]{1,0:T(8,128)} %param.8, f32[2048]{0:T(1024)S(1)} %add_rsqrt_fusion), kind=kLoop, calls=%fused_computation.4 | loop fusion | flops 262144 | bytes 2105344 | tf_op jit(solution)/shard_map/mul | solution.py:22
  26.7 17.5 %all-to-all-done.1.t_ref = f32[16,128,128]{2,1,0:T(8,128)S(1)} async-done(((f32[16,128,128]{2,1,0:T(8,128)}), f32[16,128,128]{2,1,0:T(8,128)S(1)}, u32[]{:S(2)}, u32[]{:S(2)}) %all-to-all-start.1) | async-done | bytes 1048608 | tf_op jit(solution)/shard_map/all_to_all | solution.py:152
  44.2 0.0 copy-start
  44.2 1.4 copy.14.t_ref
  45.6 0.6 broadcast_in_dim.53.c_ref
  46.2 25.3 %shard_map.77 = (f32[128,128,128]{2,1,0:T(8,128)}, f32[16,128,1]{2,1,0:T(8,128)}, f32[16,1,128]{2,1,0:T(1,128)}) custom-call(s32[128]{0:T(128)} %src_sm.5, s32[128]{0:T(128)} %slot_sm.5, f32[128]{0:T(128)} %compare_convert_fusion.live_ref, f32[16,128,128]{2,1,0:T(8,128)} %bitcast.18, f32[16,128,128]{2,1,0:T(8,128)} %copy.14.t_ref, ...), custom_call_target="tpu_custom_call" | custom-call | tf_op jit(solution)/shard_map/pallas_call | solution.py:102
  71.6 6.8 %all-to-all-start.2 = ((f32[16,1,128]{2,1,0:T(1,128)}), f32[16,1,128]{2,1,0:T(1,128)S(1)}, u32[]{:S(2)}, u32[]{:S(2)}) async-start(f32[16,1,128]{2,1,0:T(1,128)} %get-tuple-element.10), calls=%async_computation.2 | async-start | bytes 16384 | tf_op jit(solution)/shard_map/all_to_all | solution.py:157
  78.4 6.4 %all-to-all-done.2 = f32[16,1,128]{2,1,0:T(1,128)S(1)} async-done(((f32[16,1,128]{2,1,0:T(1,128)}), f32[16,1,128]{2,1,0:T(1,128)S(1)}, u32[]{:S(2)}, u32[]{:S(2)}) %all-to-all-start.2) | async-done | bytes 8224 | tf_op jit(solution)/shard_map/all_to_all | solution.py:157
  84.8 0.1 select_reduce_fusion.1
  84.9 0.6 gather_fusion.1
  85.5 0.1 broadcast_select_fusion.1
  85.5 9.5 %all_to_all.47.c_ref = f32[16,1,128]{2,1,0:T(1,128)} all-to-all(f32[16,1,128]{2,1,0:T(1,128)S(1)} %bitcast.22), channel_id=1, replica_groups=mesh['groups'=2,'rows'=16] {'rows'}, dimensions={0} | all-to-all | bytes 16384 | tf_op jit(solution)/shard_map/all_to_all | solution.py:164
  95.0 13.8 %shard_map.78 = (f32[16,128,1]{2,1,0:T(8,128)}, f32[16,1,128]{2,1,0:T(1,128)}) custom-call(s32[128]{0:T(128)} %src_sm.5, s32[128]{0:T(128)} %slot_sm.5, f32[128,128,128]{2,1,0:T(8,128)} %get-tuple-element.9.k_ref, f32[16,1,128]{2,1,0:T(1,128)} %all_to_all.47.c_ref), custom_call_target="tpu_custom_call" | custom-call | tf_op jit(solution)/shard_map/pallas_call | solution.py:117
  108.8 9.8 %all_to_all.48 = f32[16,1,128]{2,1,0:T(1,128)S(1)} all-to-all(f32[16,1,128]{2,1,0:T(1,128)} %get-tuple-element.11), channel_id=1, replica_groups=mesh['groups'=2,'rows'=16] {'rows'}, dimensions={0} | all-to-all | bytes 16384 | tf_op jit(solution)/shard_map/all_to_all | solution.py:157
  118.6 0.1 select_reduce_fusion
  118.7 0.6 gather_fusion.2
  119.2 0.1 broadcast_select_fusion
  119.3 9.5 %all_to_all.49.c_ref = f32[16,1,128]{2,1,0:T(1,128)} all-to-all(f32[16,1,128]{2,1,0:T(1,128)S(1)} %bitcast.21), channel_id=1, replica_groups=mesh['groups'=2,'rows'=16] {'rows'}, dimensions={0} | all-to-all | bytes 16384 | tf_op jit(solution)/shard_map/all_to_all | solution.py:164
  128.8 0.0 copy-done
  128.8 18.3 %shard_map.79 = (f32[16,128,128]{2,1,0:T(8,128)}, f32[16,128]{1,0:T(8,128)}) custom-call(s32[128]{0:T(128)} %src_sm.5, s32[128]{0:T(128)} %slot_sm.5, f32[128,128,128]{2,1,0:T(8,128)} %get-tuple-element.9.k_ref, f32[16,128,128]{2,1,0:T(8,128)} %copy-done, f32[16,1,128]{2,1,0:T(1,128)} %all_to_all.49.c_ref, f32[16,128,1]{2,1,0:T(8,128)} %get-tuple-element.12.r_ref), custom_call_target="tpu_custom_call" | custom-call | tf_op jit(solution)/shard_map/pallas_call | solution.py:131
  (10 shorter events, 0.1 us)
Async XLA Ops:
  2.0 13.7 %all-to-all-start = ((s32[16,1,1]{2,1,0:T(1,128)}), s32[16,1,1]{2,1,0:T(1,128)S(1)}, u32[]{:S(2)}, u32[]{:S(2)}) async-start(s32[16,1,1]{2,1,0:T(1,128)} %copy.13), calls=%async_computation | async-start | bytes 16384 | tf_op jit(solution)/shard_map/all_to_all | solution.py:149
  17.7 26.6 %all-to-all-start.1 = ((f32[16,128,128]{2,1,0:T(8,128)}), f32[16,128,128]{2,1,0:T(8,128)S(1)}, u32[]{:S(2)}, u32[]{:S(2)}) async-start(f32[16,128,128]{2,1,0:T(8,128)} %gather_fusion), calls=%async_computation.1 | async-start | bytes 2097152 | tf_op jit(solution)/shard_map/all_to_all | solution.py:152
  44.2 84.6 %copy-start = (f32[16,128,128]{2,1,0:T(8,128)}, f32[16,128,128]{2,1,0:T(8,128)S(1)}, u32[]{:S(2)}) copy-start(f32[16,128,128]{2,1,0:T(8,128)S(1)} %all-to-all-done.1.t_ref) | copy-start | bytes 3145732
  71.6 13.2 %all-to-all-start.2 = ((f32[16,1,128]{2,1,0:T(1,128)}), f32[16,1,128]{2,1,0:T(1,128)S(1)}, u32[]{:S(2)}, u32[]{:S(2)}) async-start(f32[16,1,128]{2,1,0:T(1,128)} %get-tuple-element.10), calls=%async_computation.2 | async-start | bytes 16384 | tf_op jit(solution)/shard_map/all_to_all | solution.py:157

commit v5 on v4

--- a/solution.py
+++ b/solution.py
@@ -27,8 +27,13 @@
     return jnp.exp(cosine / SOFTMAX_WARMTH)
 
 
-def _rows_cols(src_sm, slot_sm, tile_at, k_ref, c_ref, r_out, colp_out, rs_scr):
-    capacity = src_sm.shape[0]
+def _chunk(capacity):
+    return math.gcd(capacity, 16)
+
+
+def _rows_cols(src_sm, slot_sm, tile_at, chunk_done, k_ref, c_ref, r_out, colp_out, rs_scr):
+    capacity = src_sm.shape[0]
+    step = _chunk(capacity)
     rs_scr[...] = jnp.zeros_like(rs_scr)
     colp_out[...] = jnp.zeros_like(colp_out)
 
@@ -39,7 +44,10 @@
         rs_scr[q] += jnp.sum(k * c_ref[o], axis=1, keepdims=True)
         return carry
 
-    lax.fori_loop(0, capacity, rows, 0, unroll=UNROLL)
+    for part in range(capacity // step):
+        chunk_done(part, "before")
+        lax.fori_loop(part * step, (part + 1) * step, rows, 0, unroll=UNROLL)
+        chunk_done(part, "after")
     r_out[...] = 1.0 / jnp.maximum(rs_scr[...], ROW_MINIMUM)
 
     def cols(t, carry):
@@ -51,33 +59,71 @@
     lax.fori_loop(0, capacity, cols, 0, unroll=UNROLL)
 
 
-def _first_kernel(src_sm, slot_sm, live_ref, s_ref, t_ref, c_ref, k_out, r_out, colp_out, rs_scr):
+def _chunk_copies(src, dst, sems, capacity):
+    step = _chunk(capacity)
+    return [
+        pltpu.make_async_copy(
+            src.at[pl.ds(part * step, step)], dst.at[pl.ds(part * step, step)], sems.at[part]
+        )
+        for part in range(capacity // step)
+    ]
+
+
+def _first_kernel(
+    src_sm, slot_sm, live_ref, s_ref, tt_ref, c_ref, k_hbm, r_out, colp_out, k_scr, rs_scr, sems
+):
+    capacity = src_sm.shape[0]
+    copies = _chunk_copies(k_scr, k_hbm, sems, capacity)
+
     def build(t, q, o):
-        k = _tile(s_ref, t_ref, q, o) * live_ref[t]
-        k_out[t] = k
+        k = _tile(s_ref, tt_ref, q, o) * live_ref[t]
+        k_scr[t] = k
         return k
 
-    _rows_cols(src_sm, slot_sm, build, k_out, c_ref, r_out, colp_out, rs_scr)
-
-
-def _again_kernel(src_sm, slot_sm, k_ref, c_ref, r_out, colp_out, rs_scr):
-    _rows_cols(src_sm, slot_sm, lambda t, q, o: k_ref[t], k_ref, c_ref, r_out, colp_out, rs_scr)
-
-
-def _final_kernel(src_sm, slot_sm, k_ref, t_ref, c_ref, r_ref, al_out, ms_out, ms_scr):
-    capacity = src_sm.shape[0]
+    def chunk_done(part, when):
+        if when == "after":
+            copies[part].start()
+
+    _rows_cols(src_sm, slot_sm, build, chunk_done, k_scr, c_ref, r_out, colp_out, rs_scr)
+    for copy in copies:
+        copy.wait()
+
+
+def _again_kernel(src_sm, slot_sm, k_hbm, c_ref, r_out, colp_out, k_scr, rs_scr, sems):
+    capacity = src_sm.shape[0]
+    copies = _chunk_copies(k_hbm, k_scr, sems, capacity)
+    for copy in copies:
+        copy.start()
+
+    def chunk_done(part, when):
+        if when == "before":
+            copies[part].wait()
+
+    _rows_cols(
+        src_sm, slot_sm, lambda t, q, o: k_scr[t], chunk_done, k_scr, c_ref, r_out, colp_out, rs_scr
+    )
+
+
+def _final_kernel(src_sm, slot_sm, k_hbm, t_ref, c_ref, r_ref, al_out, ms_out, k_scr, ms_scr, sems):
+    capacity = src_sm.shape[0]
+    step = _chunk(capacity)
+    copies = _chunk_copies(k_hbm, k_scr, sems, capacity)
+    for copy in copies:
+        copy.start()
     al_out[...] = jnp.zeros_like(al_out)
     ms_scr[...] = jnp.zeros_like(ms_scr)
 
     def body(t, carry):
         q = src_sm[t]
         o = slot_sm[t]
-        kc = k_ref[t] * c_ref[o]
+        kc = k_scr[t] * c_ref[o]
         al_out[q] += jnp.dot(kc, t_ref[o], precision=HIGHEST, preferred_element_type=jnp.float32)
         ms_scr[q] += jnp.sum(kc, axis=1, keepdims=True)
         return carry
 
-    lax.fori_loop(0, capacity, body, 0, unroll=UNROLL)
+    for part in range(capacity // step):
+        copies[part].wait()
+        lax.fori_loop(part * step, (part + 1) * step, body, 0, unroll=UNROLL)
     r = r_ref[...]
     al_out[...] = al_out[...] * r * math.sqrt(E)
     for q in range(ms_out.shape[0]):
@@ -95,10 +141,13 @@
     return (pl.BlockSpec(memory_space=pltpu.VMEM),) * n
 
 
-def first_sweep(tile_source, tile_slot, live, source_unit, fetched, col):
+_ANY = pl.BlockSpec(memory_space=pl.ANY)
+
+
+def first_sweep(tile_source, tile_slot, live, source_unit, fetched_t, col):
     capacity = tile_source.shape[0]
     sb = source_unit.shape[0]
-    slots = fetched.shape[0]
+    slots = fetched_t.shape[0]
     return pl.pallas_call(
         _first_kernel,
         out_shape=(
@@ -107,12 +156,17 @@
             jax.ShapeDtypeStruct((slots, 1, BLOCK), jnp.float32),
         ),
         in_specs=_specs(3, 3),
-        out_specs=_vmem_out(3),
-        scratch_shapes=[pltpu.VMEM((sb, BLOCK, 1), jnp.float32)],
-    )(tile_source, tile_slot, live, source_unit, fetched, col)
+        out_specs=(_ANY,) + _vmem_out(2),
+        scratch_shapes=[
+            pltpu.VMEM((capacity, BLOCK, BLOCK), jnp.float32),
+            pltpu.VMEM((sb, BLOCK, 1), jnp.float32),
+            pltpu.SemaphoreType.DMA((capacity // _chunk(capacity),)),
+        ],
+    )(tile_source, tile_slot, live, source_unit, fetched_t, col)
 
 
 def again_sweep(tile_source, tile_slot, kernel, col, sb):
+    capacity = tile_source.shape[0]
     slots = col.shape[0]
     return pl.pallas_call(
         _again_kernel,
@@ -120,13 +174,18 @@
             jax.ShapeDtypeStruct((sb, BLOCK, 1), jnp.float32),
             jax.ShapeDtypeStruct((slots, 1, BLOCK), jnp.float32),
         ),
-        in_specs=_specs(2, 2),
+        in_specs=_specs(2, 0) + [_ANY] + _specs(0, 1),
         out_specs=_vmem_out(2),
-        scratch_shapes=[pltpu.VMEM((sb, BLOCK, 1), jnp.float32)],
+        scratch_shapes=[
+            pltpu.VMEM((capacity, BLOCK, BLOCK), jnp.float32),
+            pltpu.VMEM((sb, BLOCK, 1), jnp.float32),
+            pltpu.SemaphoreType.DMA((capacity // _chunk(capacity),)),
+        ],
     )(tile_source, tile_slot, kernel, col)
 
 
 def final(tile_source, tile_slot, kernel, fetched, col, row):
+    capacity = tile_source.shape[0]
     sb = row.shape[0]
     return pl.pallas_call(
         _final_kernel,
@@ -134,9 +193,13 @@
             jax.ShapeDtypeStruct((sb, BLOCK, E), jnp.float32),
             jax.ShapeDtypeStruct((sb, BLOCK), jnp.float32),
         ),
-        in_specs=_specs(2, 4),
+        in_specs=_specs(2, 0) + [_ANY] + _specs(0, 3),
         out_specs=_vmem_out(2),
-        scratch_shapes=[pltpu.VMEM((sb, BLOCK, 1), jnp.float32)],
+        scratch_shapes=[
+            pltpu.VMEM((capacity, BLOCK, BLOCK), jnp.float32),
+            pltpu.VMEM((sb, BLOCK, 1), jnp.float32),
+            pltpu.SemaphoreType.DMA((capacity // _chunk(capacity),)),
+        ],
     )(tile_source, tile_slot, kernel, fetched, col, row)
 
 

time: 148 us -> 143 us (0.966)
  Pallas kernels: 57.4 us -> 52.4 us
    pallas_call x1, Pallas kernels: 25.3 us -> 23 us  [first_sweep(): pl.pallas_call(_first_kernel, out_shape=(jax.ShapeDtypeStruct((capacity,...]
where the time goes in v5:
time: 143 us; the launch traced here: 142 us
  Pallas kernels  52.4 us (37%)
  blocking collectives  28.7 us (20%)
  waiting for transfers between devices  28 us (20%)
  starting transfers between devices  17.9 us (13%)
  other arithmetic  7.62 us (5%)
  local copies, waits for them, and re-layouts  6.07 us (4%)
    pallas_call x1, Pallas kernels, first_sweep(): pl.pallas_call(_first_kernel, out_shape=(jax.ShapeDtypeStruct((capacity,...  23 us
    all_to_all x2, blocking collectives, column_scale_of(): col = lax.all_to_all(back, 'rows', split_axis=0, concat_axis=0, tiled=True)  19 us
    all_to_all x1, waiting for transfers between devices, on_device(): lax.all_to_all(outgoing, 'rows', split_axis=0, concat_axis=0, tiled=True)  17.5 us
    pallas_call x1, Pallas kernels, final(): pl.pallas_call(_final_kernel, out_shape=(jax.ShapeDtypeStruct((sb, BLOCK,...  17.1 us
    pallas_call x1, Pallas kernels, again_sweep(): pl.pallas_call(_again_kernel, out_shape=(jax.ShapeDtypeStruct((sb, BLOCK,...  12.3 us
    all_to_all x1, blocking collectives, column_scale_of(): lax.all_to_all(partial, 'rows', split_axis=0, concat_axis=0, tiled=True)  9.76 us
    all_to_all x1, starting transfers between devices, on_device(): lax.all_to_all(wanted, 'rows', split_axis=0, concat_axis=0, tiled=True)  7.39 us
    all_to_all x1, starting transfers between devices, column_scale_of(): lax.all_to_all(partial, 'rows', split_axis=0, concat_axis=0, tiled=True)  6.82 us
  transfers between devices with their start and end apart: 3, of which 3 were waited for; matrix products, arithmetic and copies ran while one was open for 5% of the time, Pallas kernels for 0%

profile of v5, /device:TPU:0, one launch (start us, length us, event | category | flops | bytes accessed | tf_op | source)
XLA Modules:
  0.0 142.1 jit_solution(2035075183115932438)
XLA Ops:
  0.6 1.3 copy.13
  2.0 7.4 %all-to-all-start = ((s32[16,1,1]{2,1,0:T(1,128)}), s32[16,1,1]{2,1,0:T(1,128)S(1)}, u32[]{:S(2)}, u32[]{:S(2)}) async-start(s32[16,1,1]{2,1,0:T(1,128)} %copy.13), calls=%async_computation | async-start | bytes 16384 | tf_op jit(solution)/shard_map/all_to_all | solution.py:212
  9.4 1.1 multiply_reduce_fusion.1
  10.5 1.1 broadcast_multiply_fusion.1
  11.6 4.1 %all-to-all-done = s32[16,1,1]{2,1,0:T(1,128)S(1)} async-done(((s32[16,1,1]{2,1,0:T(1,128)}), s32[16,1,1]{2,1,0:T(1,128)S(1)}, u32[]{:S(2)}, u32[]{:S(2)}) %all-to-all-start) | async-done | bytes 96 | tf_op jit(solution)/shard_map/all_to_all | solution.py:212
  15.7 0.4 reduce
  16.1 1.6 %gather_fusion = f32[16,128,128]{2,1,0:T(8,128)} fusion(f32[4,128,128]{2,1,0:T(8,128)S(1)} %bitcast.17, s32[1024]{0:T(1024)S(1)} %pad_clamp_fusion.1), kind=kCustom, calls=%fused_computation.2 | custom fusion | bytes 2097216 | tf_op jit(solution)/shard_map/gather | solution.py:214
  17.7 3.7 %all-to-all-start.1 = ((f32[16,128,128]{2,1,0:T(8,128)}), f32[16,128,128]{2,1,0:T(8,128)S(1)}, u32[]{:S(2)}, u32[]{:S(2)}) async-start(f32[16,128,128]{2,1,0:T(8,128)} %gather_fusion), calls=%async_computation.1 | async-start | bytes 2097152 | tf_op jit(solution)/shard_map/all_to_all | solution.py:215
  22.0 0.6 compare_convert_fusion.live_ref
  22.6 1.6 %multiply_reduce_fusion = f32[2048]{0:T(1024)S(1)} fusion(f32[2048,128]{1,0:T(8,128)} %param.8), kind=kLoop, calls=%fused_computation.3 | loop fusion | flops 522240 | bytes 1056768 | tf_op jit(solution)/shard_map/reduce_sum | solution.py:22
  24.2 2.5 %broadcast_multiply_fusion = f32[2048,128]{1,0:T(8,128)} fusion(f32[2048,128]{1,0:T(8,128)} %param.8, f32[2048]{0:T(1024)S(1)} %add_rsqrt_fusion), kind=kLoop, calls=%fused_computation.4 | loop fusion | flops 262144 | bytes 2105344 | tf_op jit(solution)/shard_map/mul | solution.py:22
  26.7 17.5 %all-to-all-done.1.t_ref = f32[16,128,128]{2,1,0:T(8,128)S(1)} async-done(((f32[16,128,128]{2,1,0:T(8,128)}), f32[16,128,128]{2,1,0:T(8,128)S(1)}, u32[]{:S(2)}, u32[]{:S(2)}) %all-to-all-start.1) | async-done | bytes 1048608 | tf_op jit(solution)/shard_map/all_to_all | solution.py:215
  44.2 0.0 copy-start
  44.2 1.4 copy.14.tt_ref
  45.6 0.6 broadcast_in_dim.53.c_ref
  46.2 23.0 %shard_map.77 = (f32[128,128,128]{2,1,0:T(8,128)}, f32[16,128,1]{2,1,0:T(8,128)}, f32[16,1,128]{2,1,0:T(1,128)}) custom-call(s32[128]{0:T(128)} %src_sm.5, s32[128]{0:T(128)} %slot_sm.5, f32[128]{0:T(128)} %compare_convert_fusion.live_ref, f32[16,128,128]{2,1,0:T(8,128)} %bitcast.18, f32[16,128,128]{2,1,0:T(8,128)} %copy.14.tt_ref, ...), custom_call_target="tpu_custom_call" | custom-call | tf_op jit(solution)/shard_map/pallas_call | solution.py:151
  69.2 6.8 %all-to-all-start.2 = ((f32[16,1,128]{2,1,0:T(1,128)}), f32[16,1,128]{2,1,0:T(1,128)S(1)}, u32[]{:S(2)}, u32[]{:S(2)}) async-start(f32[16,1,128]{2,1,0:T(1,128)} %get-tuple-element.10), calls=%async_computation.2 | async-start | bytes 16384 | tf_op jit(solution)/shard_map/all_to_all | solution.py:220
  76.1 6.4 %all-to-all-done.2 = f32[16,1,128]{2,1,0:T(1,128)S(1)} async-done(((f32[16,1,128]{2,1,0:T(1,128)}), f32[16,1,128]{2,1,0:T(1,128)S(1)}, u32[]{:S(2)}, u32[]{:S(2)}) %all-to-all-start.2) | async-done | bytes 8224 | tf_op jit(solution)/shard_map/all_to_all | solution.py:220
  82.5 0.1 select_reduce_fusion.1
  82.6 0.6 gather_fusion.1
  83.1 0.1 broadcast_select_fusion.1
  83.2 9.5 %all_to_all.47.c_ref = f32[16,1,128]{2,1,0:T(1,128)} all-to-all(f32[16,1,128]{2,1,0:T(1,128)S(1)} %bitcast.22), channel_id=1, replica_groups=mesh['groups'=2,'rows'=16] {'rows'}, dimensions={0} | all-to-all | bytes 16384 | tf_op jit(solution)/shard_map/all_to_all | solution.py:227
  92.7 12.3 %shard_map.78 = (f32[16,128,1]{2,1,0:T(8,128)}, f32[16,1,128]{2,1,0:T(1,128)}) custom-call(s32[128]{0:T(128)} %src_sm.5, s32[128]{0:T(128)} %slot_sm.5, f32[128,128,128]{2,1,0:T(8,128)} %get-tuple-element.9.k_hbm, f32[16,1,128]{2,1,0:T(1,128)} %all_to_all.47.c_ref), custom_call_target="tpu_custom_call" | custom-call | tf_op jit(solution)/shard_map/pallas_call | solution.py:171
  105.0 9.8 %all_to_all.48 = f32[16,1,128]{2,1,0:T(1,128)S(1)} all-to-all(f32[16,1,128]{2,1,0:T(1,128)} %get-tuple-element.11), channel_id=1, replica_groups=mesh['groups'=2,'rows'=16] {'rows'}, dimensions={0} | all-to-all | bytes 16384 | tf_op jit(solution)/shard_map/all_to_all | solution.py:220
  114.8 0.1 select_reduce_fusion
  114.9 0.6 gather_fusion.2
  115.5 0.1 broadcast_select_fusion
  115.6 9.5 %all_to_all.49.c_ref = f32[16,1,128]{2,1,0:T(1,128)} all-to-all(f32[16,1,128]{2,1,0:T(1,128)S(1)} %bitcast.21), channel_id=1, replica_groups=mesh['groups'=2,'rows'=16] {'rows'}, dimensions={0} | all-to-all | bytes 16384 | tf_op jit(solution)/shard_map/all_to_all | solution.py:227
  125.0 0.0 copy-done
  125.0 17.1 %shard_map.79 = (f32[16,128,128]{2,1,0:T(8,128)}, f32[16,128]{1,0:T(8,128)}) custom-call(s32[128]{0:T(128)} %src_sm.5, s32[128]{0:T(128)} %slot_sm.5, f32[128,128,128]{2,1,0:T(8,128)} %get-tuple-element.9.k_hbm, f32[16,128,128]{2,1,0:T(8,128)} %copy-done, f32[16,1,128]{2,1,0:T(1,128)} %all_to_all.49.c_ref, f32[16,128,1]{2,1,0:T(8,128)} %get-tuple-element.12.r_ref), custom_call_target="tpu_custom_call" | custom-call | tf_op jit(solution)/shard_map/pallas_call | solution.py:190
  (10 shorter events, 0.1 us)
Async XLA Ops:
  2.0 13.7 %all-to-all-start = ((s32[16,1,1]{2,1,0:T(1,128)}), s32[16,1,1]{2,1,0:T(1,128)S(1)}, u32[]{:S(2)}, u32[]{:S(2)}) async-start(s32[16,1,1]{2,1,0:T(1,128)} %copy.13), calls=%async_computation | async-start | bytes 16384 | tf_op jit(solution)/shard_map/all_to_all | solution.py:212
  17.7 26.6 %all-to-all-start.1 = ((f32[16,128,128]{2,1,0:T(8,128)}), f32[16,128,128]{2,1,0:T(8,128)S(1)}, u32[]{:S(2)}, u32[]{:S(2)}) async-start(f32[16,128,128]{2,1,0:T(8,128)} %gather_fusion), calls=%async_computation.1 | async-start | bytes 2097152 | tf_op jit(solution)/shard_map/all_to_all | solution.py:215
  44.2 80.8 %copy-start = (f32[16,128,128]{2,1,0:T(8,128)}, f32[16,128,128]{2,1,0:T(8,128)S(1)}, u32[]{:S(2)}) copy-start(f32[16,128,128]{2,1,0:T(8,128)S(1)} %all-to-all-done.1.t_ref) | copy-start | bytes 3145732
  69.2 13.2 %all-to-all-start.2 = ((f32[16,1,128]{2,1,0:T(1,128)}), f32[16,1,128]{2,1,0:T(1,128)S(1)}, u32[]{:S(2)}, u32[]{:S(2)}) async-start(f32[16,1,128]{2,1,0:T(1,128)} %get-tuple-element.10), calls=%async_computation.2 | async-start | bytes 16384 | tf_op jit(solution)/shard_map/all_to_all | solution.py:220

commit v6 on v5

--- a/solution.py
+++ b/solution.py
@@ -209,23 +209,26 @@
     target_blocks = target_emb.shape[0] // BLOCK
     slots = rows_n * need
     source_unit = unit_rows(source_emb).reshape(-1, BLOCK, E)
-    asked = lax.all_to_all(wanted, "rows", split_axis=0, concat_axis=0, tiled=True)
+    owners = rows_n
+    wanted_row = wanted.reshape(1, slots)
+    wanted_all = lax.all_to_all(
+        jnp.broadcast_to(wanted_row, (rows_n, slots)), "rows", split_axis=0, concat_axis=0, tiled=True
+    )
+    me = lax.axis_index("rows")
+    asked = lax.dynamic_slice_in_dim(wanted_all, me * need, need, axis=1)
     own_unit = unit_rows(target_emb).reshape(target_blocks, BLOCK, E)
     outgoing = own_unit[asked.reshape(-1)]
     fetched = lax.all_to_all(outgoing, "rows", split_axis=0, concat_axis=0, tiled=True)
-    owner_match = asked.reshape(slots)[:, None] == jnp.arange(target_blocks)[None, :]
+    same_block = (
+        wanted_all.reshape(rows_n, owners, need, 1) == wanted.reshape(1, owners, 1, need)
+    )[..., None]
 
     def column_scale_of(colp):
-        partial = colp.reshape(rows_n, need * BLOCK)
-        received = lax.all_to_all(partial, "rows", split_axis=0, concat_axis=0, tiled=True)
-        received = received.reshape(slots, BLOCK)
-        totals = jnp.sum(
-            jnp.where(owner_match[:, :, None], received[:, None, :], 0.0), axis=0
-        )
-        scales = 1.0 / jnp.maximum(totals, COLUMN_FLOOR)
-        back = jnp.take(scales, asked.reshape(slots), axis=0).reshape(rows_n, need * BLOCK)
-        col = lax.all_to_all(back, "rows", split_axis=0, concat_axis=0, tiled=True)
-        return col.reshape(slots, 1, BLOCK)
+        spread = jnp.broadcast_to(colp.reshape(1, slots, BLOCK), (rows_n, slots, BLOCK))
+        gathered = lax.all_to_all(spread, "rows", split_axis=0, concat_axis=0, tiled=True)
+        gathered = gathered.reshape(rows_n, owners, need, 1, BLOCK)
+        totals = jnp.sum(jnp.where(same_block, gathered, 0.0), axis=(0, 2))
+        return (1.0 / jnp.maximum(totals, COLUMN_FLOOR)).reshape(slots, 1, BLOCK)
 
     live = (jnp.arange(tile_source.shape[0]) < tile_count[0]).astype(jnp.float32)
     col = jnp.ones((slots, 1, BLOCK), jnp.float32)

time: 143 us -> 128 us (0.90)
  blocking collectives: 28.7 us -> 10.5 us
  waiting for transfers between devices: 28 us -> 29.6 us
    all_to_all x3 -> x1, blocking collectives: 28.7 us -> 10.5 us  [column_scale_of(): lax.all_to_all(spread, 'rows', split_axis=0, concat_axis=0, tiled=True)]
    broadcast_in_dim x1 -> x3, local copies, waits for them, and re-layouts: 0.6 us -> 3.39 us  [the longest x2 2.07 us: column_scale_of(): jnp.broadcast_to(colp.reshape(1, slots, BLOCK), (rows_n, slots, BLOCK))]
    all_to_all x2, waiting for transfers between devices: 10.5 us -> 12 us  [the longest x1 7.91 us: column_scale_of(): lax.all_to_all(spread, 'rows', split_axis=0, concat_axis=0, tiled=True)]
where the time goes in v6:
time: 128 us
  Pallas kernels  52.4 us (41%)
  waiting for transfers between devices  29.6 us (23%)
  starting transfers between devices  17.8 us (14%)
  blocking collectives  10.5 us (8%)
  other arithmetic  8.29 us (6%)
  local copies, waits for them, and re-layouts  7.44 us (6%)
  between operations  1.41 us (1%)
    pallas_call x1, Pallas kernels, first_sweep(): pl.pallas_call(_first_kernel, out_shape=(jax.ShapeDtypeStruct((capacity,...  23 us
    all_to_all x1, waiting for transfers between devices, on_device(): lax.all_to_all(outgoing, 'rows', split_axis=0, concat_axis=0, tiled=True)  17.5 us
    pallas_call x1, Pallas kernels, final(): pl.pallas_call(_final_kernel, out_shape=(jax.ShapeDtypeStruct((sb, BLOCK,...  17.1 us
    pallas_call x1, Pallas kernels, again_sweep(): pl.pallas_call(_again_kernel, out_shape=(jax.ShapeDtypeStruct((sb, BLOCK,...  12.3 us
    all_to_all x1, blocking collectives, column_scale_of(): lax.all_to_all(spread, 'rows', split_axis=0, concat_axis=0, tiled=True)  10.5 us
    all_to_all x1, waiting for transfers between devices, column_scale_of(): lax.all_to_all(spread, 'rows', split_axis=0, concat_axis=0, tiled=True)  7.91 us
    all_to_all x1, starting transfers between devices, on_device(): lax.all_to_all(jnp.broadcast_to(wanted_row, (rows_n, slots)), 'rows', spl...  7.39 us
    all_to_all x1, starting transfers between devices, column_scale_of(): lax.all_to_all(spread, 'rows', split_axis=0, concat_axis=0, tiled=True)  6.81 us
  transfers between devices with their start and end apart: 3, of which 3 were waited for; matrix products, arithmetic and copies ran while one was open for 5% of the time, Pallas kernels for 0%

profile of v6, /device:TPU:0, one launch (start us, length us, event | category | flops | bytes accessed | tf_op | source)
XLA Modules:
  0.0 127.5 jit_solution(13098805627698452072)
XLA Ops:
  0.6 0.0 copy-start.1
  0.6 1.3 %broadcast_in_dim.42 = s32[16,1,16]{2,1,0:T(1,128)} broadcast(s32[16]{0:T(128)} %bitcast.27), dimensions={2} | broadcast | bytes 1088 | tf_op jit(solution)/shard_map/broadcast_in_dim | solution.py:215
  2.0 7.4 %all-to-all-start = ((s32[16,1,16]{2,1,0:T(1,128)}), s32[16,1,16]{2,1,0:T(1,128)S(1)}, u32[]{:S(2)}, u32[]{:S(2)}) async-start(s32[16,1,16]{2,1,0:T(1,128)} %broadcast_in_dim.42), calls=%async_computation | async-start | bytes 16384 | tf_op jit(solution)/shard_map/all_to_all | solution.py:214
  9.4 1.1 multiply_reduce_fusion.1
  10.5 1.1 broadcast_multiply_fusion.1
  11.6 4.1 %all-to-all-done = s32[16,1,16]{2,1,0:T(1,128)S(1)} async-done(((s32[16,1,16]{2,1,0:T(1,128)}), s32[16,1,16]{2,1,0:T(1,128)S(1)}, u32[]{:S(2)}, u32[]{:S(2)}) %all-to-all-start) | async-done | bytes 1056 | tf_op jit(solution)/shard_map/all_to_all | solution.py:214
  15.7 0.4 dynamic-slice_reduce_fusion
  16.2 1.6 %gather_fusion = f32[16,128,128]{2,1,0:T(8,128)} fusion(f32[4,128,128]{2,1,0:T(8,128)S(1)} %bitcast.20, s32[1024]{0:T(1024)S(1)} %pad_clamp_fusion), kind=kCustom, calls=%fused_computation | custom fusion | bytes 2097216 | tf_op jit(solution)/shard_map/gather | solution.py:220
  17.8 3.7 %all-to-all-start.1 = ((f32[16,128,128]{2,1,0:T(8,128)}), f32[16,128,128]{2,1,0:T(8,128)S(1)}, u32[]{:S(2)}, u32[]{:S(2)}) async-start(f32[16,128,128]{2,1,0:T(8,128)} %gather_fusion), calls=%async_computation.1 | async-start | bytes 2097152 | tf_op jit(solution)/shard_map/all_to_all | solution.py:221
  22.1 0.6 compare_convert_fusion.live_ref
  22.6 1.6 %multiply_reduce_fusion = f32[2048]{0:T(1024)S(1)} fusion(f32[2048,128]{1,0:T(8,128)} %param.6), kind=kLoop, calls=%fused_computation.1 | loop fusion | flops 522240 | bytes 1056768 | tf_op jit(solution)/shard_map/reduce_sum | solution.py:22
  24.2 2.5 %broadcast_multiply_fusion = f32[2048,128]{1,0:T(8,128)} fusion(f32[2048,128]{1,0:T(8,128)} %param.6, f32[2048]{0:T(1024)S(1)} %add_rsqrt_fusion), kind=kLoop, calls=%fused_computation.2 | loop fusion | flops 262144 | bytes 2105344 | tf_op jit(solution)/shard_map/mul | solution.py:22
  26.8 17.5 %all-to-all-done.1.t_ref = f32[16,128,128]{2,1,0:T(8,128)S(1)} async-done(((f32[16,128,128]{2,1,0:T(8,128)}), f32[16,128,128]{2,1,0:T(8,128)S(1)}, u32[]{:S(2)}, u32[]{:S(2)}) %all-to-all-start.1) | async-done | bytes 1048608 | tf_op jit(solution)/shard_map/all_to_all | solution.py:221
  44.3 0.0 copy-start
  44.3 1.4 %copy.15.tt_ref = f32[16,128,128]{2,1,0:T(8,128)} copy(f32[16,128,128]{1,2,0:T(8,128)S(1)} %bitcast.19) | data formatting | bytes 2097152 | tf_op jit(solution)/shard_map/transpose | solution.py:236
  45.7 0.6 broadcast_5_c_ref.2.c_ref
  46.3 23.0 %shard_map.77 = (f32[128,128,128]{2,1,0:T(8,128)}, f32[16,128,1]{2,1,0:T(8,128)}, f32[16,1,128]{2,1,0:T(1,128)}) custom-call(s32[128]{0:T(128)} %src_sm.5, s32[128]{0:T(128)} %slot_sm.5, f32[128]{0:T(128)} %compare_convert_fusion.live_ref, f32[16,128,128]{2,1,0:T(8,128)} %bitcast.21, f32[16,128,128]{2,1,0:T(8,128)} %copy.15.tt_ref, ...), custom_call_target="tpu_custom_call" | custom-call | tf_op jit(solution)/shard_map/pallas_call | solution.py:151
  69.3 1.4 %broadcast_in_dim.45 = f32[16,16,128]{2,1,0:T(8,128)} broadcast(f32[16,128]{1,0:T(8,128)} %bitcast.25), dimensions={1,2} | broadcast | bytes 139264 | tf_op jit(solution)/shard_map/broadcast_in_dim | solution.py:227
  70.7 6.8 %all-to-all-start.2 = ((f32[16,16,128]{2,1,0:T(8,128)}), f32[16,16,128]{2,1,0:T(8,128)S(1)}, u32[]{:S(2)}, u32[]{:S(2)}) async-start(f32[16,16,128]{2,1,0:T(8,128)} %broadcast_in_dim.45), calls=%async_computation.2 | async-start | bytes 262144 | tf_op jit(solution)/shard_map/all_to_all | solution.py:228
  77.5 0.0 copy-done.1
  77.5 7.9 %all-to-all-done.2 = f32[16,16,128]{2,1,0:T(8,128)S(1)} async-done(((f32[16,16,128]{2,1,0:T(8,128)}), f32[16,16,128]{2,1,0:T(8,128)S(1)}, u32[]{:S(2)}, u32[]{:S(2)}) %all-to-all-start.2) | async-done | bytes 131104 | tf_op jit(solution)/shard_map/all_to_all | solution.py:228
  85.4 0.1 select_reduce_fusion.1
  85.5 0.6 maximum_divide_fusion.1
  86.1 12.3 %shard_map.78 = (f32[16,128,1]{2,1,0:T(8,128)}, f32[16,1,128]{2,1,0:T(1,128)}) custom-call(s32[128]{0:T(128)} %src_sm.5, s32[128]{0:T(128)} %slot_sm.5, f32[128,128,128]{2,1,0:T(8,128)} %get-tuple-element.8.k_hbm, f32[16,1,128]{2,1,0:T(1,128)} %bitcast.24), custom_call_target="tpu_custom_call" | custom-call | tf_op jit(solution)/shard_map/pallas_call | solution.py:171
  98.5 0.7 broadcast_in_dim.48
  99.2 10.5 %all_to_all.24 = f32[16,16,128]{2,1,0:T(8,128)S(1)} all-to-all(f32[16,16,128]{2,1,0:T(8,128)S(1)} %broadcast_in_dim.48), channel_id=1, replica_groups=mesh['groups'=2,'rows'=16] {'rows'}, dimensions={0} | all-to-all | bytes 262144 | tf_op jit(solution)/shard_map/all_to_all | solution.py:228
  109.7 0.1 select_reduce_fusion
  109.8 0.6 maximum_divide_fusion
  110.4 0.0 copy-done
  110.4 17.1 %shard_map.79 = (f32[16,128,128]{2,1,0:T(8,128)}, f32[16,128]{1,0:T(8,128)}) custom-call(s32[128]{0:T(128)} %src_sm.5, s32[128]{0:T(128)} %slot_sm.5, f32[128,128,128]{2,1,0:T(8,128)} %get-tuple-element.8.k_hbm, f32[16,128,128]{2,1,0:T(8,128)} %copy-done, f32[16,1,128]{2,1,0:T(1,128)} %bitcast.23, f32[16,128,1]{2,1,0:T(8,128)} %get-tuple-element.11.r_ref), custom_call_target="tpu_custom_call" | custom-call | tf_op jit(solution)/shard_map/pallas_call | solution.py:190
  (5 shorter events, 0.0 us)
Async XLA Ops:
  0.6 76.9 %copy-start.1 = (s32[16,1]{0,1:T(1,128)S(1)}, s32[16,1]{0,1:T(1,128)}, u32[]{:S(2)}) copy-start(s32[16,1]{0,1:T(1,128)} %param.11) | copy-start | bytes 196
  2.0 13.7 %all-to-all-start = ((s32[16,1,16]{2,1,0:T(1,128)}), s32[16,1,16]{2,1,0:T(1,128)S(1)}, u32[]{:S(2)}, u32[]{:S(2)}) async-start(s32[16,1,16]{2,1,0:T(1,128)} %broadcast_in_dim.42), calls=%async_computation | async-start | bytes 16384 | tf_op jit(solution)/shard_map/all_to_all | solution.py:214
  17.8 26.6 %all-to-all-start.1 = ((f32[16,128,128]{2,1,0:T(8,128)}), f32[16,128,128]{2,1,0:T(8,128)S(1)}, u32[]{:S(2)}, u32[]{:S(2)}) async-start(f32[16,128,128]{2,1,0:T(8,128)} %gather_fusion), calls=%async_computation.1 | async-start | bytes 2097152 | tf_op jit(solution)/shard_map/all_to_all | solution.py:221
  44.3 66.1 %copy-start = (f32[16,128,128]{2,1,0:T(8,128)}, f32[16,128,128]{2,1,0:T(8,128)S(1)}, u32[]{:S(2)}) copy-start(f32[16,128,128]{2,1,0:T(8,128)S(1)} %all-to-all-done.1.t_ref) | copy-start | bytes 3145732
  70.7 14.8 %all-to-all-start.2 = ((f32[16,16,128]{2,1,0:T(8,128)}), f32[16,16,128]{2,1,0:T(8,128)S(1)}, u32[]{:S(2)}, u32[]{:S(2)}) async-start(f32[16,16,128]{2,1,0:T(8,128)} %broadcast_in_dim.45), calls=%async_computation.2 | async-start | bytes 262144 | tf_op jit(solution)/shard_map/all_to_all | solution.py:228

commit v7 on v6

--- a/solution.py
+++ b/solution.py
@@ -31,29 +31,32 @@
     return math.gcd(capacity, 16)
 
 
-def _rows_cols(src_sm, slot_sm, tile_at, chunk_done, k_ref, c_ref, r_out, colp_out, rs_scr):
-    capacity = src_sm.shape[0]
+def _rows_cols(src_sm, slot_sm, tile_at, chunk_done, k_ref, c_ref, r_out, colp_out, acc, rb_scr):
+    capacity = src_sm.shape[0]
+    sb = acc.shape[0]
     step = _chunk(capacity)
-    rs_scr[...] = jnp.zeros_like(rs_scr)
+    acc[...] = jnp.zeros_like(acc)
     colp_out[...] = jnp.zeros_like(colp_out)
 
     def rows(t, carry):
         q = src_sm[t]
         o = slot_sm[t]
-        k = tile_at(t, q, o)
-        rs_scr[q] += jnp.sum(k * c_ref[o], axis=1, keepdims=True)
+        acc[q] += tile_at(t, q, o) * c_ref[o]
         return carry
 
     for part in range(capacity // step):
         chunk_done(part, "before")
         lax.fori_loop(part * step, (part + 1) * step, rows, 0, unroll=UNROLL)
         chunk_done(part, "after")
-    r_out[...] = 1.0 / jnp.maximum(rs_scr[...], ROW_MINIMUM)
+    for q in range(sb):
+        r = 1.0 / jnp.maximum(jnp.sum(acc[q], axis=1, keepdims=True), ROW_MINIMUM)
+        r_out[q] = r
+        rb_scr[q] = jnp.broadcast_to(r, (BLOCK, BLOCK))
 
     def cols(t, carry):
         q = src_sm[t]
         o = slot_sm[t]
-        colp_out[o] += jnp.sum(k_ref[t] * r_out[q], axis=0, keepdims=True)
+        colp_out[o] += jnp.sum(k_ref[t] * rb_scr[q], axis=0, keepdims=True)
         return carry
 
     lax.fori_loop(0, capacity, cols, 0, unroll=UNROLL)
@@ -70,7 +73,7 @@
 
 
 def _first_kernel(
-    src_sm, slot_sm, live_ref, s_ref, tt_ref, c_ref, k_hbm, r_out, colp_out, k_scr, rs_scr, sems
+    src_sm, slot_sm, live_ref, s_ref, tt_ref, c_ref, k_hbm, r_out, colp_out, k_scr, acc, rb_scr, sems
 ):
     capacity = src_sm.shape[0]
     copies = _chunk_copies(k_scr, k_hbm, sems, capacity)
@@ -84,12 +87,12 @@
         if when == "after":
             copies[part].start()
 
-    _rows_cols(src_sm, slot_sm, build, chunk_done, k_scr, c_ref, r_out, colp_out, rs_scr)
+    _rows_cols(src_sm, slot_sm, build, chunk_done, k_scr, c_ref, r_out, colp_out, acc, rb_scr)
     for copy in copies:
         copy.wait()
 
 
-def _again_kernel(src_sm, slot_sm, k_hbm, c_ref, r_out, colp_out, k_scr, rs_scr, sems):
+def _again_kernel(src_sm, slot_sm, k_hbm, c_ref, r_out, colp_out, k_scr, acc, rb_scr, sems):
     capacity = src_sm.shape[0]
     copies = _chunk_copies(k_hbm, k_scr, sems, capacity)
     for copy in copies:
@@ -100,7 +103,7 @@
             copies[part].wait()
 
     _rows_cols(
-        src_sm, slot_sm, lambda t, q, o: k_scr[t], chunk_done, k_scr, c_ref, r_out, colp_out, rs_scr
+        src_sm, slot_sm, lambda t, q, o: k_scr[t], chunk_done, k_scr, c_ref, r_out, colp_out, acc, rb_scr
     )
 
 
@@ -118,7 +121,7 @@
         o = slot_sm[t]
         kc = k_scr[t] * c_ref[o]
         al_out[q] += jnp.dot(kc, t_ref[o], precision=HIGHEST, preferred_element_type=jnp.float32)
-        ms_scr[q] += jnp.sum(kc, axis=1, keepdims=True)
+        ms_scr[q] += kc
         return carry
 
     for part in range(capacity // step):
@@ -127,7 +130,7 @@
     r = r_ref[...]
     al_out[...] = al_out[...] * r * math.sqrt(E)
     for q in range(ms_out.shape[0]):
-        mass = jnp.broadcast_to(ms_scr[q] * r_ref[q], (BLOCK, BLOCK))
+        mass = jnp.broadcast_to(jnp.sum(ms_scr[q], axis=1, keepdims=True) * r_ref[q], (BLOCK, BLOCK))
         ms_out[q : q + 1, :] = jnp.transpose(mass)[0:1, :]
 
 
@@ -159,7 +162,8 @@
         out_specs=(_ANY,) + _vmem_out(2),
         scratch_shapes=[
             pltpu.VMEM((capacity, BLOCK, BLOCK), jnp.float32),
-            pltpu.VMEM((sb, BLOCK, 1), jnp.float32),
+            pltpu.VMEM((sb, BLOCK, BLOCK), jnp.float32),
+            pltpu.VMEM((sb, BLOCK, BLOCK), jnp.float32),
             pltpu.SemaphoreType.DMA((capacity // _chunk(capacity),)),
         ],
     )(tile_source, tile_slot, live, source_unit, fetched_t, col)
@@ -178,7 +182,8 @@
         out_specs=_vmem_out(2),
         scratch_shapes=[
             pltpu.VMEM((capacity, BLOCK, BLOCK), jnp.float32),
-            pltpu.VMEM((sb, BLOCK, 1), jnp.float32),
+            pltpu.VMEM((sb, BLOCK, BLOCK), jnp.float32),
+            pltpu.VMEM((sb, BLOCK, BLOCK), jnp.float32),
             pltpu.SemaphoreType.DMA((capacity // _chunk(capacity),)),
         ],
     )(tile_source, tile_slot, kernel, col)
@@ -197,7 +202,7 @@
         out_specs=_vmem_out(2),
         scratch_shapes=[
             pltpu.VMEM((capacity, BLOCK, BLOCK), jnp.float32),
-            pltpu.VMEM((sb, BLOCK, 1), jnp.float32),
+            pltpu.VMEM((sb, BLOCK, BLOCK), jnp.float32),
             pltpu.SemaphoreType.DMA((capacity // _chunk(capacity),)),
         ],
     )(tile_source, tile_slot, kernel, fetched, col, row)

time: 128 us -> 118 us (0.922)
  Pallas kernels: 52.4 us -> 42 us
    pallas_call x1, Pallas kernels: 23 us -> 17.2 us  [first_sweep(): pl.pallas_call(_first_kernel, out_shape=(jax.ShapeDtypeStruct((capacity,...]
    pallas_call x1, Pallas kernels: 12.3 us -> 7.02 us  [again_sweep(): pl.pallas_call(_again_kernel, out_shape=(jax.ShapeDtypeStruct((sb, BLOCK,...]
  transfers between devices with their start and end apart: 3 -> 3, of which waited for: 3 -> 3; matrix products, arithmetic and copies ran while one was open for 5% -> 6% of each run, Pallas kernels for 0% -> 0%
where the time goes in v7:
time: 118 us; the launch traced here: 117 us
  Pallas kernels  42 us (36%)
  waiting for transfers between devices  29.6 us (25%)
  starting transfers between devices  17.9 us (15%)
  blocking collectives  10.5 us (9%)
  other arithmetic  8.29 us (7%)
  local copies, waits for them, and re-layouts  7.44 us (6%)
  between operations  1.41 us (1%)
    pallas_call x1, Pallas kernels, final(): pl.pallas_call(_final_kernel, out_shape=(jax.ShapeDtypeStruct((sb, BLOCK,...  17.7 us
    all_to_all x1, waiting for transfers between devices, on_device(): lax.all_to_all(outgoing, 'rows', split_axis=0, concat_axis=0, tiled=True)  17.5 us
    pallas_call x1, Pallas kernels, first_sweep(): pl.pallas_call(_first_kernel, out_shape=(jax.ShapeDtypeStruct((capacity,...  17.2 us
    all_to_all x1, blocking collectives, column_scale_of(): lax.all_to_all(spread, 'rows', split_axis=0, concat_axis=0, tiled=True)  10.5 us
    all_to_all x1, waiting for transfers between devices, column_scale_of(): lax.all_to_all(spread, 'rows', split_axis=0, concat_axis=0, tiled=True)  7.91 us
    all_to_all x1, starting transfers between devices, on_device(): lax.all_to_all(jnp.broadcast_to(wanted_row, (rows_n, slots)), 'rows', spl...  7.39 us
    pallas_call x1, Pallas kernels, again_sweep(): pl.pallas_call(_again_kernel, out_shape=(jax.ShapeDtypeStruct((sb, BLOCK,...  7.02 us
    all_to_all x1, starting transfers between devices, column_scale_of(): lax.all_to_all(spread, 'rows', split_axis=0, concat_axis=0, tiled=True)  6.82 us
  transfers between devices with their start and end apart: 3, of which 3 were waited for; matrix products, arithmetic and copies ran while one was open for 6% of the time, Pallas kernels for 0%

profile of v7, /device:TPU:0, one launch (start us, length us, event | category | flops | bytes accessed | tf_op | source)
XLA Modules:
  0.0 117.1 jit_solution(7650484113306351096)
XLA Ops:
  0.6 0.0 copy-start.1
  0.6 1.3 %broadcast_in_dim.42 = s32[16,1,16]{2,1,0:T(1,128)} broadcast(s32[16]{0:T(128)} %bitcast.27), dimensions={2} | broadcast | bytes 1088 | tf_op jit(solution)/shard_map/broadcast_in_dim | solution.py:220
  2.0 7.4 %all-to-all-start = ((s32[16,1,16]{2,1,0:T(1,128)}), s32[16,1,16]{2,1,0:T(1,128)S(1)}, u32[]{:S(2)}, u32[]{:S(2)}) async-start(s32[16,1,16]{2,1,0:T(1,128)} %broadcast_in_dim.42), calls=%async_computation | async-start | bytes 16384 | tf_op jit(solution)/shard_map/all_to_all | solution.py:219
  9.4 1.1 multiply_reduce_fusion.1
  10.5 1.1 broadcast_multiply_fusion.1
  11.6 4.1 %all-to-all-done = s32[16,1,16]{2,1,0:T(1,128)S(1)} async-done(((s32[16,1,16]{2,1,0:T(1,128)}), s32[16,1,16]{2,1,0:T(1,128)S(1)}, u32[]{:S(2)}, u32[]{:S(2)}) %all-to-all-start) | async-done | bytes 1056 | tf_op jit(solution)/shard_map/all_to_all | solution.py:219
  15.7 0.4 dynamic-slice_reduce_fusion
  16.2 1.6 %gather_fusion = f32[16,128,128]{2,1,0:T(8,128)} fusion(f32[4,128,128]{2,1,0:T(8,128)S(1)} %bitcast.20, s32[1024]{0:T(1024)S(1)} %pad_clamp_fusion), kind=kCustom, calls=%fused_computation | custom fusion | bytes 2097216 | tf_op jit(solution)/shard_map/gather | solution.py:225
  17.8 3.7 %all-to-all-start.1 = ((f32[16,128,128]{2,1,0:T(8,128)}), f32[16,128,128]{2,1,0:T(8,128)S(1)}, u32[]{:S(2)}, u32[]{:S(2)}) async-start(f32[16,128,128]{2,1,0:T(8,128)} %gather_fusion), calls=%async_computation.1 | async-start | bytes 2097152 | tf_op jit(solution)/shard_map/all_to_all | solution.py:226
  22.1 0.6 compare_convert_fusion.live_ref
  22.6 1.6 %multiply_reduce_fusion = f32[2048]{0:T(1024)S(1)} fusion(f32[2048,128]{1,0:T(8,128)} %param.6), kind=kLoop, calls=%fused_computation.1 | loop fusion | flops 522240 | bytes 1056768 | tf_op jit(solution)/shard_map/reduce_sum | solution.py:22
  24.2 2.5 %broadcast_multiply_fusion = f32[2048,128]{1,0:T(8,128)} fusion(f32[2048,128]{1,0:T(8,128)} %param.6, f32[2048]{0:T(1024)S(1)} %add_rsqrt_fusion), kind=kLoop, calls=%fused_computation.2 | loop fusion | flops 262144 | bytes 2105344 | tf_op jit(solution)/shard_map/mul | solution.py:22
  26.8 17.5 %all-to-all-done.1.t_ref = f32[16,128,128]{2,1,0:T(8,128)S(1)} async-done(((f32[16,128,128]{2,1,0:T(8,128)}), f32[16,128,128]{2,1,0:T(8,128)S(1)}, u32[]{:S(2)}, u32[]{:S(2)}) %all-to-all-start.1) | async-done | bytes 1048608 | tf_op jit(solution)/shard_map/all_to_all | solution.py:226
  44.3 0.0 copy-start
  44.3 1.4 %copy.15.tt_ref = f32[16,128,128]{2,1,0:T(8,128)} copy(f32[16,128,128]{1,2,0:T(8,128)S(1)} %bitcast.19) | data formatting | bytes 2097152 | tf_op jit(solution)/shard_map/transpose | solution.py:241
  45.7 0.6 broadcast_5_c_ref.2.c_ref
  46.3 17.2 %shard_map.77 = (f32[128,128,128]{2,1,0:T(8,128)}, f32[16,128,1]{2,1,0:T(8,128)}, f32[16,1,128]{2,1,0:T(1,128)}) custom-call(s32[128]{0:T(128)} %src_sm.5, s32[128]{0:T(128)} %slot_sm.5, f32[128]{0:T(128)} %compare_convert_fusion.live_ref, f32[16,128,128]{2,1,0:T(8,128)} %bitcast.21, f32[16,128,128]{2,1,0:T(8,128)} %copy.15.tt_ref, ...), custom_call_target="tpu_custom_call" | custom-call | tf_op jit(solution)/shard_map/pallas_call | solution.py:154
  63.5 1.4 %broadcast_in_dim.45 = f32[16,16,128]{2,1,0:T(8,128)} broadcast(f32[16,128]{1,0:T(8,128)} %bitcast.25), dimensions={1,2} | broadcast | bytes 139264 | tf_op jit(solution)/shard_map/broadcast_in_dim | solution.py:232
  64.9 6.8 %all-to-all-start.2 = ((f32[16,16,128]{2,1,0:T(8,128)}), f32[16,16,128]{2,1,0:T(8,128)S(1)}, u32[]{:S(2)}, u32[]{:S(2)}) async-start(f32[16,16,128]{2,1,0:T(8,128)} %broadcast_in_dim.45), calls=%async_computation.2 | async-start | bytes 262144 | tf_op jit(solution)/shard_map/all_to_all | solution.py:233
  71.7 0.0 copy-done.1
  71.8 7.9 %all-to-all-done.2 = f32[16,16,128]{2,1,0:T(8,128)S(1)} async-done(((f32[16,16,128]{2,1,0:T(8,128)}), f32[16,16,128]{2,1,0:T(8,128)S(1)}, u32[]{:S(2)}, u32[]{:S(2)}) %all-to-all-start.2) | async-done | bytes 131104 | tf_op jit(solution)/shard_map/all_to_all | solution.py:233
  79.7 0.1 select_reduce_fusion.1
  79.8 0.6 maximum_divide_fusion.1
  80.4 7.0 %shard_map.78 = (f32[16,128,1]{2,1,0:T(8,128)}, f32[16,1,128]{2,1,0:T(1,128)}) custom-call(s32[128]{0:T(128)} %src_sm.5, s32[128]{0:T(128)} %slot_sm.5, f32[128,128,128]{2,1,0:T(8,128)} %get-tuple-element.8.k_hbm, f32[16,1,128]{2,1,0:T(1,128)} %bitcast.24), custom_call_target="tpu_custom_call" | custom-call | tf_op jit(solution)/shard_map/pallas_call | solution.py:175
  87.4 0.7 broadcast_in_dim.48
  88.1 10.5 %all_to_all.24 = f32[16,16,128]{2,1,0:T(8,128)S(1)} all-to-all(f32[16,16,128]{2,1,0:T(8,128)S(1)} %broadcast_in_dim.48), channel_id=1, replica_groups=mesh['groups'=2,'rows'=16] {'rows'}, dimensions={0} | all-to-all | bytes 262144 | tf_op jit(solution)/shard_map/all_to_all | solution.py:233
  98.6 0.1 select_reduce_fusion
  98.8 0.6 maximum_divide_fusion
  99.3 0.0 copy-done
  99.4 17.7 %shard_map.79 = (f32[16,128,128]{2,1,0:T(8,128)}, f32[16,128]{1,0:T(8,128)}) custom-call(s32[128]{0:T(128)} %src_sm.5, s32[128]{0:T(128)} %slot_sm.5, f32[128,128,128]{2,1,0:T(8,128)} %get-tuple-element.8.k_hbm, f32[16,128,128]{2,1,0:T(8,128)} %copy-done, f32[16,1,128]{2,1,0:T(1,128)} %bitcast.23, f32[16,128,1]{2,1,0:T(8,128)} %get-tuple-element.11.r_ref), custom_call_target="tpu_custom_call" | custom-call | tf_op jit(solution)/shard_map/pallas_call | solution.py:195
  (5 shorter events, 0.0 us)
Async XLA Ops:
  0.6 71.1 %copy-start.1 = (s32[16,1]{0,1:T(1,128)S(1)}, s32[16,1]{0,1:T(1,128)}, u32[]{:S(2)}) copy-start(s32[16,1]{0,1:T(1,128)} %param.11) | copy-start | bytes 196
  2.0 13.7 %all-to-all-start = ((s32[16,1,16]{2,1,0:T(1,128)}), s32[16,1,16]{2,1,0:T(1,128)S(1)}, u32[]{:S(2)}, u32[]{:S(2)}) async-start(s32[16,1,16]{2,1,0:T(1,128)} %broadcast_in_dim.42), calls=%async_computation | async-start | bytes 16384 | tf_op jit(solution)/shard_map/all_to_all | solution.py:219
  17.8 26.6 %all-to-all-start.1 = ((f32[16,128,128]{2,1,0:T(8,128)}), f32[16,128,128]{2,1,0:T(8,128)S(1)}, u32[]{:S(2)}, u32[]{:S(2)}) async-start(f32[16,128,128]{2,1,0:T(8,128)} %gather_fusion), calls=%async_computation.1 | async-start | bytes 2097152 | tf_op jit(solution)/shard_map/all_to_all | solution.py:226
  44.3 55.0 %copy-start = (f32[16,128,128]{2,1,0:T(8,128)}, f32[16,128,128]{2,1,0:T(8,128)S(1)}, u32[]{:S(2)}) copy-start(f32[16,128,128]{2,1,0:T(8,128)S(1)} %all-to-all-done.1.t_ref) | copy-start | bytes 3145732
  64.9 14.8 %all-to-all-start.2 = ((f32[16,16,128]{2,1,0:T(8,128)}), f32[16,16,128]{2,1,0:T(8,128)S(1)}, u32[]{:S(2)}, u32[]{:S(2)}) async-start(f32[16,16,128]{2,1,0:T(8,128)} %broadcast_in_dim.45), calls=%async_computation.2 | async-start | bytes 262144 | tf_op jit(solution)/shard_map/all_to_all | solution.py:233

commit v8 on v7

--- a/solution.py
+++ b/solution.py
@@ -17,6 +17,7 @@
 ROW_MINIMUM = 1.0
 COLUMN_FLOOR = 0.01
 HIGHEST = lax.Precision.HIGHEST
+HIGH = lax.Precision.HIGH
 
 def unit_rows(values):
     return values * lax.rsqrt(jnp.sum(values * values, axis=-1, keepdims=True) + EPSILON)
@@ -120,7 +121,7 @@
         q = src_sm[t]
         o = slot_sm[t]
         kc = k_scr[t] * c_ref[o]
-        al_out[q] += jnp.dot(kc, t_ref[o], precision=HIGHEST, preferred_element_type=jnp.float32)
+        al_out[q] += jnp.dot(kc, t_ref[o], precision=HIGH, preferred_element_type=jnp.float32)
         ms_scr[q] += kc
         return carry
 

time: 118 us -> 113 us (0.958)
  Pallas kernels: 42 us -> 37.5 us
    pallas_call x1, Pallas kernels: 17.7 us -> 13.3 us  [final(): pl.pallas_call(_final_kernel, out_shape=(jax.ShapeDtypeStruct((sb, BLOCK,...]
where the time goes in v8:
time: 113 us
  Pallas kernels  37.5 us (33%)
  waiting for transfers between devices  29.6 us (26%)
  starting transfers between devices  17.9 us (16%)
  blocking collectives  10.5 us (9%)
  other arithmetic  8.29 us (7%)
  local copies, waits for them, and re-layouts  7.44 us (7%)
  between operations  1.41 us (1%)
    all_to_all x1, waiting for transfers between devices, on_device(): lax.all_to_all(outgoing, 'rows', split_axis=0, concat_axis=0, tiled=True)  17.5 us
    pallas_call x1, Pallas kernels, first_sweep(): pl.pallas_call(_first_kernel, out_shape=(jax.ShapeDtypeStruct((capacity,...  17.2 us
    pallas_call x1, Pallas kernels, final(): pl.pallas_call(_final_kernel, out_shape=(jax.ShapeDtypeStruct((sb, BLOCK,...  13.3 us
    all_to_all x1, blocking collectives, column_scale_of(): lax.all_to_all(spread, 'rows', split_axis=0, concat_axis=0, tiled=True)  10.5 us
    all_to_all x1, waiting for transfers between devices, column_scale_of(): lax.all_to_all(spread, 'rows', split_axis=0, concat_axis=0, tiled=True)  7.91 us
    all_to_all x1, starting transfers between devices, on_device(): lax.all_to_all(jnp.broadcast_to(wanted_row, (rows_n, slots)), 'rows', spl...  7.39 us
    pallas_call x1, Pallas kernels, again_sweep(): pl.pallas_call(_again_kernel, out_shape=(jax.ShapeDtypeStruct((sb, BLOCK,...  7.02 us
    all_to_all x1, starting transfers between devices, column_scale_of(): lax.all_to_all(spread, 'rows', split_axis=0, concat_axis=0, tiled=True)  6.82 us
  transfers between devices with their start and end apart: 3, of which 3 were waited for; matrix products, arithmetic and copies ran while one was open for 6% of the time, Pallas kernels for 0%

profile of v8, /device:TPU:0, one launch (start us, length us, event | category | flops | bytes accessed | tf_op | source)
XLA Modules:
  0.0 112.6 jit_solution(842951770309374261)
XLA Ops:
  0.6 0.0 copy-start.1
  0.6 1.3 %broadcast_in_dim.42 = s32[16,1,16]{2,1,0:T(1,128)} broadcast(s32[16]{0:T(128)} %bitcast.27), dimensions={2} | broadcast | bytes 1088 | tf_op jit(solution)/shard_map/broadcast_in_dim | solution.py:221
  2.0 7.4 %all-to-all-start = ((s32[16,1,16]{2,1,0:T(1,128)}), s32[16,1,16]{2,1,0:T(1,128)S(1)}, u32[]{:S(2)}, u32[]{:S(2)}) async-start(s32[16,1,16]{2,1,0:T(1,128)} %broadcast_in_dim.42), calls=%async_computation | async-start | bytes 16384 | tf_op jit(solution)/shard_map/all_to_all | solution.py:220
  9.4 1.1 multiply_reduce_fusion.1
  10.5 1.1 broadcast_multiply_fusion.1
  11.6 4.1 %all-to-all-done = s32[16,1,16]{2,1,0:T(1,128)S(1)} async-done(((s32[16,1,16]{2,1,0:T(1,128)}), s32[16,1,16]{2,1,0:T(1,128)S(1)}, u32[]{:S(2)}, u32[]{:S(2)}) %all-to-all-start) | async-done | bytes 1056 | tf_op jit(solution)/shard_map/all_to_all | solution.py:220
  15.7 0.4 dynamic-slice_reduce_fusion
  16.2 1.6 %gather_fusion = f32[16,128,128]{2,1,0:T(8,128)} fusion(f32[4,128,128]{2,1,0:T(8,128)S(1)} %bitcast.20, s32[1024]{0:T(1024)S(1)} %pad_clamp_fusion), kind=kCustom, calls=%fused_computation | custom fusion | bytes 2097216 | tf_op jit(solution)/shard_map/gather | solution.py:226
  17.8 3.7 %all-to-all-start.1 = ((f32[16,128,128]{2,1,0:T(8,128)}), f32[16,128,128]{2,1,0:T(8,128)S(1)}, u32[]{:S(2)}, u32[]{:S(2)}) async-start(f32[16,128,128]{2,1,0:T(8,128)} %gather_fusion), calls=%async_computation.1 | async-start | bytes 2097152 | tf_op jit(solution)/shard_map/all_to_all | solution.py:227
  22.1 0.6 compare_convert_fusion.live_ref
  22.6 1.6 %multiply_reduce_fusion = f32[2048]{0:T(1024)S(1)} fusion(f32[2048,128]{1,0:T(8,128)} %param.6), kind=kLoop, calls=%fused_computation.1 | loop fusion | flops 522240 | bytes 1056768 | tf_op jit(solution)/shard_map/reduce_sum | solution.py:23
  24.2 2.5 %broadcast_multiply_fusion = f32[2048,128]{1,0:T(8,128)} fusion(f32[2048,128]{1,0:T(8,128)} %param.6, f32[2048]{0:T(1024)S(1)} %add_rsqrt_fusion), kind=kLoop, calls=%fused_computation.2 | loop fusion | flops 262144 | bytes 2105344 | tf_op jit(solution)/shard_map/mul | solution.py:23
  26.8 17.5 %all-to-all-done.1.t_ref = f32[16,128,128]{2,1,0:T(8,128)S(1)} async-done(((f32[16,128,128]{2,1,0:T(8,128)}), f32[16,128,128]{2,1,0:T(8,128)S(1)}, u32[]{:S(2)}, u32[]{:S(2)}) %all-to-all-start.1) | async-done | bytes 1048608 | tf_op jit(solution)/shard_map/all_to_all | solution.py:227
  44.3 0.0 copy-start
  44.3 1.4 %copy.15.tt_ref = f32[16,128,128]{2,1,0:T(8,128)} copy(f32[16,128,128]{1,2,0:T(8,128)S(1)} %bitcast.19) | data formatting | bytes 2097152 | tf_op jit(solution)/shard_map/transpose | solution.py:242
  45.7 0.6 broadcast_5_c_ref.2.c_ref
  46.3 17.2 %shard_map.77 = (f32[128,128,128]{2,1,0:T(8,128)}, f32[16,128,1]{2,1,0:T(8,128)}, f32[16,1,128]{2,1,0:T(1,128)}) custom-call(s32[128]{0:T(128)} %src_sm.5, s32[128]{0:T(128)} %slot_sm.5, f32[128]{0:T(128)} %compare_convert_fusion.live_ref, f32[16,128,128]{2,1,0:T(8,128)} %bitcast.21, f32[16,128,128]{2,1,0:T(8,128)} %copy.15.tt_ref, ...), custom_call_target="tpu_custom_call" | custom-call | tf_op jit(solution)/shard_map/pallas_call | solution.py:155
  63.5 1.4 %broadcast_in_dim.45 = f32[16,16,128]{2,1,0:T(8,128)} broadcast(f32[16,128]{1,0:T(8,128)} %bitcast.25), dimensions={1,2} | broadcast | bytes 139264 | tf_op jit(solution)/shard_map/broadcast_in_dim | solution.py:233
  64.9 6.8 %all-to-all-start.2 = ((f32[16,16,128]{2,1,0:T(8,128)}), f32[16,16,128]{2,1,0:T(8,128)S(1)}, u32[]{:S(2)}, u32[]{:S(2)}) async-start(f32[16,16,128]{2,1,0:T(8,128)} %broadcast_in_dim.45), calls=%async_computation.2 | async-start | bytes 262144 | tf_op jit(solution)/shard_map/all_to_all | solution.py:234
  71.7 0.0 copy-done.1
  71.8 7.9 %all-to-all-done.2 = f32[16,16,128]{2,1,0:T(8,128)S(1)} async-done(((f32[16,16,128]{2,1,0:T(8,128)}), f32[16,16,128]{2,1,0:T(8,128)S(1)}, u32[]{:S(2)}, u32[]{:S(2)}) %all-to-all-start.2) | async-done | bytes 131104 | tf_op jit(solution)/shard_map/all_to_all | solution.py:234
  79.7 0.1 select_reduce_fusion.1
  79.8 0.6 maximum_divide_fusion.1
  80.4 7.0 %shard_map.78 = (f32[16,128,1]{2,1,0:T(8,128)}, f32[16,1,128]{2,1,0:T(1,128)}) custom-call(s32[128]{0:T(128)} %src_sm.5, s32[128]{0:T(128)} %slot_sm.5, f32[128,128,128]{2,1,0:T(8,128)} %get-tuple-element.8.k_hbm, f32[16,1,128]{2,1,0:T(1,128)} %bitcast.24), custom_call_target="tpu_custom_call" | custom-call | tf_op jit(solution)/shard_map/pallas_call | solution.py:176
  87.4 0.7 broadcast_in_dim.48
  88.1 10.5 %all_to_all.24 = f32[16,16,128]{2,1,0:T(8,128)S(1)} all-to-all(f32[16,16,128]{2,1,0:T(8,128)S(1)} %broadcast_in_dim.48), channel_id=1, replica_groups=mesh['groups'=2,'rows'=16] {'rows'}, dimensions={0} | all-to-all | bytes 262144 | tf_op jit(solution)/shard_map/all_to_all | solution.py:234
  98.6 0.1 select_reduce_fusion
  98.7 0.6 maximum_divide_fusion
  99.3 0.0 copy-done
  99.3 13.3 %shard_map.79 = (f32[16,128,128]{2,1,0:T(8,128)}, f32[16,128]{1,0:T(8,128)}) custom-call(s32[128]{0:T(128)} %src_sm.5, s32[128]{0:T(128)} %slot_sm.5, f32[128,128,128]{2,1,0:T(8,128)} %get-tuple-element.8.k_hbm, f32[16,128,128]{2,1,0:T(8,128)} %copy-done, f32[16,1,128]{2,1,0:T(1,128)} %bitcast.23, f32[16,128,1]{2,1,0:T(8,128)} %get-tuple-element.11.r_ref), custom_call_target="tpu_custom_call" | custom-call | tf_op jit(solution)/shard_map/pallas_call | solution.py:196
  (5 shorter events, 0.0 us)
Async XLA Ops:
  0.6 71.1 %copy-start.1 = (s32[16,1]{0,1:T(1,128)S(1)}, s32[16,1]{0,1:T(1,128)}, u32[]{:S(2)}) copy-start(s32[16,1]{0,1:T(1,128)} %param.11) | copy-start | bytes 196
  2.0 13.7 %all-to-all-start = ((s32[16,1,16]{2,1,0:T(1,128)}), s32[16,1,16]{2,1,0:T(1,128)S(1)}, u32[]{:S(2)}, u32[]{:S(2)}) async-start(s32[16,1,16]{2,1,0:T(1,128)} %broadcast_in_dim.42), calls=%async_computation | async-start | bytes 16384 | tf_op jit(solution)/shard_map/all_to_all | solution.py:220
  17.8 26.6 %all-to-all-start.1 = ((f32[16,128,128]{2,1,0:T(8,128)}), f32[16,128,128]{2,1,0:T(8,128)S(1)}, u32[]{:S(2)}, u32[]{:S(2)}) async-start(f32[16,128,128]{2,1,0:T(8,128)} %gather_fusion), calls=%async_computation.1 | async-start | bytes 2097152 | tf_op jit(solution)/shard_map/all_to_all | solution.py:227
  44.3 55.0 %copy-start = (f32[16,128,128]{2,1,0:T(8,128)}, f32[16,128,128]{2,1,0:T(8,128)S(1)}, u32[]{:S(2)}) copy-start(f32[16,128,128]{2,1,0:T(8,128)S(1)} %all-to-all-done.1.t_ref) | copy-start | bytes 3145732
  64.9 14.8 %all-to-all-start.2 = ((f32[16,16,128]{2,1,0:T(8,128)}), f32[16,16,128]{2,1,0:T(8,128)S(1)}, u32[]{:S(2)}, u32[]{:S(2)}) async-start(f32[16,16,128]{2,1,0:T(8,128)} %broadcast_in_dim.45), calls=%async_computation.2 | async-start | bytes 262144 | tf_op jit(solution)/shard_map/all_to_all | solution.py:234

commit v9 on v8

--- a/solution.py
+++ b/solution.py
@@ -239,7 +239,7 @@
     live = (jnp.arange(tile_source.shape[0]) < tile_count[0]).astype(jnp.float32)
     col = jnp.ones((slots, 1, BLOCK), jnp.float32)
     sb = source_unit.shape[0]
-    fetched_t = jnp.swapaxes(fetched, 1, 2)
+    fetched_t, same_block = lax.optimization_barrier((jnp.swapaxes(fetched, 1, 2), same_block))
     kernel, row, colp = first_sweep(tile_source, tile_slot, live, source_unit, fetched_t, col)
     for iteration in range(1, ITERS):
         col = column_scale_of(colp)

time: 113 us -> 112 us (level)
  blocking collectives: 10.5 us -> 25.1 us
  waiting for transfers between devices: 29.6 us -> 21 us
  starting transfers between devices: 17.9 us -> 11 us
    all_to_all x1 -> x2, blocking collectives: 10.5 us -> 25.1 us  [column_scale_of(): lax.all_to_all(spread, 'rows', split_axis=0, concat_axis=0, tiled=True)]
    all_to_all x1 -> x0, waiting for transfers between devices: 7.91 us -> none  [column_scale_of(): lax.all_to_all(spread, 'rows', split_axis=0, concat_axis=0, tiled=True)]
    all_to_all x1 -> x0, starting transfers between devices: 6.82 us -> none  [column_scale_of(): lax.all_to_all(spread, 'rows', split_axis=0, concat_axis=0, tiled=True)]
    transpose x1 -> x0, local copies, waits for them, and re-layouts: 1.39 us -> none  [on_device(): fetched_t = jnp.swapaxes(fetched, 1, 2)]
    optimization_barrier x0 -> x1, local copies, waits for them, and re-layouts: none -> 1.39 us  [on_device(): lax.optimization_barrier((jnp.swapaxes(fetched, 1, 2), same_block))]
  transfers between devices with their start and end apart: 3 -> 2, of which waited for: 3 -> 2; matrix products, arithmetic and copies ran while one was open for 6% -> 7% of each run, Pallas kernels for 0% -> 0%
where the time goes in v9:
time: 112 us
  Pallas kernels  37.6 us (34%)
  blocking collectives  25.1 us (22%)
  waiting for transfers between devices  21 us (19%)
  starting transfers between devices  11 us (10%)
  other arithmetic  8.94 us (8%)
  local copies, waits for them, and re-layouts  6.72 us (6%)
  between operations  1.38 us (1%)
    all_to_all x2, blocking collectives, column_scale_of(): lax.all_to_all(spread, 'rows', split_axis=0, concat_axis=0, tiled=True)  25.1 us
    pallas_call x1, Pallas kernels, first_sweep(): pl.pallas_call(_first_kernel, out_shape=(jax.ShapeDtypeStruct((capacity,...  17.2 us
    all_to_all x1, waiting for transfers between devices, on_device(): lax.all_to_all(outgoing, 'rows', split_axis=0, concat_axis=0, tiled=True)  16.9 us
    pallas_call x1, Pallas kernels, final(): pl.pallas_call(_final_kernel, out_shape=(jax.ShapeDtypeStruct((sb, BLOCK,...  13.3 us
    all_to_all x1, starting transfers between devices, on_device(): lax.all_to_all(jnp.broadcast_to(wanted_row, (rows_n, slots)), 'rows', spl...  7.39 us
    pallas_call x1, Pallas kernels, again_sweep(): pl.pallas_call(_again_kernel, out_shape=(jax.ShapeDtypeStruct((sb, BLOCK,...  7.02 us
    all_to_all x1, waiting for transfers between devices, on_device(): lax.all_to_all(jnp.broadcast_to(wanted_row, (rows_n, slots)), 'rows', spl...  4.13 us
    all_to_all x1, starting transfers between devices, on_device(): lax.all_to_all(outgoing, 'rows', split_axis=0, concat_axis=0, tiled=True)  3.65 us
  transfers between devices with their start and end apart: 2, of which 2 were waited for; matrix products, arithmetic and copies ran while one was open for 7% of the time, Pallas kernels for 0%

profile of v9, /device:TPU:0, one launch (start us, length us, event | category | flops | bytes accessed | tf_op | source)
XLA Modules:
  0.0 111.7 jit_solution(3005563712236945693)
XLA Ops:
  0.6 1.3 %broadcast_in_dim.44 = s32[16,1,16]{2,1,0:T(1,128)} broadcast(s32[16]{0:T(128)} %bitcast.30), dimensions={2} | broadcast | bytes 1088 | tf_op jit(solution)/shard_map/broadcast_in_dim | solution.py:221
  1.9 7.4 %all-to-all-start = ((s32[16,1,16]{2,1,0:T(1,128)}), s32[16,1,16]{2,1,0:T(1,128)S(1)}, u32[]{:S(2)}, u32[]{:S(2)}) async-start(s32[16,1,16]{2,1,0:T(1,128)} %broadcast_in_dim.44), calls=%async_computation | async-start | bytes 16384 | tf_op jit(solution)/shard_map/all_to_all | solution.py:220
  9.3 1.1 multiply_reduce_fusion.1
  10.4 1.1 broadcast_multiply_fusion.1
  11.5 4.1 %all-to-all-done = s32[16,1,16]{2,1,0:T(1,128)S(1)} async-done(((s32[16,1,16]{2,1,0:T(1,128)}), s32[16,1,16]{2,1,0:T(1,128)S(1)}, u32[]{:S(2)}, u32[]{:S(2)}) %all-to-all-start) | async-done | bytes 1056 | tf_op jit(solution)/shard_map/all_to_all | solution.py:220
  15.6 0.4 dynamic-slice_reduce_fusion
  16.1 1.6 %gather_fusion = f32[16,128,128]{2,1,0:T(8,128)} fusion(f32[4,128,128]{2,1,0:T(8,128)S(1)} %bitcast.21, s32[1024]{0:T(1024)S(1)} %pad_clamp_fusion), kind=kCustom, calls=%fused_computation | custom fusion | bytes 2097216 | tf_op jit(solution)/shard_map/gather | solution.py:226
  17.7 3.7 %all-to-all-start.1 = ((f32[16,128,128]{2,1,0:T(8,128)}), f32[16,128,128]{2,1,0:T(8,128)S(1)}, u32[]{:S(2)}, u32[]{:S(2)}) async-start(f32[16,128,128]{2,1,0:T(8,128)} %gather_fusion), calls=%async_computation.1 | async-start | bytes 2097152 | tf_op jit(solution)/shard_map/all_to_all | solution.py:227
  22.0 0.6 compare_convert_fusion.live_ref
  22.6 1.6 %multiply_reduce_fusion = f32[2048]{0:T(1024)S(1)} fusion(f32[2048,128]{1,0:T(8,128)} %param.6), kind=kLoop, calls=%fused_computation.1 | loop fusion | flops 522240 | bytes 1056768 | tf_op jit(solution)/shard_map/reduce_sum | solution.py:23
  24.2 2.5 %broadcast_multiply_fusion = f32[2048,128]{1,0:T(8,128)} fusion(f32[2048,128]{1,0:T(8,128)} %param.6, f32[2048]{0:T(1024)S(1)} %add_rsqrt_fusion), kind=kLoop, calls=%fused_computation.2 | loop fusion | flops 262144 | bytes 2105344 | tf_op jit(solution)/shard_map/mul | solution.py:23
  26.7 0.7 broadcast_compare_fusion
  27.4 16.9 %all-to-all-done.1.t_ref = f32[16,128,128]{2,1,0:T(8,128)S(1)} async-done(((f32[16,128,128]{2,1,0:T(8,128)}), f32[16,128,128]{2,1,0:T(8,128)S(1)}, u32[]{:S(2)}, u32[]{:S(2)}) %all-to-all-start.1) | async-done | bytes 1048608 | tf_op jit(solution)/shard_map/all_to_all | solution.py:227
  44.2 0.0 copy-start
  44.2 1.4 %copy.15.tt_ref = f32[16,128,128]{2,1,0:T(8,128)} copy(f32[16,128,128]{1,2,0:T(8,128)S(1)} %bitcast.20) | data formatting | bytes 2097152 | tf_op jit(solution)/shard_map/optimization_barrier | solution.py:242
  45.6 0.6 broadcast_5_c_ref.2.c_ref
  46.2 17.2 %shard_map.77 = (f32[128,128,128]{2,1,0:T(8,128)}, f32[16,128,1]{2,1,0:T(8,128)}, f32[16,1,128]{2,1,0:T(1,128)}) custom-call(s32[128]{0:T(128)} %src_sm.5, s32[128]{0:T(128)} %slot_sm.5, f32[128]{0:T(128)} %compare_convert_fusion.live_ref, f32[16,128,128]{2,1,0:T(8,128)} %bitcast.22, f32[16,128,128]{2,1,0:T(8,128)} %copy.15.tt_ref, ...), custom_call_target="tpu_custom_call" | custom-call | tf_op jit(solution)/shard_map/pallas_call | solution.py:155
  63.5 0.7 broadcast_in_dim.48
  64.2 14.6 %all_to_all.24 = f32[16,16,128]{2,1,0:T(8,128)S(1)} all-to-all(f32[16,16,128]{2,1,0:T(8,128)S(1)} %broadcast_in_dim.48), channel_id=1, replica_groups=mesh['groups'=2,'rows'=16] {'rows'}, dimensions={0} | all-to-all | bytes 262144 | tf_op jit(solution)/shard_map/all_to_all | solution.py:234
  78.7 0.1 select_reduce_fusion.1
  78.8 0.6 maximum_divide_fusion.1
  79.4 7.0 %shard_map.78 = (f32[16,128,1]{2,1,0:T(8,128)}, f32[16,1,128]{2,1,0:T(1,128)}) custom-call(s32[128]{0:T(128)} %src_sm.5, s32[128]{0:T(128)} %slot_sm.5, f32[128,128,128]{2,1,0:T(8,128)} %get-tuple-element.11.k_hbm, f32[16,1,128]{2,1,0:T(1,128)} %bitcast.25), custom_call_target="tpu_custom_call" | custom-call | tf_op jit(solution)/shard_map/pallas_call | solution.py:176
  86.5 0.7 broadcast_in_dim.51
  87.2 10.5 %all_to_all.25 = f32[16,16,128]{2,1,0:T(8,128)S(1)} all-to-all(f32[16,16,128]{2,1,0:T(8,128)S(1)} %broadcast_in_dim.51), channel_id=1, replica_groups=mesh['groups'=2,'rows'=16] {'rows'}, dimensions={0} | all-to-all | bytes 262144 | tf_op jit(solution)/shard_map/all_to_all | solution.py:234
  97.7 0.1 select_reduce_fusion
  97.8 0.6 maximum_divide_fusion
  98.4 0.0 copy-done
  98.4 13.3 %shard_map.79 = (f32[16,128,128]{2,1,0:T(8,128)}, f32[16,128]{1,0:T(8,128)}) custom-call(s32[128]{0:T(128)} %src_sm.5, s32[128]{0:T(128)} %slot_sm.5, f32[128,128,128]{2,1,0:T(8,128)} %get-tuple-element.11.k_hbm, f32[16,128,128]{2,1,0:T(8,128)} %copy-done, f32[16,1,128]{2,1,0:T(1,128)} %bitcast.24, f32[16,128,1]{2,1,0:T(8,128)} %get-tuple-element.15.r_ref), custom_call_target="tpu_custom_call" | custom-call | tf_op jit(solution)/shard_map/pallas_call | solution.py:196
  (4 shorter events, 0.0 us)
Async XLA Ops:
  1.9 13.7 %all-to-all-start = ((s32[16,1,16]{2,1,0:T(1,128)}), s32[16,1,16]{2,1,0:T(1,128)S(1)}, u32[]{:S(2)}, u32[]{:S(2)}) async-start(s32[16,1,16]{2,1,0:T(1,128)} %broadcast_in_dim.44), calls=%async_computation | async-start | bytes 16384 | tf_op jit(solution)/shard_map/all_to_all | solution.py:220
  17.7 26.6 %all-to-all-start.1 = ((f32[16,128,128]{2,1,0:T(8,128)}), f32[16,128,128]{2,1,0:T(8,128)S(1)}, u32[]{:S(2)}, u32[]{:S(2)}) async-start(f32[16,128,128]{2,1,0:T(8,128)} %gather_fusion), calls=%async_computation.1 | async-start | bytes 2097152 | tf_op jit(solution)/shard_map/all_to_all | solution.py:227
  44.2 54.2 %copy-start = (f32[16,128,128]{2,1,0:T(8,128)}, f32[16,128,128]{2,1,0:T(8,128)S(1)}, u32[]{:S(2)}) copy-start(f32[16,128,128]{2,1,0:T(8,128)S(1)} %all-to-all-done.1.t_ref) | copy-start | bytes 3145732

commit v10 on v9

--- a/solution.py
+++ b/solution.py
@@ -10,7 +10,7 @@
 E = 128
 BLOCK = 128
 ITERS = 2
-UNROLL = 4
+UNROLL = 8
 
 EPSILON = 1e-06
 SOFTMAX_WARMTH = 0.03
@@ -42,7 +42,10 @@
     def rows(t, carry):
         q = src_sm[t]
         o = slot_sm[t]
-        acc[q] += tile_at(t, q, o) * c_ref[o]
+        if c_ref is None:
+            acc[q] += tile_at(t, q, o)
+        else:
+            acc[q] += tile_at(t, q, o) * c_ref[o]
         return carry
 
     for part in range(capacity // step):
@@ -88,7 +91,7 @@
         if when == "after":
             copies[part].start()
 
-    _rows_cols(src_sm, slot_sm, build, chunk_done, k_scr, c_ref, r_out, colp_out, acc, rb_scr)
+    _rows_cols(src_sm, slot_sm, build, chunk_done, k_scr, None, r_out, colp_out, acc, rb_scr)
     for copy in copies:
         copy.wait()
 

time: 112 us -> 107 us (0.955)
  Pallas kernels: 37.6 us -> 32 us
    pallas_call x1, Pallas kernels: 17.2 us -> 14.2 us  [first_sweep(): pl.pallas_call(_first_kernel, out_shape=(jax.ShapeDtypeStruct((capacity,...]
    pallas_call x1, Pallas kernels: 13.3 us -> 11.1 us  [final(): pl.pallas_call(_final_kernel, out_shape=(jax.ShapeDtypeStruct((sb, BLOCK,...]
where the time goes in v10:
time: 107 us; the launch traced here: 106 us
  Pallas kernels  32 us (30%)
  blocking collectives  25.1 us (23%)
  waiting for transfers between devices  21 us (20%)
  starting transfers between devices  11 us (10%)
  other arithmetic  8.94 us (8%)
  local copies, waits for them, and re-layouts  6.72 us (6%)
  between operations  1.54 us (1%)
    all_to_all x2, blocking collectives, column_scale_of(): lax.all_to_all(spread, 'rows', split_axis=0, concat_axis=0, tiled=True)  25.1 us
    all_to_all x1, waiting for transfers between devices, on_device(): lax.all_to_all(outgoing, 'rows', split_axis=0, concat_axis=0, tiled=True)  16.9 us
    pallas_call x1, Pallas kernels, first_sweep(): pl.pallas_call(_first_kernel, out_shape=(jax.ShapeDtypeStruct((capacity,...  14.2 us
    pallas_call x1, Pallas kernels, final(): pl.pallas_call(_final_kernel, out_shape=(jax.ShapeDtypeStruct((sb, BLOCK,...  11.1 us
    all_to_all x1, starting transfers between devices, on_device(): lax.all_to_all(jnp.broadcast_to(wanted_row, (rows_n, slots)), 'rows', spl...  7.39 us
    pallas_call x1, Pallas kernels, again_sweep(): pl.pallas_call(_again_kernel, out_shape=(jax.ShapeDtypeStruct((sb, BLOCK,...  6.67 us
    all_to_all x1, waiting for transfers between devices, on_device(): lax.all_to_all(jnp.broadcast_to(wanted_row, (rows_n, slots)), 'rows', spl...  4.13 us
    all_to_all x1, starting transfers between devices, on_device(): lax.all_to_all(outgoing, 'rows', split_axis=0, concat_axis=0, tiled=True)  3.65 us
  transfers between devices with their start and end apart: 2, of which 2 were waited for; matrix products, arithmetic and copies ran while one was open for 7% of the time, Pallas kernels for 0%

profile of v10, /device:TPU:0, one launch (start us, length us, event | category | flops | bytes accessed | tf_op | source)
XLA Modules:
  0.0 106.3 jit_solution(1194700962267894164)
XLA Ops:
  0.6 1.3 %broadcast_in_dim.44 = s32[16,1,16]{2,1,0:T(1,128)} broadcast(s32[16]{0:T(128)} %bitcast.30), dimensions={2} | broadcast | bytes 1088 | tf_op jit(solution)/shard_map/broadcast_in_dim | solution.py:224
  1.9 7.4 %all-to-all-start = ((s32[16,1,16]{2,1,0:T(1,128)}), s32[16,1,16]{2,1,0:T(1,128)S(1)}, u32[]{:S(2)}, u32[]{:S(2)}) async-start(s32[16,1,16]{2,1,0:T(1,128)} %broadcast_in_dim.44), calls=%async_computation | async-start | bytes 16384 | tf_op jit(solution)/shard_map/all_to_all | solution.py:223
  9.3 1.1 %multiply_reduce_fusion.1 = f32[512]{0:T(512)S(1)} fusion(f32[512,128]{1,0:T(8,128)} %param.7), kind=kLoop, calls=%fused_computation.3 | loop fusion | flops 130560 | bytes 264192 | tf_op jit(solution)/shard_map/reduce_sum | solution.py:23
  10.4 1.1 %broadcast_multiply_fusion.1 = f32[512,128]{1,0:T(8,128)S(1)} fusion(f32[512,128]{1,0:T(8,128)} %param.7, f32[512]{0:T(512)S(1)} %add_rsqrt_fusion.1), kind=kLoop, calls=%fused_computation.6 | loop fusion | flops 65536 | bytes 526336 | tf_op jit(solution)/shard_map/mul | solution.py:23
  11.5 4.1 %all-to-all-done = s32[16,1,16]{2,1,0:T(1,128)S(1)} async-done(((s32[16,1,16]{2,1,0:T(1,128)}), s32[16,1,16]{2,1,0:T(1,128)S(1)}, u32[]{:S(2)}, u32[]{:S(2)}) %all-to-all-start) | async-done | bytes 1056 | tf_op jit(solution)/shard_map/all_to_all | solution.py:223
  15.6 0.4 dynamic-slice_reduce_fusion
  16.1 1.6 %gather_fusion = f32[16,128,128]{2,1,0:T(8,128)} fusion(f32[4,128,128]{2,1,0:T(8,128)S(1)} %bitcast.21, s32[1024]{0:T(1024)S(1)} %pad_clamp_fusion), kind=kCustom, calls=%fused_computation | custom fusion | bytes 2097216 | tf_op jit(solution)/shard_map/gather | solution.py:229
  17.7 3.7 %all-to-all-start.1 = ((f32[16,128,128]{2,1,0:T(8,128)}), f32[16,128,128]{2,1,0:T(8,128)S(1)}, u32[]{:S(2)}, u32[]{:S(2)}) async-start(f32[16,128,128]{2,1,0:T(8,128)} %gather_fusion), calls=%async_computation.1 | async-start | bytes 2097152 | tf_op jit(solution)/shard_map/all_to_all | solution.py:230
  22.0 0.6 compare_convert_fusion.live_ref
  22.6 1.6 %multiply_reduce_fusion = f32[2048]{0:T(1024)S(1)} fusion(f32[2048,128]{1,0:T(8,128)} %param.6), kind=kLoop, calls=%fused_computation.1 | loop fusion | flops 522240 | bytes 1056768 | tf_op jit(solution)/shard_map/reduce_sum | solution.py:23
  24.2 2.5 %broadcast_multiply_fusion = f32[2048,128]{1,0:T(8,128)} fusion(f32[2048,128]{1,0:T(8,128)} %param.6, f32[2048]{0:T(1024)S(1)} %add_rsqrt_fusion), kind=kLoop, calls=%fused_computation.2 | loop fusion | flops 262144 | bytes 2105344 | tf_op jit(solution)/shard_map/mul | solution.py:23
  26.7 0.7 broadcast_compare_fusion
  27.4 16.9 %all-to-all-done.1.t_ref = f32[16,128,128]{2,1,0:T(8,128)S(1)} async-done(((f32[16,128,128]{2,1,0:T(8,128)}), f32[16,128,128]{2,1,0:T(8,128)S(1)}, u32[]{:S(2)}, u32[]{:S(2)}) %all-to-all-start.1) | async-done | bytes 1048608 | tf_op jit(solution)/shard_map/all_to_all | solution.py:230
  44.2 0.0 copy-start
  44.2 1.4 %copy.15.tt_ref = f32[16,128,128]{2,1,0:T(8,128)} copy(f32[16,128,128]{1,2,0:T(8,128)S(1)} %bitcast.20) | data formatting | bytes 2097152 | tf_op jit(solution)/shard_map/optimization_barrier | solution.py:245
  45.6 0.6 broadcast_5_c_ref.2.c_ref
  46.2 14.2 %shard_map.77 = (f32[128,128,128]{2,1,0:T(8,128)}, f32[16,128,1]{2,1,0:T(8,128)}, f32[16,1,128]{2,1,0:T(1,128)}) custom-call(s32[128]{0:T(128)} %src_sm.5, s32[128]{0:T(128)} %slot_sm.5, f32[128]{0:T(128)} %compare_convert_fusion.live_ref, f32[16,128,128]{2,1,0:T(8,128)} %bitcast.22, f32[16,128,128]{2,1,0:T(8,128)} %copy.15.tt_ref, ...), custom_call_target="tpu_custom_call" | custom-call | tf_op jit(solution)/shard_map/pallas_call | solution.py:158
  60.5 0.7 broadcast_in_dim.48
  61.2 14.6 %all_to_all.24 = f32[16,16,128]{2,1,0:T(8,128)S(1)} all-to-all(f32[16,16,128]{2,1,0:T(8,128)S(1)} %broadcast_in_dim.48), channel_id=1, replica_groups=mesh['groups'=2,'rows'=16] {'rows'}, dimensions={0} | all-to-all | bytes 262144 | tf_op jit(solution)/shard_map/all_to_all | solution.py:237
  75.7 0.1 select_reduce_fusion.1
  75.8 0.6 maximum_divide_fusion.1
  76.4 6.7 %shard_map.78 = (f32[16,128,1]{2,1,0:T(8,128)}, f32[16,1,128]{2,1,0:T(1,128)}) custom-call(s32[128]{0:T(128)} %src_sm.5, s32[128]{0:T(128)} %slot_sm.5, f32[128,128,128]{2,1,0:T(8,128)} %get-tuple-element.11.k_hbm, f32[16,1,128]{2,1,0:T(1,128)} %bitcast.25), custom_call_target="tpu_custom_call" | custom-call | tf_op jit(solution)/shard_map/pallas_call | solution.py:179
  83.1 0.7 broadcast_in_dim.51
  83.8 10.5 %all_to_all.25 = f32[16,16,128]{2,1,0:T(8,128)S(1)} all-to-all(f32[16,16,128]{2,1,0:T(8,128)S(1)} %broadcast_in_dim.51), channel_id=1, replica_groups=mesh['groups'=2,'rows'=16] {'rows'}, dimensions={0} | all-to-all | bytes 262144 | tf_op jit(solution)/shard_map/all_to_all | solution.py:237
  94.4 0.1 select_reduce_fusion
  94.5 0.6 maximum_divide_fusion
  95.1 0.0 copy-done
  95.1 11.1 %shard_map.79 = (f32[16,128,128]{2,1,0:T(8,128)}, f32[16,128]{1,0:T(8,128)}) custom-call(s32[128]{0:T(128)} %src_sm.5, s32[128]{0:T(128)} %slot_sm.5, f32[128,128,128]{2,1,0:T(8,128)} %get-tuple-element.11.k_hbm, f32[16,128,128]{2,1,0:T(8,128)} %copy-done, f32[16,1,128]{2,1,0:T(1,128)} %bitcast.24, f32[16,128,1]{2,1,0:T(8,128)} %get-tuple-element.15.r_ref), custom_call_target="tpu_custom_call" | custom-call | tf_op jit(solution)/shard_map/pallas_call | solution.py:199
  (4 shorter events, 0.0 us)
Async XLA Ops:
  1.9 13.7 %all-to-all-start = ((s32[16,1,16]{2,1,0:T(1,128)}), s32[16,1,16]{2,1,0:T(1,128)S(1)}, u32[]{:S(2)}, u32[]{:S(2)}) async-start(s32[16,1,16]{2,1,0:T(1,128)} %broadcast_in_dim.44), calls=%async_computation | async-start | bytes 16384 | tf_op jit(solution)/shard_map/all_to_all | solution.py:223
  17.7 26.6 %all-to-all-start.1 = ((f32[16,128,128]{2,1,0:T(8,128)}), f32[16,128,128]{2,1,0:T(8,128)S(1)}, u32[]{:S(2)}, u32[]{:S(2)}) async-start(f32[16,128,128]{2,1,0:T(8,128)} %gather_fusion), calls=%async_computation.1 | async-start | bytes 2097152 | tf_op jit(solution)/shard_map/all_to_all | solution.py:230
  44.2 50.8 %copy-start = (f32[16,128,128]{2,1,0:T(8,128)}, f32[16,128,128]{2,1,0:T(8,128)S(1)}, u32[]{:S(2)}) copy-start(f32[16,128,128]{2,1,0:T(8,128)S(1)} %all-to-all-done.1.t_ref) | copy-start | bytes 3145732

commit v11 on v10

--- a/solution.py
+++ b/solution.py
@@ -10,7 +10,7 @@
 E = 128
 BLOCK = 128
 ITERS = 2
-UNROLL = 8
+UNROLL = 16
 
 EPSILON = 1e-06
 SOFTMAX_WARMTH = 0.03

time: 107 us -> 103 us (0.963)
  Pallas kernels: 32 us -> 28.1 us
    pallas_call x1, Pallas kernels: 14.2 us -> 11.8 us  [first_sweep(): pl.pallas_call(_first_kernel, out_shape=(jax.ShapeDtypeStruct((capacity,...]
    pallas_call x1, Pallas kernels: 11.1 us -> 9.82 us  [final(): pl.pallas_call(_final_kernel, out_shape=(jax.ShapeDtypeStruct((sb, BLOCK,...]
where the time goes in v11:
time: 103 us; the launch traced here: 102 us
  Pallas kernels  28.1 us (27%)
  blocking collectives  25.1 us (24%)
  waiting for transfers between devices  21 us (20%)
  starting transfers between devices  11 us (11%)
  other arithmetic  8.94 us (9%)
  local copies, waits for them, and re-layouts  6.72 us (7%)
  between operations  1.54 us (1%)
    all_to_all x2, blocking collectives, column_scale_of(): lax.all_to_all(spread, 'rows', split_axis=0, concat_axis=0, tiled=True)  25.1 us
    all_to_all x1, waiting for transfers between devices, on_device(): lax.all_to_all(outgoing, 'rows', split_axis=0, concat_axis=0, tiled=True)  16.9 us
    pallas_call x1, Pallas kernels, first_sweep(): pl.pallas_call(_first_kernel, out_shape=(jax.ShapeDtypeStruct((capacity,...  11.8 us
    pallas_call x1, Pallas kernels, final(): pl.pallas_call(_final_kernel, out_shape=(jax.ShapeDtypeStruct((sb, BLOCK,...  9.82 us
    all_to_all x1, starting transfers between devices, on_device(): lax.all_to_all(jnp.broadcast_to(wanted_row, (rows_n, slots)), 'rows', spl...  7.39 us
    pallas_call x1, Pallas kernels, again_sweep(): pl.pallas_call(_again_kernel, out_shape=(jax.ShapeDtypeStruct((sb, BLOCK,...  6.53 us
    all_to_all x1, waiting for transfers between devices, on_device(): lax.all_to_all(jnp.broadcast_to(wanted_row, (rows_n, slots)), 'rows', spl...  4.13 us
    all_to_all x1, starting transfers between devices, on_device(): lax.all_to_all(outgoing, 'rows', split_axis=0, concat_axis=0, tiled=True)  3.65 us
  transfers between devices with their start and end apart: 2, of which 2 were waited for; matrix products, arithmetic and copies ran while one was open for 7% of the time, Pallas kernels for 0%

profile of v11, /device:TPU:0, one launch (start us, length us, event | category | flops | bytes accessed | tf_op | source)
XLA Modules:
  0.0 102.4 jit_solution(10737038605301235744)
XLA Ops:
  0.6 1.3 %broadcast_in_dim.44 = s32[16,1,16]{2,1,0:T(1,128)} broadcast(s32[16]{0:T(128)} %bitcast.30), dimensions={2} | broadcast | bytes 1088 | tf_op jit(solution)/shard_map/broadcast_in_dim | solution.py:224
  1.9 7.4 %all-to-all-start = ((s32[16,1,16]{2,1,0:T(1,128)}), s32[16,1,16]{2,1,0:T(1,128)S(1)}, u32[]{:S(2)}, u32[]{:S(2)}) async-start(s32[16,1,16]{2,1,0:T(1,128)} %broadcast_in_dim.44), calls=%async_computation | async-start | bytes 16384 | tf_op jit(solution)/shard_map/all_to_all | solution.py:223
  9.3 1.1 %multiply_reduce_fusion.1 = f32[512]{0:T(512)S(1)} fusion(f32[512,128]{1,0:T(8,128)} %param.7), kind=kLoop, calls=%fused_computation.3 | loop fusion | flops 130560 | bytes 264192 | tf_op jit(solution)/shard_map/reduce_sum | solution.py:23
  10.4 1.1 %broadcast_multiply_fusion.1 = f32[512,128]{1,0:T(8,128)S(1)} fusion(f32[512,128]{1,0:T(8,128)} %param.7, f32[512]{0:T(512)S(1)} %add_rsqrt_fusion.1), kind=kLoop, calls=%fused_computation.6 | loop fusion | flops 65536 | bytes 526336 | tf_op jit(solution)/shard_map/mul | solution.py:23
  11.5 4.1 %all-to-all-done = s32[16,1,16]{2,1,0:T(1,128)S(1)} async-done(((s32[16,1,16]{2,1,0:T(1,128)}), s32[16,1,16]{2,1,0:T(1,128)S(1)}, u32[]{:S(2)}, u32[]{:S(2)}) %all-to-all-start) | async-done | bytes 1056 | tf_op jit(solution)/shard_map/all_to_all | solution.py:223
  15.6 0.4 dynamic-slice_reduce_fusion
  16.1 1.6 %gather_fusion = f32[16,128,128]{2,1,0:T(8,128)} fusion(f32[4,128,128]{2,1,0:T(8,128)S(1)} %bitcast.21, s32[1024]{0:T(1024)S(1)} %pad_clamp_fusion), kind=kCustom, calls=%fused_computation | custom fusion | bytes 2097216 | tf_op jit(solution)/shard_map/gather | solution.py:229
  17.7 3.7 %all-to-all-start.1 = ((f32[16,128,128]{2,1,0:T(8,128)}), f32[16,128,128]{2,1,0:T(8,128)S(1)}, u32[]{:S(2)}, u32[]{:S(2)}) async-start(f32[16,128,128]{2,1,0:T(8,128)} %gather_fusion), calls=%async_computation.1 | async-start | bytes 2097152 | tf_op jit(solution)/shard_map/all_to_all | solution.py:230
  22.0 0.6 compare_convert_fusion.live_ref
  22.6 1.6 %multiply_reduce_fusion = f32[2048]{0:T(1024)S(1)} fusion(f32[2048,128]{1,0:T(8,128)} %param.6), kind=kLoop, calls=%fused_computation.1 | loop fusion | flops 522240 | bytes 1056768 | tf_op jit(solution)/shard_map/reduce_sum | solution.py:23
  24.2 2.5 %broadcast_multiply_fusion = f32[2048,128]{1,0:T(8,128)} fusion(f32[2048,128]{1,0:T(8,128)} %param.6, f32[2048]{0:T(1024)S(1)} %add_rsqrt_fusion), kind=kLoop, calls=%fused_computation.2 | loop fusion | flops 262144 | bytes 2105344 | tf_op jit(solution)/shard_map/mul | solution.py:23
  26.7 0.7 broadcast_compare_fusion
  27.4 16.9 %all-to-all-done.1.t_ref = f32[16,128,128]{2,1,0:T(8,128)S(1)} async-done(((f32[16,128,128]{2,1,0:T(8,128)}), f32[16,128,128]{2,1,0:T(8,128)S(1)}, u32[]{:S(2)}, u32[]{:S(2)}) %all-to-all-start.1) | async-done | bytes 1048608 | tf_op jit(solution)/shard_map/all_to_all | solution.py:230
  44.2 0.0 copy-start
  44.2 1.4 %copy.15.tt_ref = f32[16,128,128]{2,1,0:T(8,128)} copy(f32[16,128,128]{1,2,0:T(8,128)S(1)} %bitcast.20) | data formatting | bytes 2097152 | tf_op jit(solution)/shard_map/optimization_barrier | solution.py:245
  45.6 0.6 broadcast_5_c_ref.2.c_ref
  46.2 11.8 %shard_map.77 = (f32[128,128,128]{2,1,0:T(8,128)}, f32[16,128,1]{2,1,0:T(8,128)}, f32[16,1,128]{2,1,0:T(1,128)}) custom-call(s32[128]{0:T(128)} %src_sm.5, s32[128]{0:T(128)} %slot_sm.5, f32[128]{0:T(128)} %compare_convert_fusion.live_ref, f32[16,128,128]{2,1,0:T(8,128)} %bitcast.22, f32[16,128,128]{2,1,0:T(8,128)} %copy.15.tt_ref, ...), custom_call_target="tpu_custom_call" | custom-call | tf_op jit(solution)/shard_map/pallas_call | solution.py:158
  58.0 0.7 broadcast_in_dim.48
  58.7 14.6 %all_to_all.24 = f32[16,16,128]{2,1,0:T(8,128)S(1)} all-to-all(f32[16,16,128]{2,1,0:T(8,128)S(1)} %broadcast_in_dim.48), channel_id=1, replica_groups=mesh['groups'=2,'rows'=16] {'rows'}, dimensions={0} | all-to-all | bytes 262144 | tf_op jit(solution)/shard_map/all_to_all | solution.py:237
  73.3 0.1 select_reduce_fusion.1
  73.4 0.6 maximum_divide_fusion.1
  74.0 6.5 %shard_map.78 = (f32[16,128,1]{2,1,0:T(8,128)}, f32[16,1,128]{2,1,0:T(1,128)}) custom-call(s32[128]{0:T(128)} %src_sm.5, s32[128]{0:T(128)} %slot_sm.5, f32[128,128,128]{2,1,0:T(8,128)} %get-tuple-element.11.k_hbm, f32[16,1,128]{2,1,0:T(1,128)} %bitcast.25), custom_call_target="tpu_custom_call" | custom-call | tf_op jit(solution)/shard_map/pallas_call | solution.py:179
  80.5 0.7 broadcast_in_dim.51
  81.2 10.5 %all_to_all.25 = f32[16,16,128]{2,1,0:T(8,128)S(1)} all-to-all(f32[16,16,128]{2,1,0:T(8,128)S(1)} %broadcast_in_dim.51), channel_id=1, replica_groups=mesh['groups'=2,'rows'=16] {'rows'}, dimensions={0} | all-to-all | bytes 262144 | tf_op jit(solution)/shard_map/all_to_all | solution.py:237
  91.8 0.1 select_reduce_fusion
  91.9 0.6 maximum_divide_fusion
  92.5 0.0 copy-done
  92.5 9.8 %shard_map.79 = (f32[16,128,128]{2,1,0:T(8,128)}, f32[16,128]{1,0:T(8,128)}) custom-call(s32[128]{0:T(128)} %src_sm.5, s32[128]{0:T(128)} %slot_sm.5, f32[128,128,128]{2,1,0:T(8,128)} %get-tuple-element.11.k_hbm, f32[16,128,128]{2,1,0:T(8,128)} %copy-done, f32[16,1,128]{2,1,0:T(1,128)} %bitcast.24, f32[16,128,1]{2,1,0:T(8,128)} %get-tuple-element.15.r_ref), custom_call_target="tpu_custom_call" | custom-call | tf_op jit(solution)/shard_map/pallas_call | solution.py:199
  (4 shorter events, 0.0 us)
Async XLA Ops:
  1.9 13.7 %all-to-all-start = ((s32[16,1,16]{2,1,0:T(1,128)}), s32[16,1,16]{2,1,0:T(1,128)S(1)}, u32[]{:S(2)}, u32[]{:S(2)}) async-start(s32[16,1,16]{2,1,0:T(1,128)} %broadcast_in_dim.44), calls=%async_computation | async-start | bytes 16384 | tf_op jit(solution)/shard_map/all_to_all | solution.py:223
  17.7 26.6 %all-to-all-start.1 = ((f32[16,128,128]{2,1,0:T(8,128)}), f32[16,128,128]{2,1,0:T(8,128)S(1)}, u32[]{:S(2)}, u32[]{:S(2)}) async-start(f32[16,128,128]{2,1,0:T(8,128)} %gather_fusion), calls=%async_computation.1 | async-start | bytes 2097152 | tf_op jit(solution)/shard_map/all_to_all | solution.py:230
  44.2 48.2 %copy-start = (f32[16,128,128]{2,1,0:T(8,128)}, f32[16,128,128]{2,1,0:T(8,128)S(1)}, u32[]{:S(2)}) copy-start(f32[16,128,128]{2,1,0:T(8,128)S(1)} %all-to-all-done.1.t_ref) | copy-start | bytes 3145732

commit v12 on v11

--- a/solution.py
+++ b/solution.py
@@ -32,7 +32,7 @@
     return math.gcd(capacity, 16)
 
 
-def _rows_cols(src_sm, slot_sm, tile_at, chunk_done, k_ref, c_ref, r_out, colp_out, acc, rb_scr):
+def _rows_cols(src_sm, slot_sm, tile_at, chunk_done, k_ref, c_ref, r_out, spread_out, acc, rb_scr, colp_out):
     capacity = src_sm.shape[0]
     sb = acc.shape[0]
     step = _chunk(capacity)
@@ -64,6 +64,9 @@
         return carry
 
     lax.fori_loop(0, capacity, cols, 0, unroll=UNROLL)
+    partials = jnp.concatenate([colp_out[o] for o in range(colp_out.shape[0])], axis=0)
+    for d in range(spread_out.shape[0]):
+        spread_out[d] = partials
 
 
 def _chunk_copies(src, dst, sems, capacity):
@@ -77,7 +80,7 @@
 
 
 def _first_kernel(
-    src_sm, slot_sm, live_ref, s_ref, tt_ref, c_ref, k_hbm, r_out, colp_out, k_scr, acc, rb_scr, sems
+    src_sm, slot_sm, live_ref, s_ref, tt_ref, k_hbm, r_out, spread_out, k_scr, acc, rb_scr, colp, sems
 ):
     capacity = src_sm.shape[0]
     copies = _chunk_copies(k_scr, k_hbm, sems, capacity)
@@ -91,12 +94,12 @@
         if when == "after":
             copies[part].start()
 
-    _rows_cols(src_sm, slot_sm, build, chunk_done, k_scr, None, r_out, colp_out, acc, rb_scr)
+    _rows_cols(src_sm, slot_sm, build, chunk_done, k_scr, None, r_out, spread_out, acc, rb_scr, colp)
     for copy in copies:
         copy.wait()
 
 
-def _again_kernel(src_sm, slot_sm, k_hbm, c_ref, r_out, colp_out, k_scr, acc, rb_scr, sems):
+def _again_kernel(src_sm, slot_sm, k_hbm, c_ref, r_out, spread_out, k_scr, acc, rb_scr, colp, sems):
     capacity = src_sm.shape[0]
     copies = _chunk_copies(k_hbm, k_scr, sems, capacity)
     for copy in copies:
@@ -107,7 +110,17 @@
             copies[part].wait()
 
     _rows_cols(
-        src_sm, slot_sm, lambda t, q, o: k_scr[t], chunk_done, k_scr, c_ref, r_out, colp_out, acc, rb_scr
+        src_sm,
+        slot_sm,
+        lambda t, q, o: k_scr[t],
+        chunk_done,
+        k_scr,
+        c_ref,
+        r_out,
+        spread_out,
+        acc,
+        rb_scr,
+        colp,
     )
 
 
@@ -151,7 +164,7 @@
 _ANY = pl.BlockSpec(memory_space=pl.ANY)
 
 
-def first_sweep(tile_source, tile_slot, live, source_unit, fetched_t, col):
+def first_sweep(tile_source, tile_slot, live, source_unit, fetched_t, rows_n):
     capacity = tile_source.shape[0]
     sb = source_unit.shape[0]
     slots = fetched_t.shape[0]
@@ -160,27 +173,28 @@
         out_shape=(
             jax.ShapeDtypeStruct((capacity, BLOCK, BLOCK), jnp.float32),
             jax.ShapeDtypeStruct((sb, BLOCK, 1), jnp.float32),
-            jax.ShapeDtypeStruct((slots, 1, BLOCK), jnp.float32),
+            jax.ShapeDtypeStruct((rows_n, slots, BLOCK), jnp.float32),
         ),
-        in_specs=_specs(3, 3),
+        in_specs=_specs(3, 2),
         out_specs=(_ANY,) + _vmem_out(2),
         scratch_shapes=[
             pltpu.VMEM((capacity, BLOCK, BLOCK), jnp.float32),
             pltpu.VMEM((sb, BLOCK, BLOCK), jnp.float32),
             pltpu.VMEM((sb, BLOCK, BLOCK), jnp.float32),
+            pltpu.VMEM((slots, 1, BLOCK), jnp.float32),
             pltpu.SemaphoreType.DMA((capacity // _chunk(capacity),)),
         ],
-    )(tile_source, tile_slot, live, source_unit, fetched_t, col)
-
-
-def again_sweep(tile_source, tile_slot, kernel, col, sb):
+    )(tile_source, tile_slot, live, source_unit, fetched_t)
+
+
+def again_sweep(tile_source, tile_slot, kernel, col, sb, rows_n):
     capacity = tile_source.shape[0]
     slots = col.shape[0]
     return pl.pallas_call(
         _again_kernel,
         out_shape=(
             jax.ShapeDtypeStruct((sb, BLOCK, 1), jnp.float32),
-            jax.ShapeDtypeStruct((slots, 1, BLOCK), jnp.float32),
+            jax.ShapeDtypeStruct((rows_n, slots, BLOCK), jnp.float32),
         ),
         in_specs=_specs(2, 0) + [_ANY] + _specs(0, 1),
         out_specs=_vmem_out(2),
@@ -188,6 +202,7 @@
             pltpu.VMEM((capacity, BLOCK, BLOCK), jnp.float32),
             pltpu.VMEM((sb, BLOCK, BLOCK), jnp.float32),
             pltpu.VMEM((sb, BLOCK, BLOCK), jnp.float32),
+            pltpu.VMEM((slots, 1, BLOCK), jnp.float32),
             pltpu.SemaphoreType.DMA((capacity // _chunk(capacity),)),
         ],
     )(tile_source, tile_slot, kernel, col)
@@ -232,21 +247,19 @@
         wanted_all.reshape(rows_n, owners, need, 1) == wanted.reshape(1, owners, 1, need)
     )[..., None]
 
-    def column_scale_of(colp):
-        spread = jnp.broadcast_to(colp.reshape(1, slots, BLOCK), (rows_n, slots, BLOCK))
+    def column_scale_of(spread):
         gathered = lax.all_to_all(spread, "rows", split_axis=0, concat_axis=0, tiled=True)
         gathered = gathered.reshape(rows_n, owners, need, 1, BLOCK)
         totals = jnp.sum(jnp.where(same_block, gathered, 0.0), axis=(0, 2))
         return (1.0 / jnp.maximum(totals, COLUMN_FLOOR)).reshape(slots, 1, BLOCK)
 
     live = (jnp.arange(tile_source.shape[0]) < tile_count[0]).astype(jnp.float32)
-    col = jnp.ones((slots, 1, BLOCK), jnp.float32)
     sb = source_unit.shape[0]
     fetched_t, same_block = lax.optimization_barrier((jnp.swapaxes(fetched, 1, 2), same_block))
-    kernel, row, colp = first_sweep(tile_source, tile_slot, live, source_unit, fetched_t, col)
+    kernel, row, colp = first_sweep(tile_source, tile_slot, live, source_unit, fetched_t, rows_n)
     for iteration in range(1, ITERS):
         col = column_scale_of(colp)
-        row, colp = again_sweep(tile_source, tile_slot, kernel, col, sb)
+        row, colp = again_sweep(tile_source, tile_slot, kernel, col, sb, rows_n)
     col = column_scale_of(colp)
     al, ms = final(tile_source, tile_slot, kernel, fetched, col, row)
     return (al.reshape(-1, E), ms.reshape(-1))

time: 103 us -> 102 us (level)
  local copies, waits for them, and re-layouts: 6.72 us -> 4.7 us
  blocking collectives: 25.1 us -> 26.2 us
    broadcast_in_dim x2 -> x0, local copies, waits for them, and re-layouts: 1.42 us -> none  [column_scale_of(): jnp.broadcast_to(colp.reshape(1, slots, BLOCK), (rows_n, slots, BLOCK))]
    all_to_all x2, blocking collectives: 25.1 us -> 26.2 us  [column_scale_of(): lax.all_to_all(spread, 'rows', split_axis=0, concat_axis=0, tiled=True)]
where the time goes in v12:
time: 102 us
  Pallas kernels  28.4 us (28%)
  blocking collectives  26.2 us (26%)
  waiting for transfers between devices  21 us (21%)
  starting transfers between devices  11 us (11%)
  other arithmetic  8.93 us (9%)
  local copies, waits for them, and re-layouts  4.7 us (5%)
  between operations  1.54 us (2%)
    all_to_all x2, blocking collectives, column_scale_of(): lax.all_to_all(spread, 'rows', split_axis=0, concat_axis=0, tiled=True)  26.2 us
    all_to_all x1, waiting for transfers between devices, on_device(): lax.all_to_all(outgoing, 'rows', split_axis=0, concat_axis=0, tiled=True)  16.9 us
    pallas_call x1, Pallas kernels, first_sweep(): pl.pallas_call(_first_kernel, out_shape=(jax.ShapeDtypeStruct((capacity,...  12 us
    pallas_call x1, Pallas kernels, final(): pl.pallas_call(_final_kernel, out_shape=(jax.ShapeDtypeStruct((sb, BLOCK,...  9.82 us
    all_to_all x1, starting transfers between devices, on_device(): lax.all_to_all(jnp.broadcast_to(wanted_row, (rows_n, slots)), 'rows', spl...  7.39 us
    pallas_call x1, Pallas kernels, again_sweep(): pl.pallas_call(_again_kernel, out_shape=(jax.ShapeDtypeStruct((sb, BLOCK,...  6.52 us
    all_to_all x1, waiting for transfers between devices, on_device(): lax.all_to_all(jnp.broadcast_to(wanted_row, (rows_n, slots)), 'rows', spl...  4.13 us
    all_to_all x1, starting transfers between devices, on_device(): lax.all_to_all(outgoing, 'rows', split_axis=0, concat_axis=0, tiled=True)  3.65 us
  transfers between devices with their start and end apart: 2, of which 2 were waited for; matrix products, arithmetic and copies ran while one was open for 7% of the time, Pallas kernels for 0%

profile of v12, /device:TPU:0, one launch (start us, length us, event | category | flops | bytes accessed | tf_op | source)
XLA Modules:
  0.0 101.8 jit_solution(5618235735477071946)
XLA Ops:
  0.6 1.3 %broadcast_in_dim.30 = s32[16,1,16]{2,1,0:T(1,128)} broadcast(s32[16]{0:T(128)} %bitcast.26), dimensions={2} | broadcast | bytes 1088 | tf_op jit(solution)/shard_map/broadcast_in_dim | solution.py:239
  1.9 7.4 %all-to-all-start = ((s32[16,1,16]{2,1,0:T(1,128)}), s32[16,1,16]{2,1,0:T(1,128)S(1)}, u32[]{:S(2)}, u32[]{:S(2)}) async-start(s32[16,1,16]{2,1,0:T(1,128)} %broadcast_in_dim.30), calls=%async_computation | async-start | bytes 16384 | tf_op jit(solution)/shard_map/all_to_all | solution.py:238
  9.3 1.1 %multiply_reduce_fusion.1 = f32[512]{0:T(512)S(1)} fusion(f32[512,128]{1,0:T(8,128)} %param.7), kind=kLoop, calls=%fused_computation.3 | loop fusion | flops 130560 | bytes 264192 | tf_op jit(solution)/shard_map/reduce_sum | solution.py:23
  10.4 1.1 %broadcast_multiply_fusion.1 = f32[512,128]{1,0:T(8,128)S(1)} fusion(f32[512,128]{1,0:T(8,128)} %param.7, f32[512]{0:T(512)S(1)} %add_rsqrt_fusion.1), kind=kLoop, calls=%fused_computation.6 | loop fusion | flops 65536 | bytes 526336 | tf_op jit(solution)/shard_map/mul | solution.py:23
  11.5 4.1 %all-to-all-done = s32[16,1,16]{2,1,0:T(1,128)S(1)} async-done(((s32[16,1,16]{2,1,0:T(1,128)}), s32[16,1,16]{2,1,0:T(1,128)S(1)}, u32[]{:S(2)}, u32[]{:S(2)}) %all-to-all-start) | async-done | bytes 1056 | tf_op jit(solution)/shard_map/all_to_all | solution.py:238
  15.6 0.4 dynamic-slice_reduce_fusion
  16.1 1.6 %gather_fusion = f32[16,128,128]{2,1,0:T(8,128)} fusion(f32[4,128,128]{2,1,0:T(8,128)S(1)} %bitcast.19, s32[1024]{0:T(1024)S(1)} %pad_clamp_fusion), kind=kCustom, calls=%fused_computation | custom fusion | bytes 2097216 | tf_op jit(solution)/shard_map/gather | solution.py:244
  17.7 3.7 %all-to-all-start.1 = ((f32[16,128,128]{2,1,0:T(8,128)}), f32[16,128,128]{2,1,0:T(8,128)S(1)}, u32[]{:S(2)}, u32[]{:S(2)}) async-start(f32[16,128,128]{2,1,0:T(8,128)} %gather_fusion), calls=%async_computation.1 | async-start | bytes 2097152 | tf_op jit(solution)/shard_map/all_to_all | solution.py:245
  22.0 0.6 compare_convert_fusion.live_ref
  22.6 1.6 %multiply_reduce_fusion = f32[2048]{0:T(1024)S(1)} fusion(f32[2048,128]{1,0:T(8,128)} %param.6), kind=kLoop, calls=%fused_computation.1 | loop fusion | flops 522240 | bytes 1056768 | tf_op jit(solution)/shard_map/reduce_sum | solution.py:23
  24.1 2.5 %broadcast_multiply_fusion = f32[2048,128]{1,0:T(8,128)} fusion(f32[2048,128]{1,0:T(8,128)} %param.6, f32[2048]{0:T(1024)S(1)} %add_rsqrt_fusion), kind=kLoop, calls=%fused_computation.2 | loop fusion | flops 262144 | bytes 2105344 | tf_op jit(solution)/shard_map/mul | solution.py:23
  26.7 0.7 broadcast_compare_fusion
  27.3 16.9 %all-to-all-done.1.t_ref = f32[16,128,128]{2,1,0:T(8,128)S(1)} async-done(((f32[16,128,128]{2,1,0:T(8,128)}), f32[16,128,128]{2,1,0:T(8,128)S(1)}, u32[]{:S(2)}, u32[]{:S(2)}) %all-to-all-start.1) | async-done | bytes 1048608 | tf_op jit(solution)/shard_map/all_to_all | solution.py:245
  44.2 0.0 copy-start
  44.2 1.4 %copy.13.tt_ref = f32[16,128,128]{2,1,0:T(8,128)} copy(f32[16,128,128]{1,2,0:T(8,128)S(1)} %bitcast.18) | data formatting | bytes 2097152 | tf_op jit(solution)/shard_map/optimization_barrier | solution.py:258
  45.6 12.0 %shard_map.77 = (f32[128,128,128]{2,1,0:T(8,128)}, f32[16,128,1]{2,1,0:T(8,128)}, f32[16,16,128]{2,1,0:T(8,128)}) custom-call(s32[128]{0:T(128)} %src_sm.5, s32[128]{0:T(128)} %slot_sm.5, f32[128]{0:T(128)} %compare_convert_fusion.live_ref, f32[16,128,128]{2,1,0:T(8,128)} %bitcast.20, f32[16,128,128]{2,1,0:T(8,128)} %copy.13.tt_ref), custom_call_target="tpu_custom_call" | custom-call | tf_op jit(solution)/shard_map/pallas_call | solution.py:171
  57.7 14.8 %all_to_all.24 = f32[16,16,128]{2,1,0:T(8,128)S(1)} all-to-all(f32[16,16,128]{2,1,0:T(8,128)} %get-tuple-element.13), channel_id=1, replica_groups=mesh['groups'=2,'rows'=16] {'rows'}, dimensions={0} | all-to-all | bytes 262144 | tf_op jit(solution)/shard_map/all_to_all | solution.py:251
  72.4 0.1 select_reduce_fusion.1
  72.5 0.6 maximum_divide_fusion.1
  73.1 6.5 %shard_map.78 = (f32[16,128,1]{2,1,0:T(8,128)}, f32[16,16,128]{2,1,0:T(8,128)}) custom-call(s32[128]{0:T(128)} %src_sm.5, s32[128]{0:T(128)} %slot_sm.5, f32[128,128,128]{2,1,0:T(8,128)} %get-tuple-element.11.k_hbm, f32[16,1,128]{2,1,0:T(1,128)} %bitcast.23), custom_call_target="tpu_custom_call" | custom-call | tf_op jit(solution)/shard_map/pallas_call | solution.py:193
  79.7 11.4 %all_to_all.25 = f32[16,16,128]{2,1,0:T(8,128)S(1)} all-to-all(f32[16,16,128]{2,1,0:T(8,128)} %get-tuple-element.14), channel_id=1, replica_groups=mesh['groups'=2,'rows'=16] {'rows'}, dimensions={0} | all-to-all | bytes 262144 | tf_op jit(solution)/shard_map/all_to_all | solution.py:251
  91.1 0.1 select_reduce_fusion
  91.2 0.6 maximum_divide_fusion
  91.8 0.0 copy-done
  91.8 9.8 %shard_map.79 = (f32[16,128,128]{2,1,0:T(8,128)}, f32[16,128]{1,0:T(8,128)}) custom-call(s32[128]{0:T(128)} %src_sm.5, s32[128]{0:T(128)} %slot_sm.5, f32[128,128,128]{2,1,0:T(8,128)} %get-tuple-element.11.k_hbm, f32[16,128,128]{2,1,0:T(8,128)} %copy-done, f32[16,1,128]{2,1,0:T(1,128)} %bitcast.22, f32[16,128,1]{2,1,0:T(8,128)} %get-tuple-element.15.r_ref), custom_call_target="tpu_custom_call" | custom-call | tf_op jit(solution)/shard_map/pallas_call | solution.py:214
  (4 shorter events, 0.0 us)
Async XLA Ops:
  1.9 13.7 %all-to-all-start = ((s32[16,1,16]{2,1,0:T(1,128)}), s32[16,1,16]{2,1,0:T(1,128)S(1)}, u32[]{:S(2)}, u32[]{:S(2)}) async-start(s32[16,1,16]{2,1,0:T(1,128)} %broadcast_in_dim.30), calls=%async_computation | async-start | bytes 16384 | tf_op jit(solution)/shard_map/all_to_all | solution.py:238
  17.7 26.6 %all-to-all-start.1 = ((f32[16,128,128]{2,1,0:T(8,128)}), f32[16,128,128]{2,1,0:T(8,128)S(1)}, u32[]{:S(2)}, u32[]{:S(2)}) async-start(f32[16,128,128]{2,1,0:T(8,128)} %gather_fusion), calls=%async_computation.1 | async-start | bytes 2097152 | tf_op jit(solution)/shard_map/all_to_all | solution.py:245
  44.2 47.5 %copy-start = (f32[16,128,128]{2,1,0:T(8,128)}, f32[16,128,128]{2,1,0:T(8,128)S(1)}, u32[]{:S(2)}) copy-start(f32[16,128,128]{2,1,0:T(8,128)S(1)} %all-to-all-done.1.t_ref) | copy-start | bytes 3145732

commit v13 on v12

--- a/solution.py
+++ b/solution.py
@@ -10,7 +10,7 @@
 E = 128
 BLOCK = 128
 ITERS = 2
-UNROLL = 16
+UNROLL = 32
 
 EPSILON = 1e-06
 SOFTMAX_WARMTH = 0.03
@@ -29,7 +29,7 @@
 
 
 def _chunk(capacity):
-    return math.gcd(capacity, 16)
+    return math.gcd(capacity, 32)
 
 
 def _rows_cols(src_sm, slot_sm, tile_at, chunk_done, k_ref, c_ref, r_out, spread_out, acc, rb_scr, colp_out):

time: 102 us -> 102 us (level)
  no operation moved by 1% of the time
where the time goes in v13:
time: 102 us
  Pallas kernels  28.2 us (28%)
  blocking collectives  26.2 us (26%)
  waiting for transfers between devices  21 us (21%)
  starting transfers between devices  11 us (11%)
  other arithmetic  8.93 us (9%)
  local copies, waits for them, and re-layouts  4.7 us (5%)
  between operations  1.54 us (2%)
    all_to_all x2, blocking collectives, column_scale_of(): lax.all_to_all(spread, 'rows', split_axis=0, concat_axis=0, tiled=True)  26.2 us
    all_to_all x1, waiting for transfers between devices, on_device(): lax.all_to_all(outgoing, 'rows', split_axis=0, concat_axis=0, tiled=True)  16.9 us
    pallas_call x1, Pallas kernels, first_sweep(): pl.pallas_call(_first_kernel, out_shape=(jax.ShapeDtypeStruct((capacity,...  12 us
    pallas_call x1, Pallas kernels, final(): pl.pallas_call(_final_kernel, out_shape=(jax.ShapeDtypeStruct((sb, BLOCK,...  9.53 us
    all_to_all x1, starting transfers between devices, on_device(): lax.all_to_all(jnp.broadcast_to(wanted_row, (rows_n, slots)), 'rows', spl...  7.39 us
    pallas_call x1, Pallas kernels, again_sweep(): pl.pallas_call(_again_kernel, out_shape=(jax.ShapeDtypeStruct((sb, BLOCK,...  6.64 us
    all_to_all x1, waiting for transfers between devices, on_device(): lax.all_to_all(jnp.broadcast_to(wanted_row, (rows_n, slots)), 'rows', spl...  4.13 us
    all_to_all x1, starting transfers between devices, on_device(): lax.all_to_all(outgoing, 'rows', split_axis=0, concat_axis=0, tiled=True)  3.65 us
  transfers between devices with their start and end apart: 2, of which 2 were waited for; matrix products, arithmetic and copies ran while one was open for 7% of the time, Pallas kernels for 0%

profile of v13, /device:TPU:0, one launch (start us, length us, event | category | flops | bytes accessed | tf_op | source)
XLA Modules:
  0.0 101.6 jit_solution(10945116314288895856)
XLA Ops:
  0.6 1.3 %broadcast_in_dim.30 = s32[16,1,16]{2,1,0:T(1,128)} broadcast(s32[16]{0:T(128)} %bitcast.26), dimensions={2} | broadcast | bytes 1088 | tf_op jit(solution)/shard_map/broadcast_in_dim | solution.py:239
  1.9 7.4 %all-to-all-start = ((s32[16,1,16]{2,1,0:T(1,128)}), s32[16,1,16]{2,1,0:T(1,128)S(1)}, u32[]{:S(2)}, u32[]{:S(2)}) async-start(s32[16,1,16]{2,1,0:T(1,128)} %broadcast_in_dim.30), calls=%async_computation | async-start | bytes 16384 | tf_op jit(solution)/shard_map/all_to_all | solution.py:238
  9.3 1.1 %multiply_reduce_fusion.1 = f32[512]{0:T(512)S(1)} fusion(f32[512,128]{1,0:T(8,128)} %param.7), kind=kLoop, calls=%fused_computation.3 | loop fusion | flops 130560 | bytes 264192 | tf_op jit(solution)/shard_map/reduce_sum | solution.py:23
  10.4 1.1 %broadcast_multiply_fusion.1 = f32[512,128]{1,0:T(8,128)S(1)} fusion(f32[512,128]{1,0:T(8,128)} %param.7, f32[512]{0:T(512)S(1)} %add_rsqrt_fusion.1), kind=kLoop, calls=%fused_computation.6 | loop fusion | flops 65536 | bytes 526336 | tf_op jit(solution)/shard_map/mul | solution.py:23
  11.5 4.1 %all-to-all-done = s32[16,1,16]{2,1,0:T(1,128)S(1)} async-done(((s32[16,1,16]{2,1,0:T(1,128)}), s32[16,1,16]{2,1,0:T(1,128)S(1)}, u32[]{:S(2)}, u32[]{:S(2)}) %all-to-all-start) | async-done | bytes 1056 | tf_op jit(solution)/shard_map/all_to_all | solution.py:238
  15.6 0.4 dynamic-slice_reduce_fusion
  16.1 1.6 %gather_fusion = f32[16,128,128]{2,1,0:T(8,128)} fusion(f32[4,128,128]{2,1,0:T(8,128)S(1)} %bitcast.19, s32[1024]{0:T(1024)S(1)} %pad_clamp_fusion), kind=kCustom, calls=%fused_computation | custom fusion | bytes 2097216 | tf_op jit(solution)/shard_map/gather | solution.py:244
  17.7 3.7 %all-to-all-start.1 = ((f32[16,128,128]{2,1,0:T(8,128)}), f32[16,128,128]{2,1,0:T(8,128)S(1)}, u32[]{:S(2)}, u32[]{:S(2)}) async-start(f32[16,128,128]{2,1,0:T(8,128)} %gather_fusion), calls=%async_computation.1 | async-start | bytes 2097152 | tf_op jit(solution)/shard_map/all_to_all | solution.py:245
  22.0 0.6 compare_convert_fusion.live_ref
  22.6 1.6 %multiply_reduce_fusion = f32[2048]{0:T(1024)S(1)} fusion(f32[2048,128]{1,0:T(8,128)} %param.6), kind=kLoop, calls=%fused_computation.1 | loop fusion | flops 522240 | bytes 1056768 | tf_op jit(solution)/shard_map/reduce_sum | solution.py:23
  24.1 2.5 %broadcast_multiply_fusion = f32[2048,128]{1,0:T(8,128)} fusion(f32[2048,128]{1,0:T(8,128)} %param.6, f32[2048]{0:T(1024)S(1)} %add_rsqrt_fusion), kind=kLoop, calls=%fused_computation.2 | loop fusion | flops 262144 | bytes 2105344 | tf_op jit(solution)/shard_map/mul | solution.py:23
  26.7 0.7 broadcast_compare_fusion
  27.3 16.9 %all-to-all-done.1.t_ref = f32[16,128,128]{2,1,0:T(8,128)S(1)} async-done(((f32[16,128,128]{2,1,0:T(8,128)}), f32[16,128,128]{2,1,0:T(8,128)S(1)}, u32[]{:S(2)}, u32[]{:S(2)}) %all-to-all-start.1) | async-done | bytes 1048608 | tf_op jit(solution)/shard_map/all_to_all | solution.py:245
  44.2 0.0 copy-start
  44.2 1.4 %copy.13.tt_ref = f32[16,128,128]{2,1,0:T(8,128)} copy(f32[16,128,128]{1,2,0:T(8,128)S(1)} %bitcast.18) | data formatting | bytes 2097152 | tf_op jit(solution)/shard_map/optimization_barrier | solution.py:258
  45.6 12.0 %shard_map.77 = (f32[128,128,128]{2,1,0:T(8,128)}, f32[16,128,1]{2,1,0:T(8,128)}, f32[16,16,128]{2,1,0:T(8,128)}) custom-call(s32[128]{0:T(128)} %src_sm.5, s32[128]{0:T(128)} %slot_sm.5, f32[128]{0:T(128)} %compare_convert_fusion.live_ref, f32[16,128,128]{2,1,0:T(8,128)} %bitcast.20, f32[16,128,128]{2,1,0:T(8,128)} %copy.13.tt_ref), custom_call_target="tpu_custom_call" | custom-call | tf_op jit(solution)/shard_map/pallas_call | solution.py:171
  57.7 14.8 %all_to_all.24 = f32[16,16,128]{2,1,0:T(8,128)S(1)} all-to-all(f32[16,16,128]{2,1,0:T(8,128)} %get-tuple-element.13), channel_id=1, replica_groups=mesh['groups'=2,'rows'=16] {'rows'}, dimensions={0} | all-to-all | bytes 262144 | tf_op jit(solution)/shard_map/all_to_all | solution.py:251
  72.5 0.1 select_reduce_fusion.1
  72.6 0.6 maximum_divide_fusion.1
  73.2 6.6 %shard_map.78 = (f32[16,128,1]{2,1,0:T(8,128)}, f32[16,16,128]{2,1,0:T(8,128)}) custom-call(s32[128]{0:T(128)} %src_sm.5, s32[128]{0:T(128)} %slot_sm.5, f32[128,128,128]{2,1,0:T(8,128)} %get-tuple-element.11.k_hbm, f32[16,1,128]{2,1,0:T(1,128)} %bitcast.23), custom_call_target="tpu_custom_call" | custom-call | tf_op jit(solution)/shard_map/pallas_call | solution.py:193
  79.8 11.4 %all_to_all.25 = f32[16,16,128]{2,1,0:T(8,128)S(1)} all-to-all(f32[16,16,128]{2,1,0:T(8,128)} %get-tuple-element.14), channel_id=1, replica_groups=mesh['groups'=2,'rows'=16] {'rows'}, dimensions={0} | all-to-all | bytes 262144 | tf_op jit(solution)/shard_map/all_to_all | solution.py:251
  91.2 0.1 select_reduce_fusion
  91.3 0.6 maximum_divide_fusion
  91.9 0.0 copy-done
  91.9 9.5 %shard_map.79 = (f32[16,128,128]{2,1,0:T(8,128)}, f32[16,128]{1,0:T(8,128)}) custom-call(s32[128]{0:T(128)} %src_sm.5, s32[128]{0:T(128)} %slot_sm.5, f32[128,128,128]{2,1,0:T(8,128)} %get-tuple-element.11.k_hbm, f32[16,128,128]{2,1,0:T(8,128)} %copy-done, f32[16,1,128]{2,1,0:T(1,128)} %bitcast.22, f32[16,128,1]{2,1,0:T(8,128)} %get-tuple-element.15.r_ref), custom_call_target="tpu_custom_call" | custom-call | tf_op jit(solution)/shard_map/pallas_call | solution.py:214
  (4 shorter events, 0.0 us)
Async XLA Ops:
  1.9 13.7 %all-to-all-start = ((s32[16,1,16]{2,1,0:T(1,128)}), s32[16,1,16]{2,1,0:T(1,128)S(1)}, u32[]{:S(2)}, u32[]{:S(2)}) async-start(s32[16,1,16]{2,1,0:T(1,128)} %broadcast_in_dim.30), calls=%async_computation | async-start | bytes 16384 | tf_op jit(solution)/shard_map/all_to_all | solution.py:238
  17.7 26.6 %all-to-all-start.1 = ((f32[16,128,128]{2,1,0:T(8,128)}), f32[16,128,128]{2,1,0:T(8,128)S(1)}, u32[]{:S(2)}, u32[]{:S(2)}) async-start(f32[16,128,128]{2,1,0:T(8,128)} %gather_fusion), calls=%async_computation.1 | async-start | bytes 2097152 | tf_op jit(solution)/shard_map/all_to_all | solution.py:245
  44.2 47.7 %copy-start = (f32[16,128,128]{2,1,0:T(8,128)}, f32[16,128,128]{2,1,0:T(8,128)S(1)}, u32[]{:S(2)}) copy-start(f32[16,128,128]{2,1,0:T(8,128)S(1)} %all-to-all-done.1.t_ref) | copy-start | bytes 3145732

commit v14 on v13

--- a/solution.py
+++ b/solution.py
@@ -124,12 +124,16 @@
     )
 
 
-def _final_kernel(src_sm, slot_sm, k_hbm, t_ref, c_ref, r_ref, al_out, ms_out, k_scr, ms_scr, sems):
+def _final_kernel(
+    src_sm, slot_sm, k_hbm, tt_ref, c_ref, r_ref, al_out, ms_out, k_scr, ms_scr, t_ref, sems
+):
     capacity = src_sm.shape[0]
     step = _chunk(capacity)
     copies = _chunk_copies(k_hbm, k_scr, sems, capacity)
     for copy in copies:
         copy.start()
+    for o in range(t_ref.shape[0]):
+        t_ref[o] = jnp.transpose(tt_ref[o])
     al_out[...] = jnp.zeros_like(al_out)
     ms_scr[...] = jnp.zeros_like(ms_scr)
 
@@ -208,9 +212,10 @@
     )(tile_source, tile_slot, kernel, col)
 
 
-def final(tile_source, tile_slot, kernel, fetched, col, row):
+def final(tile_source, tile_slot, kernel, fetched_t, col, row):
     capacity = tile_source.shape[0]
     sb = row.shape[0]
+    slots = fetched_t.shape[0]
     return pl.pallas_call(
         _final_kernel,
         out_shape=(
@@ -222,9 +227,10 @@
         scratch_shapes=[
             pltpu.VMEM((capacity, BLOCK, BLOCK), jnp.float32),
             pltpu.VMEM((sb, BLOCK, BLOCK), jnp.float32),
+            pltpu.VMEM((slots, BLOCK, E), jnp.float32),
             pltpu.SemaphoreType.DMA((capacity // _chunk(capacity),)),
         ],
-    )(tile_source, tile_slot, kernel, fetched, col, row)
+    )(tile_source, tile_slot, kernel, fetched_t, col, row)
 
 
 def on_device(source_emb, target_emb, tile_source, tile_slot, tile_count, wanted):
@@ -240,9 +246,9 @@
     )
     me = lax.axis_index("rows")
     asked = lax.dynamic_slice_in_dim(wanted_all, me * need, need, axis=1)
-    own_unit = unit_rows(target_emb).reshape(target_blocks, BLOCK, E)
-    outgoing = own_unit[asked.reshape(-1)]
-    fetched = lax.all_to_all(outgoing, "rows", split_axis=0, concat_axis=0, tiled=True)
+    own_unit_t = jnp.swapaxes(unit_rows(target_emb).reshape(target_blocks, BLOCK, E), 1, 2)
+    outgoing = own_unit_t[asked.reshape(-1)]
+    fetched_t = lax.all_to_all(outgoing, "rows", split_axis=0, concat_axis=0, tiled=True)
     same_block = (
         wanted_all.reshape(rows_n, owners, need, 1) == wanted.reshape(1, owners, 1, need)
     )[..., None]
@@ -255,13 +261,13 @@
 
     live = (jnp.arange(tile_source.shape[0]) < tile_count[0]).astype(jnp.float32)
     sb = source_unit.shape[0]
-    fetched_t, same_block = lax.optimization_barrier((jnp.swapaxes(fetched, 1, 2), same_block))
+    fetched_t, same_block = lax.optimization_barrier((fetched_t, same_block))
     kernel, row, colp = first_sweep(tile_source, tile_slot, live, source_unit, fetched_t, rows_n)
     for iteration in range(1, ITERS):
         col = column_scale_of(colp)
         row, colp = again_sweep(tile_source, tile_slot, kernel, col, sb, rows_n)
     col = column_scale_of(colp)
-    al, ms = final(tile_source, tile_slot, kernel, fetched, col, row)
+    al, ms = final(tile_source, tile_slot, kernel, fetched_t, col, row)
     return (al.reshape(-1, E), ms.reshape(-1))
 
 

time: 102 us -> 102 us (level)
    optimization_barrier x1 -> x0, local copies, waits for them, and re-layouts: 1.39 us -> none  [on_device(): lax.optimization_barrier((jnp.swapaxes(fetched, 1, 2), same_block))]
    unnamed x2 -> x4, local copies, waits for them, and re-layouts: 0.01 us -> 1.07 us
where the time goes in v14:
time: 102 us; the launch traced here: 101 us
  Pallas kernels  28.2 us (28%)
  blocking collectives  26.2 us (26%)
  waiting for transfers between devices  21.5 us (21%)
  starting transfers between devices  11 us (11%)
  other arithmetic  8.3 us (8%)
  local copies, waits for them, and re-layouts  4.57 us (4%)
  between operations  1.56 us (2%)
    all_to_all x2, blocking collectives, column_scale_of(): lax.all_to_all(spread, 'rows', split_axis=0, concat_axis=0, tiled=True)  26.2 us
    all_to_all x1, waiting for transfers between devices, on_device(): lax.all_to_all(outgoing, 'rows', split_axis=0, concat_axis=0, tiled=True)  17.5 us
    pallas_call x1, Pallas kernels, first_sweep(): pl.pallas_call(_first_kernel, out_shape=(jax.ShapeDtypeStruct((capacity,...  12 us
    pallas_call x1, Pallas kernels, final(): pl.pallas_call(_final_kernel, out_shape=(jax.ShapeDtypeStruct((sb, BLOCK,...  9.52 us
    all_to_all x1, starting transfers between devices, on_device(): lax.all_to_all(jnp.broadcast_to(wanted_row, (rows_n, slots)), 'rows', spl...  7.39 us
    pallas_call x1, Pallas kernels, again_sweep(): pl.pallas_call(_again_kernel, out_shape=(jax.ShapeDtypeStruct((sb, BLOCK,...  6.65 us
    all_to_all x1, waiting for transfers between devices, on_device(): lax.all_to_all(jnp.broadcast_to(wanted_row, (rows_n, slots)), 'rows', spl...  3.99 us
    all_to_all x1, starting transfers between devices, on_device(): lax.all_to_all(outgoing, 'rows', split_axis=0, concat_axis=0, tiled=True)  3.65 us
  transfers between devices with their start and end apart: 2, of which 2 were waited for; matrix products, arithmetic and copies ran while one was open for 7% of the time, Pallas kernels for 0%

profile of v14, /device:TPU:0, one launch (start us, length us, event | category | flops | bytes accessed | tf_op | source)
XLA Modules:
  0.0 101.4 jit_solution(77148831498979223)
XLA Ops:
  0.6 0.0 copy-start.1
  0.6 1.3 %broadcast_in_dim.30 = s32[16,1,16]{2,1,0:T(1,128)} broadcast(s32[16]{0:T(128)} %bitcast.26), dimensions={2} | broadcast | bytes 1088 | tf_op jit(solution)/shard_map/broadcast_in_dim | solution.py:245
  2.0 7.4 %all-to-all-start = ((s32[16,1,16]{2,1,0:T(1,128)}), s32[16,1,16]{2,1,0:T(1,128)S(1)}, u32[]{:S(2)}, u32[]{:S(2)}) async-start(s32[16,1,16]{2,1,0:T(1,128)} %broadcast_in_dim.30), calls=%async_computation | async-start | bytes 16384 | tf_op jit(solution)/shard_map/all_to_all | solution.py:244
  9.4 1.1 %multiply_reduce_fusion.1 = f32[512]{0:T(512)S(1)} fusion(f32[512,128]{1,0:T(8,128)} %param.7), kind=kLoop, calls=%fused_computation.3 | loop fusion | flops 130560 | bytes 264192 | tf_op jit(solution)/shard_map/reduce_sum | solution.py:23
  10.5 1.1 %broadcast_multiply_fusion.1 = f32[512,128]{1,0:T(8,128)S(1)} fusion(f32[512,128]{1,0:T(8,128)} %param.7, f32[512]{0:T(512)S(1)} %add_rsqrt_fusion.1), kind=kLoop, calls=%fused_computation.6 | loop fusion | flops 65536 | bytes 526336 | tf_op jit(solution)/shard_map/mul | solution.py:23
  11.6 0.1 copy.17
  11.7 4.0 %all-to-all-done = s32[16,1,16]{2,1,0:T(1,128)S(1)} async-done(((s32[16,1,16]{2,1,0:T(1,128)}), s32[16,1,16]{2,1,0:T(1,128)S(1)}, u32[]{:S(2)}, u32[]{:S(2)}) %all-to-all-start) | async-done | bytes 1056 | tf_op jit(solution)/shard_map/all_to_all | solution.py:244
  15.7 0.4 dynamic-slice_reduce_fusion
  16.2 1.6 %gather_fusion = f32[16,128,128]{2,1,0:T(8,128)} fusion(f32[4,128,128]{2,1,0:T(8,128)S(1)} %bitcast.18, s32[1024]{0:T(1024)S(1)} %pad_clamp_fusion), kind=kCustom, calls=%fused_computation | custom fusion | bytes 2097216 | tf_op jit(solution)/shard_map/gather | solution.py:250
  17.8 3.7 %all-to-all-start.1 = ((f32[16,128,128]{2,1,0:T(8,128)}), f32[16,128,128]{2,1,0:T(8,128)S(1)}, u32[]{:S(2)}, u32[]{:S(2)}) async-start(f32[16,128,128]{2,1,0:T(8,128)} %gather_fusion), calls=%async_computation.1 | async-start | bytes 2097152 | tf_op jit(solution)/shard_map/all_to_all | solution.py:251
  22.1 0.6 compare_convert_fusion.live_ref
  22.7 1.6 %multiply_reduce_fusion = f32[2048]{0:T(1024)S(1)} fusion(f32[2048,128]{1,0:T(8,128)} %param.6), kind=kLoop, calls=%fused_computation.1 | loop fusion | flops 522240 | bytes 1056768 | tf_op jit(solution)/shard_map/reduce_sum | solution.py:23
  24.2 2.5 %broadcast_multiply_fusion = f32[2048,128]{1,0:T(8,128)} fusion(f32[2048,128]{1,0:T(8,128)} %param.6, f32[2048]{0:T(1024)S(1)} %add_rsqrt_fusion), kind=kLoop, calls=%fused_computation.2 | loop fusion | flops 262144 | bytes 2105344 | tf_op jit(solution)/shard_map/mul | solution.py:23
  26.8 0.0 copy-done.1
  26.8 17.5 %all-to-all-done.1.tt_ref = f32[16,128,128]{2,1,0:T(8,128)S(1)} async-done(((f32[16,128,128]{2,1,0:T(8,128)}), f32[16,128,128]{2,1,0:T(8,128)S(1)}, u32[]{:S(2)}, u32[]{:S(2)}) %all-to-all-start.1) | async-done | bytes 1048608 | tf_op jit(solution)/shard_map/all_to_all | solution.py:251
  44.3 0.0 copy-start
  44.3 1.1 %copy-done = f32[16,128,128]{2,1,0:T(8,128)} copy-done((f32[16,128,128]{2,1,0:T(8,128)}, f32[16,128,128]{2,1,0:T(8,128)S(1)}, u32[]{:S(2)}) %copy-start) | copy-done | bytes 1048600
  45.4 12.0 %shard_map.77 = (f32[128,128,128]{2,1,0:T(8,128)}, f32[16,128,1]{2,1,0:T(8,128)}, f32[16,16,128]{2,1,0:T(8,128)}) custom-call(s32[128]{0:T(128)} %src_sm.5, s32[128]{0:T(128)} %slot_sm.5, f32[128]{0:T(128)} %compare_convert_fusion.live_ref, f32[16,128,128]{2,1,0:T(8,128)} %bitcast.19, f32[16,128,128]{2,1,0:T(8,128)} %copy-done), custom_call_target="tpu_custom_call" | custom-call | tf_op jit(solution)/shard_map/pallas_call | solution.py:175
  57.4 14.8 %all_to_all.24 = f32[16,16,128]{2,1,0:T(8,128)S(1)} all-to-all(f32[16,16,128]{2,1,0:T(8,128)} %get-tuple-element.13), channel_id=1, replica_groups=mesh['groups'=2,'rows'=16] {'rows'}, dimensions={0} | all-to-all | bytes 262144 | tf_op jit(solution)/shard_map/all_to_all | solution.py:257
  72.2 0.1 select_reduce_fusion.1
  72.3 0.6 maximum_divide_fusion.1
  72.9 6.6 %shard_map.78 = (f32[16,128,1]{2,1,0:T(8,128)}, f32[16,16,128]{2,1,0:T(8,128)}) custom-call(s32[128]{0:T(128)} %src_sm.5, s32[128]{0:T(128)} %slot_sm.5, f32[128,128,128]{2,1,0:T(8,128)} %get-tuple-element.11.k_hbm, f32[16,1,128]{2,1,0:T(1,128)} %bitcast.23), custom_call_target="tpu_custom_call" | custom-call | tf_op jit(solution)/shard_map/pallas_call | solution.py:197
  79.5 11.4 %all_to_all.25 = f32[16,16,128]{2,1,0:T(8,128)S(1)} all-to-all(f32[16,16,128]{2,1,0:T(8,128)} %get-tuple-element.14), channel_id=1, replica_groups=mesh['groups'=2,'rows'=16] {'rows'}, dimensions={0} | all-to-all | bytes 262144 | tf_op jit(solution)/shard_map/all_to_all | solution.py:257
  91.0 0.1 select_reduce_fusion
  91.1 0.6 maximum_divide_fusion
  91.7 9.5 %shard_map.79 = (f32[16,128,128]{2,1,0:T(8,128)}, f32[16,128]{1,0:T(8,128)}) custom-call(s32[128]{0:T(128)} %src_sm.5, s32[128]{0:T(128)} %slot_sm.5, f32[128,128,128]{2,1,0:T(8,128)} %get-tuple-element.11.k_hbm, f32[16,128,128]{2,1,0:T(8,128)} %copy-done, f32[16,1,128]{2,1,0:T(1,128)} %bitcast.22, f32[16,128,1]{2,1,0:T(8,128)} %get-tuple-element.15.r_ref), custom_call_target="tpu_custom_call" | custom-call | tf_op jit(solution)/shard_map/pallas_call | solution.py:219
  (5 shorter events, 0.0 us)
Async XLA Ops:
  0.6 26.2 %copy-start.1 = (s32[16,1]{0,1:T(1,128)S(1)}, s32[16,1]{0,1:T(1,128)}, u32[]{:S(2)}) copy-start(s32[16,1]{0,1:T(1,128)} %param.11) | copy-start | bytes 196
  2.0 13.7 %all-to-all-start = ((s32[16,1,16]{2,1,0:T(1,128)}), s32[16,1,16]{2,1,0:T(1,128)S(1)}, u32[]{:S(2)}, u32[]{:S(2)}) async-start(s32[16,1,16]{2,1,0:T(1,128)} %broadcast_in_dim.30), calls=%async_computation | async-start | bytes 16384 | tf_op jit(solution)/shard_map/all_to_all | solution.py:244
  17.8 26.6 %all-to-all-start.1 = ((f32[16,128,128]{2,1,0:T(8,128)}), f32[16,128,128]{2,1,0:T(8,128)S(1)}, u32[]{:S(2)}, u32[]{:S(2)}) async-start(f32[16,128,128]{2,1,0:T(8,128)} %gather_fusion), calls=%async_computation.1 | async-start | bytes 2097152 | tf_op jit(solution)/shard_map/all_to_all | solution.py:251
  44.3 1.1 %copy-start = (f32[16,128,128]{2,1,0:T(8,128)}, f32[16,128,128]{2,1,0:T(8,128)S(1)}, u32[]{:S(2)}) copy-start(f32[16,128,128]{2,1,0:T(8,128)S(1)} %all-to-all-done.1.tt_ref) | copy-start | bytes 3145732

commit v15 on v14

--- a/solution.py
+++ b/solution.py
@@ -28,14 +28,21 @@
     return jnp.exp(cosine / SOFTMAX_WARMTH)
 
 
-def _chunk(capacity):
-    return math.gcd(capacity, 32)
+def _bounds(capacity):
+    step = math.gcd(capacity, 32)
+    if step == 32 and capacity >= 64:
+        return [0, 8] + list(range(32, capacity + 1, 32))
+    return list(range(0, capacity + 1, step))
+
+
+def _loop(lo, hi, body):
+    lax.fori_loop(lo, hi, body, 0, unroll=min(UNROLL, hi - lo))
 
 
 def _rows_cols(src_sm, slot_sm, tile_at, chunk_done, k_ref, c_ref, r_out, spread_out, acc, rb_scr, colp_out):
     capacity = src_sm.shape[0]
     sb = acc.shape[0]
-    step = _chunk(capacity)
+    bounds = _bounds(capacity)
     acc[...] = jnp.zeros_like(acc)
     colp_out[...] = jnp.zeros_like(colp_out)
 
@@ -48,9 +55,9 @@
             acc[q] += tile_at(t, q, o) * c_ref[o]
         return carry
 
-    for part in range(capacity // step):
+    for part in range(len(bounds) - 1):
         chunk_done(part, "before")
-        lax.fori_loop(part * step, (part + 1) * step, rows, 0, unroll=UNROLL)
+        _loop(bounds[part], bounds[part + 1], rows)
         chunk_done(part, "after")
     for q in range(sb):
         r = 1.0 / jnp.maximum(jnp.sum(acc[q], axis=1, keepdims=True), ROW_MINIMUM)
@@ -70,12 +77,12 @@
 
 
 def _chunk_copies(src, dst, sems, capacity):
-    step = _chunk(capacity)
+    bounds = _bounds(capacity)
     return [
         pltpu.make_async_copy(
-            src.at[pl.ds(part * step, step)], dst.at[pl.ds(part * step, step)], sems.at[part]
+            src.at[pl.ds(lo, hi - lo)], dst.at[pl.ds(lo, hi - lo)], sems.at[part]
         )
-        for part in range(capacity // step)
+        for part, (lo, hi) in enumerate(zip(bounds[:-1], bounds[1:]))
     ]
 
 
@@ -128,7 +135,7 @@
     src_sm, slot_sm, k_hbm, tt_ref, c_ref, r_ref, al_out, ms_out, k_scr, ms_scr, t_ref, sems
 ):
     capacity = src_sm.shape[0]
-    step = _chunk(capacity)
+    bounds = _bounds(capacity)
     copies = _chunk_copies(k_hbm, k_scr, sems, capacity)
     for copy in copies:
         copy.start()
@@ -145,9 +152,9 @@
         ms_scr[q] += kc
         return carry
 
-    for part in range(capacity // step):
+    for part in range(len(bounds) - 1):
         copies[part].wait()
-        lax.fori_loop(part * step, (part + 1) * step, body, 0, unroll=UNROLL)
+        _loop(bounds[part], bounds[part + 1], body)
     r = r_ref[...]
     al_out[...] = al_out[...] * r * math.sqrt(E)
     for q in range(ms_out.shape[0]):
@@ -186,7 +193,7 @@
             pltpu.VMEM((sb, BLOCK, BLOCK), jnp.float32),
             pltpu.VMEM((sb, BLOCK, BLOCK), jnp.float32),
             pltpu.VMEM((slots, 1, BLOCK), jnp.float32),
-            pltpu.SemaphoreType.DMA((capacity // _chunk(capacity),)),
+            pltpu.SemaphoreType.DMA((len(_bounds(capacity)) - 1,)),
         ],
     )(tile_source, tile_slot, live, source_unit, fetched_t)
 
@@ -207,7 +214,7 @@
             pltpu.VMEM((sb, BLOCK, BLOCK), jnp.float32),
             pltpu.VMEM((sb, BLOCK, BLOCK), jnp.float32),
             pltpu.VMEM((slots, 1, BLOCK), jnp.float32),
-            pltpu.SemaphoreType.DMA((capacity // _chunk(capacity),)),
+            pltpu.SemaphoreType.DMA((len(_bounds(capacity)) - 1,)),
         ],
     )(tile_source, tile_slot, kernel, col)
 
@@ -228,7 +235,7 @@
             pltpu.VMEM((capacity, BLOCK, BLOCK), jnp.float32),
             pltpu.VMEM((sb, BLOCK, BLOCK), jnp.float32),
             pltpu.VMEM((slots, BLOCK, E), jnp.float32),
-            pltpu.SemaphoreType.DMA((capacity // _chunk(capacity),)),
+            pltpu.SemaphoreType.DMA((len(_bounds(capacity)) - 1,)),
         ],
     )(tile_source, tile_slot, kernel, fetched_t, col, row)
 

time: 102 us -> 102 us (level)
  no operation moved by 1% of the time
where the time goes in v15:
time: 102 us; the launch traced here: 101 us
  Pallas kernels  27.9 us (27%)
  blocking collectives  26.2 us (26%)
  waiting for transfers between devices  21.5 us (21%)
  starting transfers between devices  11 us (11%)
  other arithmetic  8.3 us (8%)
  local copies, waits for them, and re-layouts  4.57 us (4%)
  between operations  1.56 us (2%)
    all_to_all x2, blocking collectives, column_scale_of(): lax.all_to_all(spread, 'rows', split_axis=0, concat_axis=0, tiled=True)  26.2 us
    all_to_all x1, waiting for transfers between devices, on_device(): lax.all_to_all(outgoing, 'rows', split_axis=0, concat_axis=0, tiled=True)  17.5 us
    pallas_call x1, Pallas kernels, first_sweep(): pl.pallas_call(_first_kernel, out_shape=(jax.ShapeDtypeStruct((capacity,...  12 us
    pallas_call x1, Pallas kernels, final(): pl.pallas_call(_final_kernel, out_shape=(jax.ShapeDtypeStruct((sb, BLOCK,...  9.23 us
    all_to_all x1, starting transfers between devices, on_device(): lax.all_to_all(jnp.broadcast_to(wanted_row, (rows_n, slots)), 'rows', spl...  7.39 us
    pallas_call x1, Pallas kernels, again_sweep(): pl.pallas_call(_again_kernel, out_shape=(jax.ShapeDtypeStruct((sb, BLOCK,...  6.67 us
    all_to_all x1, waiting for transfers between devices, on_device(): lax.all_to_all(jnp.broadcast_to(wanted_row, (rows_n, slots)), 'rows', spl...  3.99 us
    all_to_all x1, starting transfers between devices, on_device(): lax.all_to_all(outgoing, 'rows', split_axis=0, concat_axis=0, tiled=True)  3.65 us
  transfers between devices with their start and end apart: 2, of which 2 were waited for; matrix products, arithmetic and copies ran while one was open for 7% of the time, Pallas kernels for 0%

profile of v15, /device:TPU:0, one launch (start us, length us, event | category | flops | bytes accessed | tf_op | source)
XLA Modules:
  0.0 101.1 jit_solution(1187052486440907385)
XLA Ops:
  0.6 0.0 copy-start.1
  0.6 1.3 %broadcast_in_dim.30 = s32[16,1,16]{2,1,0:T(1,128)} broadcast(s32[16]{0:T(128)} %bitcast.26), dimensions={2} | broadcast | bytes 1088 | tf_op jit(solution)/shard_map/broadcast_in_dim | solution.py:252
  2.0 7.4 %all-to-all-start = ((s32[16,1,16]{2,1,0:T(1,128)}), s32[16,1,16]{2,1,0:T(1,128)S(1)}, u32[]{:S(2)}, u32[]{:S(2)}) async-start(s32[16,1,16]{2,1,0:T(1,128)} %broadcast_in_dim.30), calls=%async_computation | async-start | bytes 16384 | tf_op jit(solution)/shard_map/all_to_all | solution.py:251
  9.4 1.1 %multiply_reduce_fusion.1 = f32[512]{0:T(512)S(1)} fusion(f32[512,128]{1,0:T(8,128)} %param.7), kind=kLoop, calls=%fused_computation.3 | loop fusion | flops 130560 | bytes 264192 | tf_op jit(solution)/shard_map/reduce_sum | solution.py:23
  10.5 1.1 %broadcast_multiply_fusion.1 = f32[512,128]{1,0:T(8,128)S(1)} fusion(f32[512,128]{1,0:T(8,128)} %param.7, f32[512]{0:T(512)S(1)} %add_rsqrt_fusion.1), kind=kLoop, calls=%fused_computation.6 | loop fusion | flops 65536 | bytes 526336 | tf_op jit(solution)/shard_map/mul | solution.py:23
  11.6 0.1 copy.17
  11.7 4.0 %all-to-all-done = s32[16,1,16]{2,1,0:T(1,128)S(1)} async-done(((s32[16,1,16]{2,1,0:T(1,128)}), s32[16,1,16]{2,1,0:T(1,128)S(1)}, u32[]{:S(2)}, u32[]{:S(2)}) %all-to-all-start) | async-done | bytes 1056 | tf_op jit(solution)/shard_map/all_to_all | solution.py:251
  15.7 0.4 dynamic-slice_reduce_fusion
  16.2 1.6 %gather_fusion = f32[16,128,128]{2,1,0:T(8,128)} fusion(f32[4,128,128]{2,1,0:T(8,128)S(1)} %bitcast.18, s32[1024]{0:T(1024)S(1)} %pad_clamp_fusion), kind=kCustom, calls=%fused_computation | custom fusion | bytes 2097216 | tf_op jit(solution)/shard_map/gather | solution.py:257
  17.8 3.7 %all-to-all-start.1 = ((f32[16,128,128]{2,1,0:T(8,128)}), f32[16,128,128]{2,1,0:T(8,128)S(1)}, u32[]{:S(2)}, u32[]{:S(2)}) async-start(f32[16,128,128]{2,1,0:T(8,128)} %gather_fusion), calls=%async_computation.1 | async-start | bytes 2097152 | tf_op jit(solution)/shard_map/all_to_all | solution.py:258
  22.1 0.6 compare_convert_fusion.live_ref
  22.7 1.6 %multiply_reduce_fusion = f32[2048]{0:T(1024)S(1)} fusion(f32[2048,128]{1,0:T(8,128)} %param.6), kind=kLoop, calls=%fused_computation.1 | loop fusion | flops 522240 | bytes 1056768 | tf_op jit(solution)/shard_map/reduce_sum | solution.py:23
  24.2 2.5 %broadcast_multiply_fusion = f32[2048,128]{1,0:T(8,128)} fusion(f32[2048,128]{1,0:T(8,128)} %param.6, f32[2048]{0:T(1024)S(1)} %add_rsqrt_fusion), kind=kLoop, calls=%fused_computation.2 | loop fusion | flops 262144 | bytes 2105344 | tf_op jit(solution)/shard_map/mul | solution.py:23
  26.8 0.0 copy-done.1
  26.8 17.5 %all-to-all-done.1.tt_ref = f32[16,128,128]{2,1,0:T(8,128)S(1)} async-done(((f32[16,128,128]{2,1,0:T(8,128)}), f32[16,128,128]{2,1,0:T(8,128)S(1)}, u32[]{:S(2)}, u32[]{:S(2)}) %all-to-all-start.1) | async-done | bytes 1048608 | tf_op jit(solution)/shard_map/all_to_all | solution.py:258
  44.3 0.0 copy-start
  44.3 1.1 %copy-done = f32[16,128,128]{2,1,0:T(8,128)} copy-done((f32[16,128,128]{2,1,0:T(8,128)}, f32[16,128,128]{2,1,0:T(8,128)S(1)}, u32[]{:S(2)}) %copy-start) | copy-done | bytes 1048600
  45.4 12.0 %shard_map.77 = (f32[128,128,128]{2,1,0:T(8,128)}, f32[16,128,1]{2,1,0:T(8,128)}, f32[16,16,128]{2,1,0:T(8,128)}) custom-call(s32[128]{0:T(128)} %src_sm.5, s32[128]{0:T(128)} %slot_sm.5, f32[128]{0:T(128)} %compare_convert_fusion.live_ref, f32[16,128,128]{2,1,0:T(8,128)} %bitcast.19, f32[16,128,128]{2,1,0:T(8,128)} %copy-done), custom_call_target="tpu_custom_call" | custom-call | tf_op jit(solution)/shard_map/pallas_call | solution.py:182
  57.4 14.8 %all_to_all.24 = f32[16,16,128]{2,1,0:T(8,128)S(1)} all-to-all(f32[16,16,128]{2,1,0:T(8,128)} %get-tuple-element.13), channel_id=1, replica_groups=mesh['groups'=2,'rows'=16] {'rows'}, dimensions={0} | all-to-all | bytes 262144 | tf_op jit(solution)/shard_map/all_to_all | solution.py:264
  72.2 0.1 select_reduce_fusion.1
  72.3 0.6 maximum_divide_fusion.1
  72.9 6.7 %shard_map.78 = (f32[16,128,1]{2,1,0:T(8,128)}, f32[16,16,128]{2,1,0:T(8,128)}) custom-call(s32[128]{0:T(128)} %src_sm.5, s32[128]{0:T(128)} %slot_sm.5, f32[128,128,128]{2,1,0:T(8,128)} %get-tuple-element.11.k_hbm, f32[16,1,128]{2,1,0:T(1,128)} %bitcast.23), custom_call_target="tpu_custom_call" | custom-call | tf_op jit(solution)/shard_map/pallas_call | solution.py:204
  79.6 11.4 %all_to_all.25 = f32[16,16,128]{2,1,0:T(8,128)S(1)} all-to-all(f32[16,16,128]{2,1,0:T(8,128)} %get-tuple-element.14), channel_id=1, replica_groups=mesh['groups'=2,'rows'=16] {'rows'}, dimensions={0} | all-to-all | bytes 262144 | tf_op jit(solution)/shard_map/all_to_all | solution.py:264
  91.0 0.1 select_reduce_fusion
  91.1 0.6 maximum_divide_fusion
  91.7 9.2 %shard_map.79 = (f32[16,128,128]{2,1,0:T(8,128)}, f32[16,128]{1,0:T(8,128)}) custom-call(s32[128]{0:T(128)} %src_sm.5, s32[128]{0:T(128)} %slot_sm.5, f32[128,128,128]{2,1,0:T(8,128)} %get-tuple-element.11.k_hbm, f32[16,128,128]{2,1,0:T(8,128)} %copy-done, f32[16,1,128]{2,1,0:T(1,128)} %bitcast.22, f32[16,128,1]{2,1,0:T(8,128)} %get-tuple-element.15.r_ref), custom_call_target="tpu_custom_call" | custom-call | tf_op jit(solution)/shard_map/pallas_call | solution.py:226
  (5 shorter events, 0.0 us)
Async XLA Ops:
  0.6 26.2 %copy-start.1 = (s32[16,1]{0,1:T(1,128)S(1)}, s32[16,1]{0,1:T(1,128)}, u32[]{:S(2)}) copy-start(s32[16,1]{0,1:T(1,128)} %param.11) | copy-start | bytes 196
  2.0 13.7 %all-to-all-start = ((s32[16,1,16]{2,1,0:T(1,128)}), s32[16,1,16]{2,1,0:T(1,128)S(1)}, u32[]{:S(2)}, u32[]{:S(2)}) async-start(s32[16,1,16]{2,1,0:T(1,128)} %broadcast_in_dim.30), calls=%async_computation | async-start | bytes 16384 | tf_op jit(solution)/shard_map/all_to_all | solution.py:251
  17.8 26.6 %all-to-all-start.1 = ((f32[16,128,128]{2,1,0:T(8,128)}), f32[16,128,128]{2,1,0:T(8,128)S(1)}, u32[]{:S(2)}, u32[]{:S(2)}) async-start(f32[16,128,128]{2,1,0:T(8,128)} %gather_fusion), calls=%async_computation.1 | async-start | bytes 2097152 | tf_op jit(solution)/shard_map/all_to_all | solution.py:258
  44.3 1.1 %copy-start = (f32[16,128,128]{2,1,0:T(8,128)}, f32[16,128,128]{2,1,0:T(8,128)S(1)}, u32[]{:S(2)}) copy-start(f32[16,128,128]{2,1,0:T(8,128)S(1)} %all-to-all-done.1.tt_ref) | copy-start | bytes 3145732

commit v16 on v15

--- a/solution.py
+++ b/solution.py
@@ -76,6 +76,15 @@
         spread_out[d] = partials
 
 
+def _column_scale(g_ref, m_ref, c_scr):
+    totals = g_ref[0] * m_ref[0]
+    for d in range(1, g_ref.shape[0]):
+        totals = totals + g_ref[d] * m_ref[d]
+    scale = 1.0 / jnp.maximum(totals, COLUMN_FLOOR)
+    for o in range(c_scr.shape[0]):
+        c_scr[o] = scale[o : o + 1, :]
+
+
 def _chunk_copies(src, dst, sems, capacity):
     bounds = _bounds(capacity)
     return [
@@ -106,11 +115,14 @@
         copy.wait()
 
 
-def _again_kernel(src_sm, slot_sm, k_hbm, c_ref, r_out, spread_out, k_scr, acc, rb_scr, colp, sems):
+def _again_kernel(
+    src_sm, slot_sm, k_hbm, g_ref, m_ref, r_out, spread_out, k_scr, acc, rb_scr, colp, c_ref, sems
+):
     capacity = src_sm.shape[0]
     copies = _chunk_copies(k_hbm, k_scr, sems, capacity)
     for copy in copies:
         copy.start()
+    _column_scale(g_ref, m_ref, c_ref)
 
     def chunk_done(part, when):
         if when == "before":
@@ -132,13 +144,14 @@
 
 
 def _final_kernel(
-    src_sm, slot_sm, k_hbm, tt_ref, c_ref, r_ref, al_out, ms_out, k_scr, ms_scr, t_ref, sems
+    src_sm, slot_sm, k_hbm, tt_ref, g_ref, m_ref, r_ref, al_out, ms_out, k_scr, ms_scr, t_ref, c_ref, sems
 ):
     capacity = src_sm.shape[0]
     bounds = _bounds(capacity)
     copies = _chunk_copies(k_hbm, k_scr, sems, capacity)
     for copy in copies:
         copy.start()
+    _column_scale(g_ref, m_ref, c_ref)
     for o in range(t_ref.shape[0]):
         t_ref[o] = jnp.transpose(tt_ref[o])
     al_out[...] = jnp.zeros_like(al_out)
@@ -200,23 +213,24 @@
 
 def again_sweep(tile_source, tile_slot, kernel, col, sb, rows_n):
     capacity = tile_source.shape[0]
-    slots = col.shape[0]
+    slots = col[0].shape[1]
     return pl.pallas_call(
         _again_kernel,
         out_shape=(
             jax.ShapeDtypeStruct((sb, BLOCK, 1), jnp.float32),
             jax.ShapeDtypeStruct((rows_n, slots, BLOCK), jnp.float32),
         ),
-        in_specs=_specs(2, 0) + [_ANY] + _specs(0, 1),
+        in_specs=_specs(2, 0) + [_ANY] + _specs(0, 2),
         out_specs=_vmem_out(2),
         scratch_shapes=[
             pltpu.VMEM((capacity, BLOCK, BLOCK), jnp.float32),
             pltpu.VMEM((sb, BLOCK, BLOCK), jnp.float32),
             pltpu.VMEM((sb, BLOCK, BLOCK), jnp.float32),
             pltpu.VMEM((slots, 1, BLOCK), jnp.float32),
+            pltpu.VMEM((slots, 1, BLOCK), jnp.float32),
             pltpu.SemaphoreType.DMA((len(_bounds(capacity)) - 1,)),
         ],
-    )(tile_source, tile_slot, kernel, col)
+    )(tile_source, tile_slot, kernel, *col)
 
 
 def final(tile_source, tile_slot, kernel, fetched_t, col, row):
@@ -229,15 +243,16 @@
             jax.ShapeDtypeStruct((sb, BLOCK, E), jnp.float32),
             jax.ShapeDtypeStruct((sb, BLOCK), jnp.float32),
         ),
-        in_specs=_specs(2, 0) + [_ANY] + _specs(0, 3),
+        in_specs=_specs(2, 0) + [_ANY] + _specs(0, 4),
         out_specs=_vmem_out(2),
         scratch_shapes=[
             pltpu.VMEM((capacity, BLOCK, BLOCK), jnp.float32),
             pltpu.VMEM((sb, BLOCK, BLOCK), jnp.float32),
             pltpu.VMEM((slots, BLOCK, E), jnp.float32),
+            pltpu.VMEM((slots, 1, BLOCK), jnp.float32),
             pltpu.SemaphoreType.DMA((len(_bounds(capacity)) - 1,)),
         ],
-    )(tile_source, tile_slot, kernel, fetched_t, col, row)
+    )(tile_source, tile_slot, kernel, fetched_t, *col, row)
 
 
 def on_device(source_emb, target_emb, tile_source, tile_slot, tile_count, wanted):
@@ -262,9 +277,11 @@
 
     def column_scale_of(spread):
         gathered = lax.all_to_all(spread, "rows", split_axis=0, concat_axis=0, tiled=True)
+        if need == 1:
+            return gathered, same_block.reshape(rows_n, slots, 1).astype(jnp.float32)
         gathered = gathered.reshape(rows_n, owners, need, 1, BLOCK)
         totals = jnp.sum(jnp.where(same_block, gathered, 0.0), axis=(0, 2))
-        return (1.0 / jnp.maximum(totals, COLUMN_FLOOR)).reshape(slots, 1, BLOCK)
+        return totals.reshape(1, slots, BLOCK), jnp.ones((1, slots, 1), jnp.float32)
 
     live = (jnp.arange(tile_source.shape[0]) < tile_count[0]).astype(jnp.float32)
     sb = source_unit.shape[0]

time: 102 us -> 102 us (level)
  blocking collectives: 26.2 us -> 12.1 us
  waiting for transfers between devices: 21.5 us -> 28.7 us
  starting transfers between devices: 11 us -> 17.9 us
  other arithmetic: 8.3 us -> 6.85 us
  local copies, waits for them, and re-layouts: 4.57 us -> 6.01 us
    all_to_all x2 -> x1, blocking collectives: 26.2 us -> 12.1 us  [column_scale_of(): lax.all_to_all(spread, 'rows', split_axis=0, concat_axis=0, tiled=True)]
    all_to_all x0 -> x1, waiting for transfers between devices: none -> 7.1 us  [column_scale_of(): lax.all_to_all(spread, 'rows', split_axis=0, concat_axis=0, tiled=True)]
    all_to_all x0 -> x1, starting transfers between devices: none -> 6.84 us  [column_scale_of(): lax.all_to_all(spread, 'rows', split_axis=0, concat_axis=0, tiled=True)]
    div x2 -> x0, other arithmetic: 1.2 us -> none  [column_scale_of(): return (1.0 / jnp.maximum(totals, COLUMN_FLOOR)).reshape(slots, 1, BLOCK)]
  transfers between devices with their start and end apart: 2 -> 3, of which waited for: 2 -> 3; matrix products, arithmetic and copies ran while one was open for 7% -> 8% of each run, Pallas kernels for 0% -> 0%
where the time goes in v16:
time: 102 us; the launch traced here: 101 us
  waiting for transfers between devices  28.7 us (28%)
  Pallas kernels  28.3 us (28%)
  starting transfers between devices  17.9 us (18%)
  blocking collectives  12.1 us (12%)
  other arithmetic  6.85 us (7%)
  local copies, waits for them, and re-layouts  6.01 us (6%)
  between operations  1.56 us (2%)
    all_to_all x1, waiting for transfers between devices, on_device(): lax.all_to_all(outgoing, 'rows', split_axis=0, concat_axis=0, tiled=True)  17.6 us
    all_to_all x1, blocking collectives, column_scale_of(): lax.all_to_all(spread, 'rows', split_axis=0, concat_axis=0, tiled=True)  12.1 us
    pallas_call x1, Pallas kernels, first_sweep(): pl.pallas_call(_first_kernel, out_shape=(jax.ShapeDtypeStruct((capacity,...  12 us
    pallas_call x1, Pallas kernels, final(): pl.pallas_call(_final_kernel, out_shape=(jax.ShapeDtypeStruct((sb, BLOCK,...  9.32 us
    all_to_all x1, starting transfers between devices, on_device(): lax.all_to_all(jnp.broadcast_to(wanted_row, (rows_n, slots)), 'rows', spl...  7.39 us
    all_to_all x1, waiting for transfers between devices, column_scale_of(): lax.all_to_all(spread, 'rows', split_axis=0, concat_axis=0, tiled=True)  7.1 us
    pallas_call x1, Pallas kernels, again_sweep(): pl.pallas_call(_again_kernel, out_shape=(jax.ShapeDtypeStruct((sb, BLOCK,...  6.97 us
    all_to_all x1, starting transfers between devices, column_scale_of(): lax.all_to_all(spread, 'rows', split_axis=0, concat_axis=0, tiled=True)  6.84 us
  transfers between devices with their start and end apart: 3, of which 3 were waited for; matrix products, arithmetic and copies ran while one was open for 8% of the time, Pallas kernels for 0%

profile of v16, /device:TPU:0, one launch (start us, length us, event | category | flops | bytes accessed | tf_op | source)
XLA Modules:
  0.0 101.4 jit_solution(15782783267695387024)
XLA Ops:
  0.6 0.0 copy-start.2
  0.6 1.3 %broadcast_in_dim.5 = s32[16,1,16]{2,1,0:T(1,128)} broadcast(s32[16]{0:T(128)} %bitcast.19), dimensions={2} | broadcast | bytes 1088 | tf_op jit(solution)/shard_map/broadcast_in_dim | solution.py:267
  2.0 7.4 %all-to-all-start = ((s32[16,1,16]{2,1,0:T(1,128)}), s32[16,1,16]{2,1,0:T(1,128)S(1)}, u32[]{:S(2)}, u32[]{:S(2)}) async-start(s32[16,1,16]{2,1,0:T(1,128)} %broadcast_in_dim.5), calls=%async_computation | async-start | bytes 16384 | tf_op jit(solution)/shard_map/all_to_all | solution.py:266
  9.4 1.1 %multiply_reduce_fusion.1 = f32[512]{0:T(512)S(1)} fusion(f32[512,128]{1,0:T(8,128)} %param.7), kind=kLoop, calls=%fused_computation.3 | loop fusion | flops 130560 | bytes 264192 | tf_op jit(solution)/shard_map/reduce_sum | solution.py:23
  10.5 1.1 %broadcast_multiply_fusion.1 = f32[512,128]{1,0:T(8,128)S(1)} fusion(f32[512,128]{1,0:T(8,128)} %param.7, f32[512]{0:T(512)S(1)} %add_rsqrt_fusion.1), kind=kLoop, calls=%fused_computation.4 | loop fusion | flops 65536 | bytes 526336 | tf_op jit(solution)/shard_map/mul | solution.py:23
  11.6 0.1 copy.13
  11.7 4.0 %all-to-all-done = s32[16,1,16]{2,1,0:T(1,128)S(1)} async-done(((s32[16,1,16]{2,1,0:T(1,128)}), s32[16,1,16]{2,1,0:T(1,128)S(1)}, u32[]{:S(2)}, u32[]{:S(2)}) %all-to-all-start) | async-done | bytes 1056 | tf_op jit(solution)/shard_map/all_to_all | solution.py:266
  15.7 0.4 dynamic-slice_reduce_fusion
  16.2 1.6 %gather_fusion = f32[16,128,128]{2,1,0:T(8,128)} fusion(f32[4,128,128]{2,1,0:T(8,128)S(1)} %bitcast.15, s32[1024]{0:T(1024)S(1)} %pad_clamp_fusion), kind=kCustom, calls=%fused_computation | custom fusion | bytes 2097216 | tf_op jit(solution)/shard_map/gather | solution.py:272
  17.7 3.7 %all-to-all-start.1 = ((f32[16,128,128]{2,1,0:T(8,128)}), f32[16,128,128]{2,1,0:T(8,128)S(1)}, u32[]{:S(2)}, u32[]{:S(2)}) async-start(f32[16,128,128]{2,1,0:T(8,128)} %gather_fusion), calls=%async_computation.1 | async-start | bytes 2097152 | tf_op jit(solution)/shard_map/all_to_all | solution.py:273
  22.0 0.5 compare_convert_fusion.live_ref
  22.6 1.6 %multiply_reduce_fusion = f32[2048]{0:T(1024)S(1)} fusion(f32[2048,128]{1,0:T(8,128)} %param.6), kind=kLoop, calls=%fused_computation.1 | loop fusion | flops 522240 | bytes 1056768 | tf_op jit(solution)/shard_map/reduce_sum | solution.py:23
  24.2 2.5 %broadcast_multiply_fusion = f32[2048,128]{1,0:T(8,128)} fusion(f32[2048,128]{1,0:T(8,128)} %param.6, f32[2048]{0:T(1024)S(1)} %add_rsqrt_fusion), kind=kLoop, calls=%fused_computation.2 | loop fusion | flops 262144 | bytes 2105344 | tf_op jit(solution)/shard_map/mul | solution.py:23
  26.7 0.0 copy-done.2
  26.7 17.6 %all-to-all-done.1.tt_ref = f32[16,128,128]{2,1,0:T(8,128)S(1)} async-done(((f32[16,128,128]{2,1,0:T(8,128)}), f32[16,128,128]{2,1,0:T(8,128)S(1)}, u32[]{:S(2)}, u32[]{:S(2)}) %all-to-all-start.1) | async-done | bytes 1048608 | tf_op jit(solution)/shard_map/all_to_all | solution.py:273
  44.3 0.0 copy-start
  44.3 1.0 %copy-done = f32[16,128,128]{2,1,0:T(8,128)} copy-done((f32[16,128,128]{2,1,0:T(8,128)}, f32[16,128,128]{2,1,0:T(8,128)S(1)}, u32[]{:S(2)}) %copy-start) | copy-done | bytes 1048600
  45.3 12.0 %shard_map.77 = (f32[128,128,128]{2,1,0:T(8,128)}, f32[16,128,1]{2,1,0:T(8,128)}, f32[16,16,128]{2,1,0:T(8,128)}) custom-call(s32[128]{0:T(128)} %src_sm.5, s32[128]{0:T(128)} %slot_sm.5, f32[128]{0:T(128)} %compare_convert_fusion.live_ref, f32[16,128,128]{2,1,0:T(8,128)} %bitcast.16, f32[16,128,128]{2,1,0:T(8,128)} %copy-done), custom_call_target="tpu_custom_call" | custom-call | tf_op jit(solution)/shard_map/pallas_call | solution.py:195
  57.4 6.8 %all-to-all-start.2 = ((f32[16,16,128]{2,1,0:T(8,128)}), f32[16,16,128]{2,1,0:T(8,128)S(1)}, u32[]{:S(2)}, u32[]{:S(2)}) async-start(f32[16,16,128]{2,1,0:T(8,128)} %get-tuple-element.12), calls=%async_computation.2 | async-start | bytes 262144 | tf_op jit(solution)/shard_map/all_to_all | solution.py:279
  64.2 0.8 copy.14.m_ref
  65.1 7.1 %all-to-all-done.2.g_ref = f32[16,16,128]{2,1,0:T(8,128)S(1)} async-done(((f32[16,16,128]{2,1,0:T(8,128)}), f32[16,16,128]{2,1,0:T(8,128)S(1)}, u32[]{:S(2)}, u32[]{:S(2)}) %all-to-all-start.2) | async-done | bytes 131104 | tf_op jit(solution)/shard_map/all_to_all | solution.py:279
  72.2 0.0 copy-start.1
  72.2 0.7 copy-done.1
  72.8 7.0 %shard_map.78 = (f32[16,128,1]{2,1,0:T(8,128)}, f32[16,16,128]{2,1,0:T(8,128)}) custom-call(s32[128]{0:T(128)} %src_sm.5, s32[128]{0:T(128)} %slot_sm.5, f32[128,128,128]{2,1,0:T(8,128)} %get-tuple-element.11.k_hbm, f32[16,16,128]{2,1,0:T(8,128)} %copy-done.1, f32[16,16,1]{2,1,0:T(8,128)} %copy.14.m_ref), custom_call_target="tpu_custom_call" | custom-call | tf_op jit(solution)/shard_map/pallas_call | solution.py:217
  79.8 12.1 %all_to_all.24.g_ref = f32[16,16,128]{2,1,0:T(8,128)} all-to-all(f32[16,16,128]{2,1,0:T(8,128)} %get-tuple-element.14), channel_id=1, replica_groups=mesh['groups'=2,'rows'=16] {'rows'}, dimensions={0} | all-to-all | bytes 262144 | tf_op jit(solution)/shard_map/all_to_all | solution.py:279
  91.9 9.3 %shard_map.79 = (f32[16,128,128]{2,1,0:T(8,128)}, f32[16,128]{1,0:T(8,128)}) custom-call(s32[128]{0:T(128)} %src_sm.5, s32[128]{0:T(128)} %slot_sm.5, f32[128,128,128]{2,1,0:T(8,128)} %get-tuple-element.11.k_hbm, f32[16,128,128]{2,1,0:T(8,128)} %copy-done, f32[16,16,128]{2,1,0:T(8,128)} %all_to_all.24.g_ref, f32[16,16,1]{2,1,0:T(8,128)} %copy.14.m_ref, ...), custom_call_target="tpu_custom_call" | custom-call | tf_op jit(solution)/shard_map/pallas_call | solution.py:240
  (6 shorter events, 0.0 us)
Async XLA Ops:
  0.6 26.1 %copy-start.2 = (s32[16,1]{0,1:T(1,128)S(1)}, s32[16,1]{0,1:T(1,128)}, u32[]{:S(2)}) copy-start(s32[16,1]{0,1:T(1,128)} %param.11) | copy-start | bytes 196
  2.0 13.7 %all-to-all-start = ((s32[16,1,16]{2,1,0:T(1,128)}), s32[16,1,16]{2,1,0:T(1,128)S(1)}, u32[]{:S(2)}, u32[]{:S(2)}) async-start(s32[16,1,16]{2,1,0:T(1,128)} %broadcast_in_dim.5), calls=%async_computation | async-start | bytes 16384 | tf_op jit(solution)/shard_map/all_to_all | solution.py:266
  17.7 26.6 %all-to-all-start.1 = ((f32[16,128,128]{2,1,0:T(8,128)}), f32[16,128,128]{2,1,0:T(8,128)S(1)}, u32[]{:S(2)}, u32[]{:S(2)}) async-start(f32[16,128,128]{2,1,0:T(8,128)} %gather_fusion), calls=%async_computation.1 | async-start | bytes 2097152 | tf_op jit(solution)/shard_map/all_to_all | solution.py:273
  44.3 1.1 %copy-start = (f32[16,128,128]{2,1,0:T(8,128)}, f32[16,128,128]{2,1,0:T(8,128)S(1)}, u32[]{:S(2)}) copy-start(f32[16,128,128]{2,1,0:T(8,128)S(1)} %all-to-all-done.1.tt_ref) | copy-start | bytes 3145732
  57.4 14.8 %all-to-all-start.2 = ((f32[16,16,128]{2,1,0:T(8,128)}), f32[16,16,128]{2,1,0:T(8,128)S(1)}, u32[]{:S(2)}, u32[]{:S(2)}) async-start(f32[16,16,128]{2,1,0:T(8,128)} %get-tuple-element.12), calls=%async_computation.2 | async-start | bytes 262144 | tf_op jit(solution)/shard_map/all_to_all | solution.py:279
  72.2 0.7 copy-start.1

commit v17 on v14

--- a/solution.py
+++ b/solution.py
@@ -25,7 +25,7 @@
 
 def _tile(s_ref, tt_ref, q, o):
     cosine = jnp.dot(s_ref[q], tt_ref[o], precision=HIGHEST, preferred_element_type=jnp.float32)
-    return jnp.exp(cosine / SOFTMAX_WARMTH)
+    return jnp.exp(cosine * (1.0 / SOFTMAX_WARMTH))
 
 
 def _chunk(capacity):

time: 102 us -> 102 us (level)
  no operation moved by 1% of the time
where the time goes in v17:
time: 102 us; the launch traced here: 101 us
  Pallas kernels  28.2 us (28%)
  blocking collectives  26.2 us (26%)
  waiting for transfers between devices  21.5 us (21%)
  starting transfers between devices  11 us (11%)
  other arithmetic  8.3 us (8%)
  local copies, waits for them, and re-layouts  4.57 us (4%)
  between operations  1.56 us (2%)
    all_to_all x2, blocking collectives, column_scale_of(): lax.all_to_all(spread, 'rows', split_axis=0, concat_axis=0, tiled=True)  26.2 us
    all_to_all x1, waiting for transfers between devices, on_device(): lax.all_to_all(outgoing, 'rows', split_axis=0, concat_axis=0, tiled=True)  17.5 us
    pallas_call x1, Pallas kernels, first_sweep(): pl.pallas_call(_first_kernel, out_shape=(jax.ShapeDtypeStruct((capacity,...  12 us
    pallas_call x1, Pallas kernels, final(): pl.pallas_call(_final_kernel, out_shape=(jax.ShapeDtypeStruct((sb, BLOCK,...  9.52 us
    all_to_all x1, starting transfers between devices, on_device(): lax.all_to_all(jnp.broadcast_to(wanted_row, (rows_n, slots)), 'rows', spl...  7.39 us
    pallas_call x1, Pallas kernels, again_sweep(): pl.pallas_call(_again_kernel, out_shape=(jax.ShapeDtypeStruct((sb, BLOCK,...  6.65 us
    all_to_all x1, waiting for transfers between devices, on_device(): lax.all_to_all(jnp.broadcast_to(wanted_row, (rows_n, slots)), 'rows', spl...  3.99 us
    all_to_all x1, starting transfers between devices, on_device(): lax.all_to_all(outgoing, 'rows', split_axis=0, concat_axis=0, tiled=True)  3.65 us
  transfers between devices with their start and end apart: 2, of which 2 were waited for; matrix products, arithmetic and copies ran while one was open for 7% of the time, Pallas kernels for 0%

profile of v17, /device:TPU:0, one launch (start us, length us, event | category | flops | bytes accessed | tf_op | source)
XLA Modules:
  0.0 101.3 jit_solution(6212933198255812558)
XLA Ops:
  0.6 0.0 copy-start.1
  0.6 1.3 %broadcast_in_dim.30 = s32[16,1,16]{2,1,0:T(1,128)} broadcast(s32[16]{0:T(128)} %bitcast.26), dimensions={2} | broadcast | bytes 1088 | tf_op jit(solution)/shard_map/broadcast_in_dim | solution.py:245
  2.0 7.4 %all-to-all-start = ((s32[16,1,16]{2,1,0:T(1,128)}), s32[16,1,16]{2,1,0:T(1,128)S(1)}, u32[]{:S(2)}, u32[]{:S(2)}) async-start(s32[16,1,16]{2,1,0:T(1,128)} %broadcast_in_dim.30), calls=%async_computation | async-start | bytes 16384 | tf_op jit(solution)/shard_map/all_to_all | solution.py:244
  9.4 1.1 %multiply_reduce_fusion.1 = f32[512]{0:T(512)S(1)} fusion(f32[512,128]{1,0:T(8,128)} %param.7), kind=kLoop, calls=%fused_computation.3 | loop fusion | flops 130560 | bytes 264192 | tf_op jit(solution)/shard_map/reduce_sum | solution.py:23
  10.5 1.1 %broadcast_multiply_fusion.1 = f32[512,128]{1,0:T(8,128)S(1)} fusion(f32[512,128]{1,0:T(8,128)} %param.7, f32[512]{0:T(512)S(1)} %add_rsqrt_fusion.1), kind=kLoop, calls=%fused_computation.6 | loop fusion | flops 65536 | bytes 526336 | tf_op jit(solution)/shard_map/mul | solution.py:23
  11.6 0.1 copy.17
  11.7 4.0 %all-to-all-done = s32[16,1,16]{2,1,0:T(1,128)S(1)} async-done(((s32[16,1,16]{2,1,0:T(1,128)}), s32[16,1,16]{2,1,0:T(1,128)S(1)}, u32[]{:S(2)}, u32[]{:S(2)}) %all-to-all-start) | async-done | bytes 1056 | tf_op jit(solution)/shard_map/all_to_all | solution.py:244
  15.7 0.4 dynamic-slice_reduce_fusion
  16.2 1.6 %gather_fusion = f32[16,128,128]{2,1,0:T(8,128)} fusion(f32[4,128,128]{2,1,0:T(8,128)S(1)} %bitcast.18, s32[1024]{0:T(1024)S(1)} %pad_clamp_fusion), kind=kCustom, calls=%fused_computation | custom fusion | bytes 2097216 | tf_op jit(solution)/shard_map/gather | solution.py:250
  17.8 3.7 %all-to-all-start.1 = ((f32[16,128,128]{2,1,0:T(8,128)}), f32[16,128,128]{2,1,0:T(8,128)S(1)}, u32[]{:S(2)}, u32[]{:S(2)}) async-start(f32[16,128,128]{2,1,0:T(8,128)} %gather_fusion), calls=%async_computation.1 | async-start | bytes 2097152 | tf_op jit(solution)/shard_map/all_to_all | solution.py:251
  22.1 0.6 compare_convert_fusion.live_ref
  22.7 1.6 %multiply_reduce_fusion = f32[2048]{0:T(1024)S(1)} fusion(f32[2048,128]{1,0:T(8,128)} %param.6), kind=kLoop, calls=%fused_computation.1 | loop fusion | flops 522240 | bytes 1056768 | tf_op jit(solution)/shard_map/reduce_sum | solution.py:23
  24.2 2.5 %broadcast_multiply_fusion = f32[2048,128]{1,0:T(8,128)} fusion(f32[2048,128]{1,0:T(8,128)} %param.6, f32[2048]{0:T(1024)S(1)} %add_rsqrt_fusion), kind=kLoop, calls=%fused_computation.2 | loop fusion | flops 262144 | bytes 2105344 | tf_op jit(solution)/shard_map/mul | solution.py:23
  26.8 0.0 copy-done.1
  26.8 17.5 %all-to-all-done.1.tt_ref = f32[16,128,128]{2,1,0:T(8,128)S(1)} async-done(((f32[16,128,128]{2,1,0:T(8,128)}), f32[16,128,128]{2,1,0:T(8,128)S(1)}, u32[]{:S(2)}, u32[]{:S(2)}) %all-to-all-start.1) | async-done | bytes 1048608 | tf_op jit(solution)/shard_map/all_to_all | solution.py:251
  44.3 0.0 copy-start
  44.3 1.1 %copy-done = f32[16,128,128]{2,1,0:T(8,128)} copy-done((f32[16,128,128]{2,1,0:T(8,128)}, f32[16,128,128]{2,1,0:T(8,128)S(1)}, u32[]{:S(2)}) %copy-start) | copy-done | bytes 1048600
  45.4 12.0 %shard_map.77 = (f32[128,128,128]{2,1,0:T(8,128)}, f32[16,128,1]{2,1,0:T(8,128)}, f32[16,16,128]{2,1,0:T(8,128)}) custom-call(s32[128]{0:T(128)} %src_sm.5, s32[128]{0:T(128)} %slot_sm.5, f32[128]{0:T(128)} %compare_convert_fusion.live_ref, f32[16,128,128]{2,1,0:T(8,128)} %bitcast.19, f32[16,128,128]{2,1,0:T(8,128)} %copy-done), custom_call_target="tpu_custom_call" | custom-call | tf_op jit(solution)/shard_map/pallas_call | solution.py:175
  57.4 14.8 %all_to_all.24 = f32[16,16,128]{2,1,0:T(8,128)S(1)} all-to-all(f32[16,16,128]{2,1,0:T(8,128)} %get-tuple-element.13), channel_id=1, replica_groups=mesh['groups'=2,'rows'=16] {'rows'}, dimensions={0} | all-to-all | bytes 262144 | tf_op jit(solution)/shard_map/all_to_all | solution.py:257
  72.2 0.1 select_reduce_fusion.1
  72.3 0.6 maximum_divide_fusion.1
  72.9 6.6 %shard_map.78 = (f32[16,128,1]{2,1,0:T(8,128)}, f32[16,16,128]{2,1,0:T(8,128)}) custom-call(s32[128]{0:T(128)} %src_sm.5, s32[128]{0:T(128)} %slot_sm.5, f32[128,128,128]{2,1,0:T(8,128)} %get-tuple-element.11.k_hbm, f32[16,1,128]{2,1,0:T(1,128)} %bitcast.23), custom_call_target="tpu_custom_call" | custom-call | tf_op jit(solution)/shard_map/pallas_call | solution.py:197
  79.5 11.4 %all_to_all.25 = f32[16,16,128]{2,1,0:T(8,128)S(1)} all-to-all(f32[16,16,128]{2,1,0:T(8,128)} %get-tuple-element.14), channel_id=1, replica_groups=mesh['groups'=2,'rows'=16] {'rows'}, dimensions={0} | all-to-all | bytes 262144 | tf_op jit(solution)/shard_map/all_to_all | solution.py:257
  91.0 0.1 select_reduce_fusion
  91.1 0.6 maximum_divide_fusion
  91.7 9.5 %shard_map.79 = (f32[16,128,128]{2,1,0:T(8,128)}, f32[16,128]{1,0:T(8,128)}) custom-call(s32[128]{0:T(128)} %src_sm.5, s32[128]{0:T(128)} %slot_sm.5, f32[128,128,128]{2,1,0:T(8,128)} %get-tuple-element.11.k_hbm, f32[16,128,128]{2,1,0:T(8,128)} %copy-done, f32[16,1,128]{2,1,0:T(1,128)} %bitcast.22, f32[16,128,1]{2,1,0:T(8,128)} %get-tuple-element.15.r_ref), custom_call_target="tpu_custom_call" | custom-call | tf_op jit(solution)/shard_map/pallas_call | solution.py:219
  (5 shorter events, 0.0 us)
Async XLA Ops:
  0.6 26.2 %copy-start.1 = (s32[16,1]{0,1:T(1,128)S(1)}, s32[16,1]{0,1:T(1,128)}, u32[]{:S(2)}) copy-start(s32[16,1]{0,1:T(1,128)} %param.11) | copy-start | bytes 196
  2.0 13.7 %all-to-all-start = ((s32[16,1,16]{2,1,0:T(1,128)}), s32[16,1,16]{2,1,0:T(1,128)S(1)}, u32[]{:S(2)}, u32[]{:S(2)}) async-start(s32[16,1,16]{2,1,0:T(1,128)} %broadcast_in_dim.30), calls=%async_computation | async-start | bytes 16384 | tf_op jit(solution)/shard_map/all_to_all | solution.py:244
  17.8 26.6 %all-to-all-start.1 = ((f32[16,128,128]{2,1,0:T(8,128)}), f32[16,128,128]{2,1,0:T(8,128)S(1)}, u32[]{:S(2)}, u32[]{:S(2)}) async-start(f32[16,128,128]{2,1,0:T(8,128)} %gather_fusion), calls=%async_computation.1 | async-start | bytes 2097152 | tf_op jit(solution)/shard_map/all_to_all | solution.py:251
  44.3 1.1 %copy-start = (f32[16,128,128]{2,1,0:T(8,128)}, f32[16,128,128]{2,1,0:T(8,128)S(1)}, u32[]{:S(2)}) copy-start(f32[16,128,128]{2,1,0:T(8,128)S(1)} %all-to-all-done.1.tt_ref) | copy-start | bytes 3145732
